TPU v7x, 512 devices: a whole 4x4x16 slice. The times are simulated.
512 devices in a mesh: lat: 16 (over z_lo, core), lon: 32 (over y, z_hi, x).
Axes of the slice: x: 4, y: 4, z: 16 (z_hi: 2, z_lo: 8; z = z_hi * 8 + z_lo), core: 2. Of those that a mesh axis runs over, the one named last changes fastest.
Arguments:
- initial_state: float32 [16, 32, 64, 256], P('lat', 'lon'), may hold values from -6 to 6
- initial_reservoir: bfloat16 [16, 32, 64, 2048], P('lat', 'lon'), may hold values from -0.8984375 to 0.8984375
- coupling: bfloat16 [16, 32, 16, 4, 128, 128], P('lat', 'lon'), may hold values from -0.1875 to 0.1875
- input_weight: bfloat16 [16, 32, 16, 128, 128], P('lat', 'lon'), may hold values from -0.5 to 0.5
- readout: bfloat16 [16, 32, 2048, 256], P('lat', 'lon'), may hold values from -0.125 to 0.125
- intersection: int32 [16, 32, 2, 4], P('lat', 'lon'), may hold values from -1 to 7, as said below
Outputs:
- forecast: float32 [8, 16, 32, 64, 256], P(None, 'lat', 'lon')
Inputs may be any that keep to these rules, and one draw needn't show every extreme that they name: `intersection`: each list holds distinct point numbers in its first slots and -1 in the rest, with one or more live slots; the north lists of band 0 and the south lists of the last band hold only -1; in longitude sector 0 every list that is not a polar one has all four slots live.
All inputs are finite; a program needn't handle non-finite values.
Results may differ from a plain program's by a relative error of at most 0.018.
Values may be sent and summed in bfloat16 or wider, within the bound.
No kernel may reach another device: no remote copies, remote signals or barrier semaphores. Data moves between devices by JAX's collectives and lax.ppermute only.
A program may use at most 64 MiB of HBM per device.

v0:
```python
import jax
import jax.numpy as jnp
import numpy as np
from jax import lax
from jax.sharding import PartitionSpec as P

VARS = 32
LATR = 4
LONC = 2
OV = 4
STEPS = 8
PTS = 8


def with_halo(value, sides, width):
    for axis, dim in sides:
        peers, length = (lax.axis_size(axis), value.shape[dim])
        up = [(i, (i + 1) % peers) for i in range(peers)]
        down = [(j, i) for i, j in up]
        last = lax.slice_in_dim(value, length - width, length, axis=dim)
        initial = lax.slice_in_dim(value, 0, width, axis=dim)
        before = lax.ppermute(last, axis, up)
        after = lax.ppermute(initial, axis, down)
        value = jnp.concatenate([before, value, after], axis=dim)
    return value


def shifted(value, axis, by):
    peers = lax.axis_size(axis)
    pairs = [(i, i + by) for i in range(peers) if 0 <= i + by < peers]
    return lax.ppermute(value, axis, pairs)


def select_points(source, slot_list):
    members = source.shape[0]
    points = source.reshape(members, PTS, VARS)
    onehot = (slot_list[:, None] == jnp.arange(PTS, dtype=jnp.int32)[None, :]).astype(jnp.bfloat16)
    picked = jnp.einsum("sp,mpv->msv", onehot, points, preferred_element_type=jnp.float32)
    return picked.astype(jnp.bfloat16).reshape(members, OV * VARS)


def per_device(initial_state, initial_reservoir, coupling, input_weight, readout, intersection):
    current = initial_state[0, 0]
    reservoir = initial_reservoir[0, 0]
    block_weight = coupling[0, 0]
    entry_weight = input_weight[0, 0]
    read_weight = readout[0, 0]
    lists = intersection[0, 0]
    members = current.shape[0]
    nodes = reservoir.shape[1]
    res_blocks = block_weight.shape[0]
    links = block_weight.shape[1]
    breadth = block_weight.shape[2]
    in_blocks = (current.shape[1] + 2 * LATR * VARS + 2 * OV * VARS) // breadth
    linked = (np.arange(res_blocks)[:, None] + np.arange(links)[None, :]) % res_blocks
    block_index = np.arange(res_blocks) % in_blocks
    even_nodes = jnp.arange(nodes) % 2 == 0
    outputs = []
    for moment in range(STEPS):
        rounded = current.astype(jnp.bfloat16)
        blocks = reservoir.reshape(members, res_blocks, breadth)
        activation = jnp.einsum(
            "mbki,bkio->mbo", blocks[:, linked], block_weight, preferred_element_type=jnp.float32
        )
        columns = rounded.reshape(members, LONC, LATR * VARS)
        padded = with_halo(columns, (("lon", 1),), 1)
        west_col = padded[:, 0]
        east_col = padded[:, -1]
        from_north = shifted(rounded, "lat", 1)
        from_south = shifted(rounded, "lat", -1)
        north_part = select_points(from_north, lists[0])
        south_part = select_points(from_south, lists[1])
        inputs = jnp.concatenate([rounded, west_col, east_col, north_part, south_part], axis=-1)
        chosen = inputs.reshape(members, in_blocks, breadth)[:, block_index]
        activation = activation + jnp.einsum(
            "mbi,bio->mbo", chosen, entry_weight, preferred_element_type=jnp.float32
        )
        reservoir = jnp.tanh(activation).astype(jnp.bfloat16).reshape(members, nodes)
        widened = reservoir.astype(jnp.float32)
        features = jnp.where(even_nodes, widened * widened, widened).astype(jnp.bfloat16)
        current = jnp.dot(features, read_weight, preferred_element_type=jnp.float32)
        outputs.append(current)
    return jnp.stack(outputs)[:, None, None]


def solution(mesh):
    in_specs = (
        P("lat", "lon", None, None),
        P("lat", "lon", None, None),
        P("lat", "lon", None, None, None, None),
        P("lat", "lon", None, None, None),
        P("lat", "lon", None, None),
        P("lat", "lon", None, None),
    )
    out_specs = P(None, "lat", "lon", None, None)
    return jax.shard_map(
        per_device, mesh=mesh, in_specs=in_specs, out_specs=out_specs, check_vma=False
    )
```

profile of v0, /device:TPU:414, one launch (start us, length us, event | category | flops | bytes accessed | tf_op | source)
XLA Modules:
  0.0 319.8 jit_solution(12461430607116411967)
XLA Ops:
  1.1 1.9 collective-permute-start.2
  3.0 4.9 %collective-permute-start.3 = (bf16[64,256]{0,1:T(8,128)(2,1)S(1)}, bf16[64,256]{0,1:T(8,128)(2,1)S(1)}, u32[]{:S(2)}, u32[]{:S(2)}) collective-permute-start(bf16[64,256]{0,1:T(8,128)(2,1)S(1)} %bitcast.445), channel_id=1, source_target_pairs={{32,0},{64,32},{96,64},{128,96},{160,128},{192,160},{224,192},{256... | collective-permute-start | bytes 98312 | tf_op jit(solution)/shard_map/ppermute | solution.py:31
  8.5 3.2 %collective-permute-start = (bf16[64,1,128]{0,2,1:T(8,128)(2,1)}, bf16[64,1,128]{0,2,1:T(8,128)(2,1)}, u32[]{:S(2)}, u32[]{:S(2)}) collective-permute-start(bf16[64,1,128]{0,2,1:T(8,128)(2,1)} %get-tuple-element.20), channel_id=1, source_target_pairs={{0,1},{1,2},{2,3},{3,4},{4,5},{5,6},{6,7},{7,8},{8,9},{9,10},{10,1... | collective-permute-start | bytes 49160 | tf_op jit(solution)/shard_map/ppermute | solution.py:22
  11.7 2.6 collective-permute-start.1
  16.9 1.7 gather_fusion
  18.6 1.8 fusion.16
  21.7 9.4 %collective-permute-done.1 = bf16[64,1,128]{0,2,1:T(8,128)(2,1)} collective-permute-done((bf16[64,1,128]{0,2,1:T(8,128)(2,1)}, bf16[64,1,128]{0,2,1:T(8,128)(2,1)}, u32[]{:S(2)}, u32[]{:S(2)}) %collective-permute-start.1) | collective-permute-done | bytes 16416 | tf_op jit(solution)/shard_map/ppermute | solution.py:23
  36.7 1.7 gather_fusion.2
  38.4 2.1 constant_dynamic-update-slice_fusion.46
  40.6 1.9 collective-permute-start.6
  42.5 4.9 %collective-permute-start.7 = (bf16[64,256]{1,0:T(8,128)(2,1)S(1)}, bf16[64,256]{1,0:T(8,128)(2,1)S(1)}, u32[]{:S(2)}, u32[]{:S(2)}) collective-permute-start(bf16[64,256]{1,0:T(8,128)(2,1)S(1)} %get-tuple-element.18), channel_id=1, source_target_pairs={{32,0},{64,32},{96,64},{128,96},{160,128},{192,160},{224,192},{256... | collective-permute-start | bytes 98312 | tf_op jit(solution)/shard_map/ppermute | solution.py:31
  47.4 6.7 %collective-permute-start.4 = (bf16[64,1,128]{2,0,1:T(8,128)(2,1)S(1)}, bf16[64,1,128]{2,0,1:T(8,128)(2,1)S(1)}, u32[]{:S(2)}, u32[]{:S(2)}) collective-permute-start(bf16[64,1,128]{2,0,1:T(8,128)(2,1)S(1)} %copy.254), channel_id=1, source_target_pairs={{0,1},{1,2},{2,3},{3,4},{4,5},{5,6},{6,7},{7,8},{8,9},{9,10},{10,1... | collective-permute-start | bytes 49160 | tf_op jit(solution)/shard_map/ppermute | solution.py:22
  54.2 1.7 fusion.19
  55.9 1.9 collective-permute-start.5
  57.9 16.6 %collective-permute-done.5 = bf16[64,1,128]{2,0,1:T(8,128)(2,1)S(1)} collective-permute-done((bf16[64,1,128]{2,0,1:T(8,128)(2,1)S(1)}, bf16[64,1,128]{2,0,1:T(8,128)(2,1)S(1)}, u32[]{:S(2)}, u32[]{:S(2)}) %collective-permute-start.5) | collective-permute-done | bytes 16416 | tf_op jit(solution)/shard_map/ppermute | solution.py:23
  80.2 1.7 gather_fusion.4
  81.9 2.1 constant_dynamic-update-slice_fusion.45
  84.7 1.9 collective-permute-start.10
  86.6 4.9 %collective-permute-start.11 = (bf16[64,256]{1,0:T(8,128)(2,1)S(1)}, bf16[64,256]{1,0:T(8,128)(2,1)S(1)}, u32[]{:S(2)}, u32[]{:S(2)}) collective-permute-start(bf16[64,256]{1,0:T(8,128)(2,1)S(1)} %get-tuple-element.16), channel_id=1, source_target_pairs={{32,0},{64,32},{96,64},{128,96},{160,128},{192,160},{224,192},{256... | collective-permute-start | bytes 98312 | tf_op jit(solution)/shard_map/ppermute | solution.py:31
  91.5 1.9 collective-permute-start.8
  93.4 1.7 fusion.22
  95.2 3.9 %collective-permute-start.9 = (bf16[64,1,128]{2,0,1:T(8,128)(2,1)S(1)}, bf16[64,1,128]{2,0,1:T(8,128)(2,1)S(1)}, u32[]{:S(2)}, u32[]{:S(2)}) collective-permute-start(bf16[64,1,128]{2,0,1:T(8,128)(2,1)S(1)} %copy.257), channel_id=1, source_target_pairs={{1,0},{2,1},{3,2},{4,3},{5,4},{6,5},{7,6},{8,7},{9,8},{10,9},{11,1... | collective-permute-start | bytes 49160 | tf_op jit(solution)/shard_map/ppermute | solution.py:23
  99.7 14.0 %collective-permute-done.9 = bf16[64,1,128]{2,0,1:T(8,128)(2,1)S(1)} collective-permute-done((bf16[64,1,128]{2,0,1:T(8,128)(2,1)S(1)}, bf16[64,1,128]{2,0,1:T(8,128)(2,1)S(1)}, u32[]{:S(2)}, u32[]{:S(2)}) %collective-permute-start.9) | collective-permute-done | bytes 16416 | tf_op jit(solution)/shard_map/ppermute | solution.py:23
  120.0 1.7 gather_fusion.6
  121.7 2.1 constant_dynamic-update-slice_fusion.44
  124.5 1.9 collective-permute-start.14
  126.4 4.9 %collective-permute-start.15 = (bf16[64,256]{1,0:T(8,128)(2,1)S(1)}, bf16[64,256]{1,0:T(8,128)(2,1)S(1)}, u32[]{:S(2)}, u32[]{:S(2)}) collective-permute-start(bf16[64,256]{1,0:T(8,128)(2,1)S(1)} %get-tuple-element.14), channel_id=1, source_target_pairs={{32,0},{64,32},{96,64},{128,96},{160,128},{192,160},{224,192},{256... | collective-permute-start | bytes 98312 | tf_op jit(solution)/shard_map/ppermute | solution.py:31
  131.4 1.9 collective-permute-start.12
  133.3 1.7 fusion.25
  135.0 3.9 %collective-permute-start.13 = (bf16[64,1,128]{2,0,1:T(8,128)(2,1)S(1)}, bf16[64,1,128]{2,0,1:T(8,128)(2,1)S(1)}, u32[]{:S(2)}, u32[]{:S(2)}) collective-permute-start(bf16[64,1,128]{2,0,1:T(8,128)(2,1)S(1)} %copy.259), channel_id=1, source_target_pairs={{1,0},{2,1},{3,2},{4,3},{5,4},{6,5},{7,6},{8,7},{9,8},{10,9},{11,1... | collective-permute-start | bytes 49160 | tf_op jit(solution)/shard_map/ppermute | solution.py:23
  139.6 14.0 %collective-permute-done.13 = bf16[64,1,128]{2,0,1:T(8,128)(2,1)S(1)} collective-permute-done((bf16[64,1,128]{2,0,1:T(8,128)(2,1)S(1)}, bf16[64,1,128]{2,0,1:T(8,128)(2,1)S(1)}, u32[]{:S(2)}, u32[]{:S(2)}) %collective-permute-start.13) | collective-permute-done | bytes 16416 | tf_op jit(solution)/shard_map/ppermute | solution.py:23
  159.9 1.7 gather_fusion.8
  161.6 2.1 constant_dynamic-update-slice_fusion.43
  164.4 1.9 collective-permute-start.18
  166.3 4.9 %collective-permute-start.19 = (bf16[64,256]{1,0:T(8,128)(2,1)S(1)}, bf16[64,256]{1,0:T(8,128)(2,1)S(1)}, u32[]{:S(2)}, u32[]{:S(2)}) collective-permute-start(bf16[64,256]{1,0:T(8,128)(2,1)S(1)} %get-tuple-element.12), channel_id=1, source_target_pairs={{32,0},{64,32},{96,64},{128,96},{160,128},{192,160},{224,192},{256... | collective-permute-start | bytes 98312 | tf_op jit(solution)/shard_map/ppermute | solution.py:31
  171.2 1.9 collective-permute-start.16
  173.2 1.7 fusion.28
  174.9 3.9 %collective-permute-start.17 = (bf16[64,1,128]{2,0,1:T(8,128)(2,1)S(1)}, bf16[64,1,128]{2,0,1:T(8,128)(2,1)S(1)}, u32[]{:S(2)}, u32[]{:S(2)}) collective-permute-start(bf16[64,1,128]{2,0,1:T(8,128)(2,1)S(1)} %copy.261), channel_id=1, source_target_pairs={{1,0},{2,1},{3,2},{4,3},{5,4},{6,5},{7,6},{8,7},{9,8},{10,9},{11,1... | collective-permute-start | bytes 49160 | tf_op jit(solution)/shard_map/ppermute | solution.py:23
  179.4 14.0 %collective-permute-done.17 = bf16[64,1,128]{2,0,1:T(8,128)(2,1)S(1)} collective-permute-done((bf16[64,1,128]{2,0,1:T(8,128)(2,1)S(1)}, bf16[64,1,128]{2,0,1:T(8,128)(2,1)S(1)}, u32[]{:S(2)}, u32[]{:S(2)}) %collective-permute-start.17) | collective-permute-done | bytes 16416 | tf_op jit(solution)/shard_map/ppermute | solution.py:23
  199.8 1.7 gather_fusion.10
  201.5 2.1 constant_dynamic-update-slice_fusion.42
  204.2 1.9 collective-permute-start.22
  206.2 4.9 %collective-permute-start.23 = (bf16[64,256]{1,0:T(8,128)(2,1)S(1)}, bf16[64,256]{1,0:T(8,128)(2,1)S(1)}, u32[]{:S(2)}, u32[]{:S(2)}) collective-permute-start(bf16[64,256]{1,0:T(8,128)(2,1)S(1)} %get-tuple-element.10), channel_id=1, source_target_pairs={{32,0},{64,32},{96,64},{128,96},{160,128},{192,160},{224,192},{256... | collective-permute-start | bytes 98312 | tf_op jit(solution)/shard_map/ppermute | solution.py:31
  211.1 1.9 collective-permute-start.20
  213.0 1.7 fusion.31
  214.8 3.9 %collective-permute-start.21 = (bf16[64,1,128]{2,0,1:T(8,128)(2,1)S(1)}, bf16[64,1,128]{2,0,1:T(8,128)(2,1)S(1)}, u32[]{:S(2)}, u32[]{:S(2)}) collective-permute-start(bf16[64,1,128]{2,0,1:T(8,128)(2,1)S(1)} %copy.263), channel_id=1, source_target_pairs={{1,0},{2,1},{3,2},{4,3},{5,4},{6,5},{7,6},{8,7},{9,8},{10,9},{11,1... | collective-permute-start | bytes 49160 | tf_op jit(solution)/shard_map/ppermute | solution.py:23
  219.3 14.0 %collective-permute-done.21 = bf16[64,1,128]{2,0,1:T(8,128)(2,1)S(1)} collective-permute-done((bf16[64,1,128]{2,0,1:T(8,128)(2,1)S(1)}, bf16[64,1,128]{2,0,1:T(8,128)(2,1)S(1)}, u32[]{:S(2)}, u32[]{:S(2)}) %collective-permute-start.21) | collective-permute-done | bytes 16416 | tf_op jit(solution)/shard_map/ppermute | solution.py:23
  239.6 1.7 gather_fusion.12
  241.3 2.1 constant_dynamic-update-slice_fusion.41
  244.1 1.9 collective-permute-start.26
  246.0 4.9 %collective-permute-start.27 = (bf16[64,256]{1,0:T(8,128)(2,1)S(1)}, bf16[64,256]{1,0:T(8,128)(2,1)S(1)}, u32[]{:S(2)}, u32[]{:S(2)}) collective-permute-start(bf16[64,256]{1,0:T(8,128)(2,1)S(1)} %get-tuple-element.8), channel_id=1, source_target_pairs={{32,0},{64,32},{96,64},{128,96},{160,128},{192,160},{224,192},{256... | collective-permute-start | bytes 98312 | tf_op jit(solution)/shard_map/ppermute | solution.py:31
  250.9 1.9 collective-permute-start.24
  252.9 1.7 fusion.34
  254.6 4.1 %collective-permute-start.25 = (bf16[64,1,128]{2,0,1:T(8,128)(2,1)S(1)}, bf16[64,1,128]{2,0,1:T(8,128)(2,1)S(1)}, u32[]{:S(2)}, u32[]{:S(2)}) collective-permute-start(bf16[64,1,128]{2,0,1:T(8,128)(2,1)S(1)} %copy.265), channel_id=1, source_target_pairs={{1,0},{2,1},{3,2},{4,3},{5,4},{6,5},{7,6},{8,7},{9,8},{10,9},{11,1... | collective-permute-start | bytes 49160 | tf_op jit(solution)/shard_map/ppermute | solution.py:23
  259.3 13.8 %collective-permute-done.25 = bf16[64,1,128]{2,0,1:T(8,128)(2,1)S(1)} collective-permute-done((bf16[64,1,128]{2,0,1:T(8,128)(2,1)S(1)}, bf16[64,1,128]{2,0,1:T(8,128)(2,1)S(1)}, u32[]{:S(2)}, u32[]{:S(2)}) %collective-permute-start.25) | collective-permute-done | bytes 16416 | tf_op jit(solution)/shard_map/ppermute | solution.py:23
  279.5 1.7 gather_fusion.14
  281.2 2.1 constant_dynamic-update-slice_fusion.40
  283.9 1.9 collective-permute-start.30
  285.9 4.9 %collective-permute-start.31 = (bf16[64,256]{1,0:T(8,128)(2,1)S(1)}, bf16[64,256]{1,0:T(8,128)(2,1)S(1)}, u32[]{:S(2)}, u32[]{:S(2)}) collective-permute-start(bf16[64,256]{1,0:T(8,128)(2,1)S(1)} %get-tuple-element.6), channel_id=1, source_target_pairs={{32,0},{64,32},{96,64},{128,96},{160,128},{192,160},{224,192},{256... | collective-permute-start | bytes 98312 | tf_op jit(solution)/shard_map/ppermute | solution.py:31
  290.8 1.9 collective-permute-start.28
  292.7 1.7 fusion.37
  294.5 3.9 %collective-permute-start.29 = (bf16[64,1,128]{2,0,1:T(8,128)(2,1)S(1)}, bf16[64,1,128]{2,0,1:T(8,128)(2,1)S(1)}, u32[]{:S(2)}, u32[]{:S(2)}) collective-permute-start(bf16[64,1,128]{2,0,1:T(8,128)(2,1)S(1)} %copy.267), channel_id=1, source_target_pairs={{1,0},{2,1},{3,2},{4,3},{5,4},{6,5},{7,6},{8,7},{9,8},{10,9},{11,1... | collective-permute-start | bytes 49160 | tf_op jit(solution)/shard_map/ppermute | solution.py:23
  299.0 14.0 %collective-permute-done.29 = bf16[64,1,128]{2,0,1:T(8,128)(2,1)S(1)} collective-permute-done((bf16[64,1,128]{2,0,1:T(8,128)(2,1)S(1)}, bf16[64,1,128]{2,0,1:T(8,128)(2,1)S(1)}, u32[]{:S(2)}, u32[]{:S(2)}) %collective-permute-start.29) | collective-permute-done | bytes 16416 | tf_op jit(solution)/shard_map/ppermute | solution.py:23
  317.7 2.2 fusion.65
  (195 shorter events, 60.2 us)
Async XLA Ops:
  0.0 18.6 %copy-start = (bf16[1,1,16,4,128,128]{5,4,3,2,1,0:T(8,128)(2,1)S(1)}, bf16[1,1,16,4,128,128]{5,4,3,2,1,0:T(8,128)(2,1)}, u32[]{:S(2)}) copy-start(bf16[1,1,16,4,128,128]{5,4,3,2,1,0:T(8,128)(2,1)} %param.26) | copy-start | bytes 6291460
  1.1 30.8 %collective-permute-start.2 = (bf16[64,256]{0,1:T(8,128)(2,1)S(1)}, bf16[64,256]{0,1:T(8,128)(2,1)S(1)}, u32[]{:S(2)}, u32[]{:S(2)}) collective-permute-start(bf16[64,256]{0,1:T(8,128)(2,1)S(1)} %bitcast.444), channel_id=1, source_target_pairs={{0,32},{32,64},{64,96},{96,128},{128,160},{160,192},{192,224},{224... | collective-permute-start | bytes 98312 | tf_op jit(solution)/shard_map/ppermute | solution.py:31
  3.0 29.1 %collective-permute-start.3 = (bf16[64,256]{0,1:T(8,128)(2,1)S(1)}, bf16[64,256]{0,1:T(8,128)(2,1)S(1)}, u32[]{:S(2)}, u32[]{:S(2)}) collective-permute-start(bf16[64,256]{0,1:T(8,128)(2,1)S(1)} %bitcast.445), channel_id=1, source_target_pairs={{32,0},{64,32},{96,64},{128,96},{160,128},{192,160},{224,192},{256... | collective-permute-start | bytes 98312 | tf_op jit(solution)/shard_map/ppermute | solution.py:31
  8.5 12.5 %collective-permute-start = (bf16[64,1,128]{0,2,1:T(8,128)(2,1)}, bf16[64,1,128]{0,2,1:T(8,128)(2,1)}, u32[]{:S(2)}, u32[]{:S(2)}) collective-permute-start(bf16[64,1,128]{0,2,1:T(8,128)(2,1)} %get-tuple-element.20), channel_id=1, source_target_pairs={{0,1},{1,2},{2,3},{3,4},{4,5},{5,6},{6,7},{7,8},{8,9},{9,10},{10,1... | collective-permute-start | bytes 49160 | tf_op jit(solution)/shard_map/ppermute | solution.py:22
  11.7 19.4 %collective-permute-start.1 = (bf16[64,1,128]{0,2,1:T(8,128)(2,1)}, bf16[64,1,128]{0,2,1:T(8,128)(2,1)}, u32[]{:S(2)}, u32[]{:S(2)}) collective-permute-start(bf16[64,1,128]{0,2,1:T(8,128)(2,1)} %get-tuple-element.19), channel_id=1, source_target_pairs={{1,0},{2,1},{3,2},{4,3},{5,4},{6,5},{7,6},{8,7},{9,8},{10,9},{11,1... | collective-permute-start | bytes 49160 | tf_op jit(solution)/shard_map/ppermute | solution.py:23
  16.9 17.3 %copy-start.4 = (s32[1024]{0:T(1024)}, s32[1024]{0:T(1024)S(1)}, u32[]{:S(2)}) copy-start(s32[1024]{0:T(1024)S(1)} %get-tuple-element.51) | copy-start | bytes 12292
  18.6 16.8 %copy-start.1 = (bf16[1,1,16,128,128]{4,3,2,1,0:T(8,128)(2,1)S(1)}, bf16[1,1,16,128,128]{4,3,2,1,0:T(8,128)(2,1)}, u32[]{:S(2)}) copy-start(bf16[1,1,16,128,128]{4,3,2,1,0:T(8,128)(2,1)} %param.27) | copy-start | bytes 1572868
  32.4 0.7 copy-start.2
  34.2 4.2 %copy-start.5 = (pred[16,128]{1,0:T(8,128)(4,1)S(1)}, pred[16,128]{1,0:T(8,128)(4,1)}, u32[]{:S(2)}) copy-start(pred[16,128]{1,0:T(8,128)(4,1)} %fusion.161) | copy-start | bytes 6148
  40.6 33.9 %collective-permute-start.6 = (bf16[64,256]{1,0:T(8,128)(2,1)S(1)}, bf16[64,256]{1,0:T(8,128)(2,1)S(1)}, u32[]{:S(2)}, u32[]{:S(2)}) collective-permute-start(bf16[64,256]{1,0:T(8,128)(2,1)S(1)} %get-tuple-element.18), channel_id=1, source_target_pairs={{0,32},{32,64},{64,96},{96,128},{128,160},{160,192},{192,224},{224... | collective-permute-start | bytes 98312 | tf_op jit(solution)/shard_map/ppermute | solution.py:31
  42.5 32.4 %collective-permute-start.7 = (bf16[64,256]{1,0:T(8,128)(2,1)S(1)}, bf16[64,256]{1,0:T(8,128)(2,1)S(1)}, u32[]{:S(2)}, u32[]{:S(2)}) collective-permute-start(bf16[64,256]{1,0:T(8,128)(2,1)S(1)} %get-tuple-element.18), channel_id=1, source_target_pairs={{32,0},{64,32},{96,64},{128,96},{160,128},{192,160},{224,192},{256... | collective-permute-start | bytes 98312 | tf_op jit(solution)/shard_map/ppermute | solution.py:31
  47.4 10.4 %collective-permute-start.4 = (bf16[64,1,128]{2,0,1:T(8,128)(2,1)S(1)}, bf16[64,1,128]{2,0,1:T(8,128)(2,1)S(1)}, u32[]{:S(2)}, u32[]{:S(2)}) collective-permute-start(bf16[64,1,128]{2,0,1:T(8,128)(2,1)S(1)} %copy.254), channel_id=1, source_target_pairs={{0,1},{1,2},{2,3},{3,4},{4,5},{5,6},{6,7},{7,8},{8,9},{9,10},{10,1... | collective-permute-start | bytes 49160 | tf_op jit(solution)/shard_map/ppermute | solution.py:22
  55.9 18.6 %collective-permute-start.5 = (bf16[64,1,128]{2,0,1:T(8,128)(2,1)S(1)}, bf16[64,1,128]{2,0,1:T(8,128)(2,1)S(1)}, u32[]{:S(2)}, u32[]{:S(2)}) collective-permute-start(bf16[64,1,128]{2,0,1:T(8,128)(2,1)S(1)} %copy.255), channel_id=1, source_target_pairs={{1,0},{2,1},{3,2},{4,3},{5,4},{6,5},{7,6},{8,7},{9,8},{10,9},{11,1... | collective-permute-start | bytes 49160 | tf_op jit(solution)/shard_map/ppermute | solution.py:23
  74.5 0.9 copy-start.3
  84.7 29.7 %collective-permute-start.10 = (bf16[64,256]{1,0:T(8,128)(2,1)S(1)}, bf16[64,256]{1,0:T(8,128)(2,1)S(1)}, u32[]{:S(2)}, u32[]{:S(2)}) collective-permute-start(bf16[64,256]{1,0:T(8,128)(2,1)S(1)} %get-tuple-element.16), channel_id=1, source_target_pairs={{0,32},{32,64},{64,96},{96,128},{128,160},{160,192},{192,224},{224... | collective-permute-start | bytes 98312 | tf_op jit(solution)/shard_map/ppermute | solution.py:31
  86.6 28.2 %collective-permute-start.11 = (bf16[64,256]{1,0:T(8,128)(2,1)S(1)}, bf16[64,256]{1,0:T(8,128)(2,1)S(1)}, u32[]{:S(2)}, u32[]{:S(2)}) collective-permute-start(bf16[64,256]{1,0:T(8,128)(2,1)S(1)} %get-tuple-element.16), channel_id=1, source_target_pairs={{32,0},{64,32},{96,64},{128,96},{160,128},{192,160},{224,192},{256... | collective-permute-start | bytes 98312 | tf_op jit(solution)/shard_map/ppermute | solution.py:31
  91.5 7.6 %collective-permute-start.8 = (bf16[64,1,128]{2,0,1:T(8,128)(2,1)S(1)}, bf16[64,1,128]{2,0,1:T(8,128)(2,1)S(1)}, u32[]{:S(2)}, u32[]{:S(2)}) collective-permute-start(bf16[64,1,128]{2,0,1:T(8,128)(2,1)S(1)} %copy.256), channel_id=1, source_target_pairs={{0,1},{1,2},{2,3},{3,4},{4,5},{5,6},{6,7},{7,8},{8,9},{9,10},{10,1... | collective-permute-start | bytes 49160 | tf_op jit(solution)/shard_map/ppermute | solution.py:22
  95.2 18.6 %collective-permute-start.9 = (bf16[64,1,128]{2,0,1:T(8,128)(2,1)S(1)}, bf16[64,1,128]{2,0,1:T(8,128)(2,1)S(1)}, u32[]{:S(2)}, u32[]{:S(2)}) collective-permute-start(bf16[64,1,128]{2,0,1:T(8,128)(2,1)S(1)} %copy.257), channel_id=1, source_target_pairs={{1,0},{2,1},{3,2},{4,3},{5,4},{6,5},{7,6},{8,7},{9,8},{10,9},{11,1... | collective-permute-start | bytes 49160 | tf_op jit(solution)/shard_map/ppermute | solution.py:23
  124.5 29.7 %collective-permute-start.14 = (bf16[64,256]{1,0:T(8,128)(2,1)S(1)}, bf16[64,256]{1,0:T(8,128)(2,1)S(1)}, u32[]{:S(2)}, u32[]{:S(2)}) collective-permute-start(bf16[64,256]{1,0:T(8,128)(2,1)S(1)} %get-tuple-element.14), channel_id=1, source_target_pairs={{0,32},{32,64},{64,96},{96,128},{128,160},{160,192},{192,224},{224... | collective-permute-start | bytes 98312 | tf_op jit(solution)/shard_map/ppermute | solution.py:31
  126.4 28.2 %collective-permute-start.15 = (bf16[64,256]{1,0:T(8,128)(2,1)S(1)}, bf16[64,256]{1,0:T(8,128)(2,1)S(1)}, u32[]{:S(2)}, u32[]{:S(2)}) collective-permute-start(bf16[64,256]{1,0:T(8,128)(2,1)S(1)} %get-tuple-element.14), channel_id=1, source_target_pairs={{32,0},{64,32},{96,64},{128,96},{160,128},{192,160},{224,192},{256... | collective-permute-start | bytes 98312 | tf_op jit(solution)/shard_map/ppermute | solution.py:31
  131.4 7.6 %collective-permute-start.12 = (bf16[64,1,128]{2,0,1:T(8,128)(2,1)S(1)}, bf16[64,1,128]{2,0,1:T(8,128)(2,1)S(1)}, u32[]{:S(2)}, u32[]{:S(2)}) collective-permute-start(bf16[64,1,128]{2,0,1:T(8,128)(2,1)S(1)} %copy.258), channel_id=1, source_target_pairs={{0,1},{1,2},{2,3},{3,4},{4,5},{5,6},{6,7},{7,8},{8,9},{9,10},{10,1... | collective-permute-start | bytes 49160 | tf_op jit(solution)/shard_map/ppermute | solution.py:22
  135.0 18.6 %collective-permute-start.13 = (bf16[64,1,128]{2,0,1:T(8,128)(2,1)S(1)}, bf16[64,1,128]{2,0,1:T(8,128)(2,1)S(1)}, u32[]{:S(2)}, u32[]{:S(2)}) collective-permute-start(bf16[64,1,128]{2,0,1:T(8,128)(2,1)S(1)} %copy.259), channel_id=1, source_target_pairs={{1,0},{2,1},{3,2},{4,3},{5,4},{6,5},{7,6},{8,7},{9,8},{10,9},{11,1... | collective-permute-start | bytes 49160 | tf_op jit(solution)/shard_map/ppermute | solution.py:23
  164.4 29.7 %collective-permute-start.18 = (bf16[64,256]{1,0:T(8,128)(2,1)S(1)}, bf16[64,256]{1,0:T(8,128)(2,1)S(1)}, u32[]{:S(2)}, u32[]{:S(2)}) collective-permute-start(bf16[64,256]{1,0:T(8,128)(2,1)S(1)} %get-tuple-element.12), channel_id=1, source_target_pairs={{0,32},{32,64},{64,96},{96,128},{128,160},{160,192},{192,224},{224... | collective-permute-start | bytes 98312 | tf_op jit(solution)/shard_map/ppermute | solution.py:31
  166.3 28.2 %collective-permute-start.19 = (bf16[64,256]{1,0:T(8,128)(2,1)S(1)}, bf16[64,256]{1,0:T(8,128)(2,1)S(1)}, u32[]{:S(2)}, u32[]{:S(2)}) collective-permute-start(bf16[64,256]{1,0:T(8,128)(2,1)S(1)} %get-tuple-element.12), channel_id=1, source_target_pairs={{32,0},{64,32},{96,64},{128,96},{160,128},{192,160},{224,192},{256... | collective-permute-start | bytes 98312 | tf_op jit(solution)/shard_map/ppermute | solution.py:31
  171.2 7.6 %collective-permute-start.16 = (bf16[64,1,128]{2,0,1:T(8,128)(2,1)S(1)}, bf16[64,1,128]{2,0,1:T(8,128)(2,1)S(1)}, u32[]{:S(2)}, u32[]{:S(2)}) collective-permute-start(bf16[64,1,128]{2,0,1:T(8,128)(2,1)S(1)} %copy.260), channel_id=1, source_target_pairs={{0,1},{1,2},{2,3},{3,4},{4,5},{5,6},{6,7},{7,8},{8,9},{9,10},{10,1... | collective-permute-start | bytes 49160 | tf_op jit(solution)/shard_map/ppermute | solution.py:22
  174.9 18.6 %collective-permute-start.17 = (bf16[64,1,128]{2,0,1:T(8,128)(2,1)S(1)}, bf16[64,1,128]{2,0,1:T(8,128)(2,1)S(1)}, u32[]{:S(2)}, u32[]{:S(2)}) collective-permute-start(bf16[64,1,128]{2,0,1:T(8,128)(2,1)S(1)} %copy.261), channel_id=1, source_target_pairs={{1,0},{2,1},{3,2},{4,3},{5,4},{6,5},{7,6},{8,7},{9,8},{10,9},{11,1... | collective-permute-start | bytes 49160 | tf_op jit(solution)/shard_map/ppermute | solution.py:23
  204.2 29.7 %collective-permute-start.22 = (bf16[64,256]{1,0:T(8,128)(2,1)S(1)}, bf16[64,256]{1,0:T(8,128)(2,1)S(1)}, u32[]{:S(2)}, u32[]{:S(2)}) collective-permute-start(bf16[64,256]{1,0:T(8,128)(2,1)S(1)} %get-tuple-element.10), channel_id=1, source_target_pairs={{0,32},{32,64},{64,96},{96,128},{128,160},{160,192},{192,224},{224... | collective-permute-start | bytes 98312 | tf_op jit(solution)/shard_map/ppermute | solution.py:31
  206.2 28.2 %collective-permute-start.23 = (bf16[64,256]{1,0:T(8,128)(2,1)S(1)}, bf16[64,256]{1,0:T(8,128)(2,1)S(1)}, u32[]{:S(2)}, u32[]{:S(2)}) collective-permute-start(bf16[64,256]{1,0:T(8,128)(2,1)S(1)} %get-tuple-element.10), channel_id=1, source_target_pairs={{32,0},{64,32},{96,64},{128,96},{160,128},{192,160},{224,192},{256... | collective-permute-start | bytes 98312 | tf_op jit(solution)/shard_map/ppermute | solution.py:31
  211.1 7.6 %collective-permute-start.20 = (bf16[64,1,128]{2,0,1:T(8,128)(2,1)S(1)}, bf16[64,1,128]{2,0,1:T(8,128)(2,1)S(1)}, u32[]{:S(2)}, u32[]{:S(2)}) collective-permute-start(bf16[64,1,128]{2,0,1:T(8,128)(2,1)S(1)} %copy.262), channel_id=1, source_target_pairs={{0,1},{1,2},{2,3},{3,4},{4,5},{5,6},{6,7},{7,8},{8,9},{9,10},{10,1... | collective-permute-start | bytes 49160 | tf_op jit(solution)/shard_map/ppermute | solution.py:22
  214.8 18.6 %collective-permute-start.21 = (bf16[64,1,128]{2,0,1:T(8,128)(2,1)S(1)}, bf16[64,1,128]{2,0,1:T(8,128)(2,1)S(1)}, u32[]{:S(2)}, u32[]{:S(2)}) collective-permute-start(bf16[64,1,128]{2,0,1:T(8,128)(2,1)S(1)} %copy.263), channel_id=1, source_target_pairs={{1,0},{2,1},{3,2},{4,3},{5,4},{6,5},{7,6},{8,7},{9,8},{10,9},{11,1... | collective-permute-start | bytes 49160 | tf_op jit(solution)/shard_map/ppermute | solution.py:23
  244.1 29.7 %collective-permute-start.26 = (bf16[64,256]{1,0:T(8,128)(2,1)S(1)}, bf16[64,256]{1,0:T(8,128)(2,1)S(1)}, u32[]{:S(2)}, u32[]{:S(2)}) collective-permute-start(bf16[64,256]{1,0:T(8,128)(2,1)S(1)} %get-tuple-element.8), channel_id=1, source_target_pairs={{0,32},{32,64},{64,96},{96,128},{128,160},{160,192},{192,224},{224... | collective-permute-start | bytes 98312 | tf_op jit(solution)/shard_map/ppermute | solution.py:31
  246.0 28.2 %collective-permute-start.27 = (bf16[64,256]{1,0:T(8,128)(2,1)S(1)}, bf16[64,256]{1,0:T(8,128)(2,1)S(1)}, u32[]{:S(2)}, u32[]{:S(2)}) collective-permute-start(bf16[64,256]{1,0:T(8,128)(2,1)S(1)} %get-tuple-element.8), channel_id=1, source_target_pairs={{32,0},{64,32},{96,64},{128,96},{160,128},{192,160},{224,192},{256... | collective-permute-start | bytes 98312 | tf_op jit(solution)/shard_map/ppermute | solution.py:31
  250.9 7.8 %collective-permute-start.24 = (bf16[64,1,128]{2,0,1:T(8,128)(2,1)S(1)}, bf16[64,1,128]{2,0,1:T(8,128)(2,1)S(1)}, u32[]{:S(2)}, u32[]{:S(2)}) collective-permute-start(bf16[64,1,128]{2,0,1:T(8,128)(2,1)S(1)} %copy.264), channel_id=1, source_target_pairs={{0,1},{1,2},{2,3},{3,4},{4,5},{5,6},{6,7},{7,8},{8,9},{9,10},{10,1... | collective-permute-start | bytes 49160 | tf_op jit(solution)/shard_map/ppermute | solution.py:22
  254.6 18.6 %collective-permute-start.25 = (bf16[64,1,128]{2,0,1:T(8,128)(2,1)S(1)}, bf16[64,1,128]{2,0,1:T(8,128)(2,1)S(1)}, u32[]{:S(2)}, u32[]{:S(2)}) collective-permute-start(bf16[64,1,128]{2,0,1:T(8,128)(2,1)S(1)} %copy.265), channel_id=1, source_target_pairs={{1,0},{2,1},{3,2},{4,3},{5,4},{6,5},{7,6},{8,7},{9,8},{10,9},{11,1... | collective-permute-start | bytes 49160 | tf_op jit(solution)/shard_map/ppermute | solution.py:23
  283.9 29.7 %collective-permute-start.30 = (bf16[64,256]{1,0:T(8,128)(2,1)S(1)}, bf16[64,256]{1,0:T(8,128)(2,1)S(1)}, u32[]{:S(2)}, u32[]{:S(2)}) collective-permute-start(bf16[64,256]{1,0:T(8,128)(2,1)S(1)} %get-tuple-element.6), channel_id=1, source_target_pairs={{0,32},{32,64},{64,96},{96,128},{128,160},{160,192},{192,224},{224... | collective-permute-start | bytes 98312 | tf_op jit(solution)/shard_map/ppermute | solution.py:31
  285.9 28.2 %collective-permute-start.31 = (bf16[64,256]{1,0:T(8,128)(2,1)S(1)}, bf16[64,256]{1,0:T(8,128)(2,1)S(1)}, u32[]{:S(2)}, u32[]{:S(2)}) collective-permute-start(bf16[64,256]{1,0:T(8,128)(2,1)S(1)} %get-tuple-element.6), channel_id=1, source_target_pairs={{32,0},{64,32},{96,64},{128,96},{160,128},{192,160},{224,192},{256... | collective-permute-start | bytes 98312 | tf_op jit(solution)/shard_map/ppermute | solution.py:31
  290.8 7.6 %collective-permute-start.28 = (bf16[64,1,128]{2,0,1:T(8,128)(2,1)S(1)}, bf16[64,1,128]{2,0,1:T(8,128)(2,1)S(1)}, u32[]{:S(2)}, u32[]{:S(2)}) collective-permute-start(bf16[64,1,128]{2,0,1:T(8,128)(2,1)S(1)} %copy.266), channel_id=1, source_target_pairs={{0,1},{1,2},{2,3},{3,4},{4,5},{5,6},{6,7},{7,8},{8,9},{9,10},{10,1... | collective-permute-start | bytes 49160 | tf_op jit(solution)/shard_map/ppermute | solution.py:22
  294.5 18.6 %collective-permute-start.29 = (bf16[64,1,128]{2,0,1:T(8,128)(2,1)S(1)}, bf16[64,1,128]{2,0,1:T(8,128)(2,1)S(1)}, u32[]{:S(2)}, u32[]{:S(2)}) collective-permute-start(bf16[64,1,128]{2,0,1:T(8,128)(2,1)S(1)} %copy.267), channel_id=1, source_target_pairs={{1,0},{2,1},{3,2},{4,3},{5,4},{6,5},{7,6},{8,7},{9,8},{10,9},{11,1... | collective-permute-start | bytes 49160 | tf_op jit(solution)/shard_map/ppermute | solution.py:23
where the time goes:
time: 322 us; the launch traced here: 320 us
  waiting for transfers between devices  110 us (34%)
  starting transfers between devices  104 us (32%)
  local copies, waits for them, and re-layouts  60.3 us (19%)
  matrix products  43.3 us (13%)
    ppermute x8, waiting for transfers between devices, with_halo(): after = lax.ppermute(initial, axis, down)  110 us
    ppermute x16, starting transfers between devices, shifted(): return lax.ppermute(value, axis, pairs)  54.2 us
    ppermute x8, starting transfers between devices, with_halo(): after = lax.ppermute(initial, axis, down)  28.2 us
    ppermute x8, starting transfers between devices, with_halo(): before = lax.ppermute(last, axis, up)  21.5 us
    unnamed x60, local copies, waits for them, and re-layouts  19.6 us
    dot_general x8, matrix products, per_device(): current = jnp.dot(features, read_weight, preferred_element_type=jnp.float32)  17.2 us
    dot_general x8, matrix products, per_device(): jnp.einsum('mbki,bkio->mbo', blocks[:, linked], block_weight, preferred_e...  13.8 us
    gather x8, local copies, waits for them, and re-layouts, per_device(): blocks[:, linked]  13.6 us
  transfers between devices with their start and end apart: 32, of which 8 were waited for; matrix products, arithmetic and copies ran while one was open for 10% of the time, Pallas kernels for 0%

commit v1 on v0

v1 whole, which is shorter than its diff:
```python
import jax
import jax.numpy as jnp
import numpy as np
from jax import lax
from jax.experimental import pallas as pl
from jax.experimental.pallas import tpu as pltpu
from jax.sharding import PartitionSpec as P

VARS = 32
LATR = 4
LONC = 2
OV = 4
STEPS = 8
PTS = 8


def shifted(value, axis, by):
    peers = lax.axis_size(axis)
    pairs = [(i, i + by) for i in range(peers) if 0 <= i + by < peers]
    return lax.ppermute(value, axis, pairs)


def ring(value, axis, by):
    peers = lax.axis_size(axis)
    return lax.ppermute(value, axis, [(i, (i + by) % peers) for i in range(peers)])


def selector(slot_list, breadth):
    onehot = (slot_list[:, None] == jnp.arange(PTS, dtype=jnp.int32)[None, :]).astype(jnp.bfloat16)
    eye = jnp.eye(VARS, dtype=jnp.bfloat16)
    full = onehot.T[:, None, :, None] * eye[None, :, None, :]
    return full.reshape(PTS * VARS, OV * VARS)


def step_kernel(u_ref, w_ref, e_ref, n_ref, s_ref, sn_ref, ss_ref, r_ref, c_ref, win_ref, ro_ref,
                f_out, u_out, lo_out, hi_out, r_out, feat_scr):
    members, half = lo_out.shape
    res_blocks, links, breadth, _ = c_ref.shape
    u = u_ref[...]
    north = jnp.dot(n_ref[...], sn_ref[...], preferred_element_type=jnp.float32).astype(jnp.bfloat16)
    south = jnp.dot(s_ref[...], ss_ref[...], preferred_element_type=jnp.float32).astype(jnp.bfloat16)
    pieces = [u[:, j * breadth:(j + 1) * breadth] for j in range(u.shape[1] // breadth)]
    pieces += [w_ref[...], e_ref[...], north, south]
    r = r_ref[...]
    even = lax.broadcasted_iota(jnp.int32, (members, breadth), 1) % 2 == 0
    for b in range(res_blocks):
        acc = jnp.dot(pieces[b % len(pieces)], win_ref[b], preferred_element_type=jnp.float32)
        for k in range(links):
            blk = (b + k) % res_blocks
            acc = acc + jnp.dot(r[:, blk * breadth:(blk + 1) * breadth], c_ref[b, k],
                                preferred_element_type=jnp.float32)
        rb = jnp.tanh(acc).astype(jnp.bfloat16)
        r_out[:, b * breadth:(b + 1) * breadth] = rb
        wide = rb.astype(jnp.float32)
        feat_scr[:, b * breadth:(b + 1) * breadth] = jnp.where(even, wide * wide, wide).astype(jnp.bfloat16)
    f = jnp.dot(feat_scr[...], ro_ref[...], preferred_element_type=jnp.float32)
    f_out[...] = f
    ub = f.astype(jnp.bfloat16)
    u_out[...] = ub
    lo_out[...] = ub[:, :half]
    hi_out[...] = ub[:, half:]


def step_call(u, west, east, north_src, south_src, sel_n, sel_s, reservoir, block_weight, entry_weight, read_weight):
    members, feats = u.shape
    nodes = reservoir.shape[1]
    half = feats // LONC
    vmem = pltpu.MemorySpace.VMEM
    spec = pl.BlockSpec(memory_space=vmem)
    out_shape = (
        jax.ShapeDtypeStruct((members, feats), jnp.float32),
        jax.ShapeDtypeStruct((members, feats), jnp.bfloat16),
        jax.ShapeDtypeStruct((members, half), jnp.bfloat16),
        jax.ShapeDtypeStruct((members, half), jnp.bfloat16),
        jax.ShapeDtypeStruct((members, nodes), jnp.bfloat16),
    )
    return pl.pallas_call(
        step_kernel,
        out_shape=out_shape,
        in_specs=[spec] * 11,
        out_specs=tuple([spec] * 5),
        scratch_shapes=[pltpu.VMEM((members, nodes), jnp.bfloat16)],
        compiler_params=pltpu.CompilerParams(vmem_limit_bytes=32 * 1024 * 1024),
    )(u, west, east, north_src, south_src, sel_n, sel_s, reservoir, block_weight, entry_weight, read_weight)


def per_device(initial_state, initial_reservoir, coupling, input_weight, readout, intersection):
    current = initial_state[0, 0]
    reservoir = initial_reservoir[0, 0]
    block_weight = coupling[0, 0]
    entry_weight = input_weight[0, 0]
    read_weight = readout[0, 0]
    lists = intersection[0, 0]
    breadth = block_weight.shape[2]
    half = current.shape[1] // LONC
    sel_n = selector(lists[0], breadth)
    sel_s = selector(lists[1], breadth)
    rounded = current.astype(jnp.bfloat16)
    low = rounded[:, :half]
    high = rounded[:, half:]
    outputs = []
    for moment in range(STEPS):
        west = ring(high, "lon", 1)
        east = ring(low, "lon", -1)
        from_north = shifted(rounded, "lat", 1)
        from_south = shifted(rounded, "lat", -1)
        current, rounded, low, high, reservoir = step_call(
            rounded, west, east, from_north, from_south, sel_n, sel_s,
            reservoir, block_weight, entry_weight, read_weight)
        outputs.append(current)
    return jnp.stack(outputs)[:, None, None]


def solution(mesh):
    in_specs = (
        P("lat", "lon", None, None),
        P("lat", "lon", None, None),
        P("lat", "lon", None, None, None, None),
        P("lat", "lon", None, None, None),
        P("lat", "lon", None, None),
        P("lat", "lon", None, None),
    )
    out_specs = P(None, "lat", "lon", None, None)
    return jax.shard_map(
        per_device, mesh=mesh, in_specs=in_specs, out_specs=out_specs, check_vma=False
    )
```

time: 322 us -> 235 us (0.73)
  local copies, waits for them, and re-layouts: 60.3 us -> 7.16 us
  matrix products: 43.3 us -> 0 us
  Pallas kernels: 0 us -> 7.16 us
  waiting for transfers between devices: 110 us -> 117 us
    dot_general x40 -> x0, matrix products: 43.3 us -> none  [the longest x8 17.2 us: per_device(): current = jnp.dot(features, read_weight, preferred_element_type=jnp.float32)]
    gather x16 -> x0, local copies, waits for them, and re-layouts: 24.1 us -> none  [the longest x8 13.6 us: per_device(): blocks[:, linked]]
    unnamed x60 -> x19, local copies, waits for them, and re-layouts: 19.6 us -> 4.42 us
    reshape x29 -> x0, local copies, waits for them, and re-layouts: 8.73 us -> none  [the longest x8 7.42 us: per_device(): chosen = inputs.reshape(members, in_blocks, breadth)[:, block_index]]
    pallas_call x0 -> x7, Pallas kernels: none -> 7.16 us  [step_call(): pl.pallas_call(step_kernel, out_shape=out_shape, in_specs=[spec] * 11, ou...]
    ppermute x16, waiting for transfers between devices: 110 us -> 117 us  [ring(): lax.ppermute(value, axis, [(i, (i + by) % peers) for i in range(peers)])]
    concatenate x8 -> x0, local copies, waits for them, and re-layouts: 4.25 us -> none  [per_device(): jnp.concatenate([rounded, west_col, east_col, north_part, south_part], ax...]
  transfers between devices with their start and end apart: 32 -> 32, of which waited for: 8 -> 8; matrix products, arithmetic and copies ran while one was open for 10% -> 1% of each run, Pallas kernels for 0% -> 0%
where the time goes in v1:
time: 235 us; the launch traced here: 234 us
  waiting for transfers between devices  117 us (50%)
  starting transfers between devices  101 us (43%)
  local copies, waits for them, and re-layouts  7.16 us (3%)
  Pallas kernels  7.16 us (3%)
    ppermute x16, waiting for transfers between devices, ring(): lax.ppermute(value, axis, [(i, (i + by) % peers) for i in range(peers)])  117 us
    ppermute x16, starting transfers between devices, shifted(): return lax.ppermute(value, axis, pairs)  54.2 us
    ppermute x16, starting transfers between devices, ring(): lax.ppermute(value, axis, [(i, (i + by) % peers) for i in range(peers)])  46.7 us
    pallas_call x7, Pallas kernels, step_call(): pl.pallas_call(step_kernel, out_shape=out_shape, in_specs=[spec] * 11, ou...  7.16 us
  transfers between devices with their start and end apart: 32, of which 8 were waited for; matrix products, arithmetic and copies ran while one was open for 1% of the time, Pallas kernels for 0%

profile of v1, /device:TPU:414, one launch (start us, length us, event | category | flops | bytes accessed | tf_op | source)
XLA Modules:
  0.0 233.8 jit_solution(15855949411778497743)
XLA Ops:
  0.0 0.9 convert_bitcast_fusion.u_ref
  0.9 1.9 collective-permute-start.2
  2.9 4.9 %collective-permute-start.3 = (bf16[64,256]{1,0:T(8,128)(2,1)S(1)}, bf16[64,256]{1,0:T(8,128)(2,1)S(1)}, u32[]{:S(2)}, u32[]{:S(2)}) collective-permute-start(bf16[64,256]{1,0:T(8,128)(2,1)S(1)} %convert_bitcast_fusion.u_ref), channel_id=1, source_target_pairs={{32,0},{64,32},{96,64},{128,96},{160,128},{192,160},{224,192},{256... | collective-permute-start | bytes 98312 | tf_op jit(solution)/shard_map/ppermute | solution.py:20
  7.7 3.2 %collective-permute-start = (bf16[64,128]{1,0:T(8,128)(2,1)S(1)}, bf16[64,128]{1,0:T(8,128)(2,1)S(1)}, u32[]{:S(2)}, u32[]{:S(2)}) collective-permute-start(bf16[64,128]{1,0:T(8,128)(2,1)S(1)} %get-tuple-element.92), channel_id=1, source_target_pairs={{0,1},{1,2},{2,3},{3,4},{4,5},{5,6},{6,7},{7,8},{8,9},{9,10},{10,1... | collective-permute-start | bytes 49160 | tf_op jit(solution)/shard_map/ppermute | solution.py:25
  10.9 2.6 %collective-permute-start.1 = (bf16[64,128]{1,0:T(8,128)(2,1)S(1)}, bf16[64,128]{1,0:T(8,128)(2,1)S(1)}, u32[]{:S(2)}, u32[]{:S(2)}) collective-permute-start(bf16[64,128]{1,0:T(8,128)(2,1)S(1)} %get-tuple-element.91), channel_id=1, source_target_pairs={{0,31},{1,0},{2,1},{3,2},{4,3},{5,4},{6,5},{7,6},{8,7},{9,8},{10,9... | collective-permute-start | bytes 49160 | tf_op jit(solution)/shard_map/ppermute | solution.py:25
  13.6 0.8 slice_bitcast_fusion
  14.4 0.3 broadcast_multiply_fusion
  14.6 0.2 mul.37.sn_ref
  14.8 0.2 mul.40.ss_ref
  15.0 0.0 collective-permute-done.w_ref
  15.0 14.5 %collective-permute-done.1.e_ref = bf16[64,128]{1,0:T(8,128)(2,1)S(1)} collective-permute-done((bf16[64,128]{1,0:T(8,128)(2,1)S(1)}, bf16[64,128]{1,0:T(8,128)(2,1)S(1)}, u32[]{:S(2)}, u32[]{:S(2)}) %collective-permute-start.1) | collective-permute-done | bytes 16416 | tf_op jit(solution)/shard_map/ppermute | solution.py:25
  29.5 0.0 collective-permute-done.2.n_ref
  29.5 0.0 collective-permute-done.3.s_ref
  29.5 0.0 copy-start
  29.5 1.6 copy-done
  31.1 1.0 copy-done.3
  32.2 0.9 copy-done.4
  33.1 1.0 shard_map.64
  34.1 1.9 collective-permute-start.6
  36.1 4.9 %collective-permute-start.7 = (bf16[64,256]{1,0:T(8,128)(2,1)S(1)}, bf16[64,256]{1,0:T(8,128)(2,1)S(1)}, u32[]{:S(2)}, u32[]{:S(2)}) collective-permute-start(bf16[64,256]{1,0:T(8,128)(2,1)S(1)} %get-tuple-element.42.u_ref), channel_id=1, source_target_pairs={{32,0},{64,32},{96,64},{128,96},{160,128},{192,160},{224,192},{256... | collective-permute-start | bytes 98312 | tf_op jit(solution)/shard_map/ppermute | solution.py:20
  40.9 1.9 collective-permute-start.4
  42.9 3.9 %collective-permute-start.5 = (bf16[64,128]{1,0:T(8,128)(2,1)S(1)}, bf16[64,128]{1,0:T(8,128)(2,1)S(1)}, u32[]{:S(2)}, u32[]{:S(2)}) collective-permute-start(bf16[64,128]{1,0:T(8,128)(2,1)S(1)} %get-tuple-element.44), channel_id=1, source_target_pairs={{0,31},{1,0},{2,1},{3,2},{4,3},{5,4},{6,5},{7,6},{8,7},{9,8},{10,9... | collective-permute-start | bytes 49160 | tf_op jit(solution)/shard_map/ppermute | solution.py:25
  46.8 0.0 collective-permute-done.4.w_ref
  46.8 14.6 %collective-permute-done.5.e_ref = bf16[64,128]{1,0:T(8,128)(2,1)S(1)} collective-permute-done((bf16[64,128]{1,0:T(8,128)(2,1)S(1)}, bf16[64,128]{1,0:T(8,128)(2,1)S(1)}, u32[]{:S(2)}, u32[]{:S(2)}) %collective-permute-start.5) | collective-permute-done | bytes 16416 | tf_op jit(solution)/shard_map/ppermute | solution.py:25
  61.4 0.0 collective-permute-done.6.n_ref
  61.4 1.0 shard_map.65
  62.5 1.9 collective-permute-start.10
  64.4 4.9 %collective-permute-start.11 = (bf16[64,256]{1,0:T(8,128)(2,1)S(1)}, bf16[64,256]{1,0:T(8,128)(2,1)S(1)}, u32[]{:S(2)}, u32[]{:S(2)}) collective-permute-start(bf16[64,256]{1,0:T(8,128)(2,1)S(1)} %get-tuple-element.47.u_ref), channel_id=1, source_target_pairs={{32,0},{64,32},{96,64},{128,96},{160,128},{192,160},{224,192},{256... | collective-permute-start | bytes 98312 | tf_op jit(solution)/shard_map/ppermute | solution.py:20
  69.3 1.9 collective-permute-start.8
  71.2 3.9 %collective-permute-start.9 = (bf16[64,128]{1,0:T(8,128)(2,1)S(1)}, bf16[64,128]{1,0:T(8,128)(2,1)S(1)}, u32[]{:S(2)}, u32[]{:S(2)}) collective-permute-start(bf16[64,128]{1,0:T(8,128)(2,1)S(1)} %get-tuple-element.49), channel_id=1, source_target_pairs={{0,31},{1,0},{2,1},{3,2},{4,3},{5,4},{6,5},{7,6},{8,7},{9,8},{10,9... | collective-permute-start | bytes 49160 | tf_op jit(solution)/shard_map/ppermute | solution.py:25
  75.1 14.6 %collective-permute-done.9.e_ref = bf16[64,128]{1,0:T(8,128)(2,1)S(1)} collective-permute-done((bf16[64,128]{1,0:T(8,128)(2,1)S(1)}, bf16[64,128]{1,0:T(8,128)(2,1)S(1)}, u32[]{:S(2)}, u32[]{:S(2)}) %collective-permute-start.9) | collective-permute-done | bytes 16416 | tf_op jit(solution)/shard_map/ppermute | solution.py:25
  89.8 0.0 collective-permute-done.10.n_ref
  89.8 1.0 shard_map.66
  90.8 1.9 collective-permute-start.14
  92.7 4.9 %collective-permute-start.15 = (bf16[64,256]{1,0:T(8,128)(2,1)S(1)}, bf16[64,256]{1,0:T(8,128)(2,1)S(1)}, u32[]{:S(2)}, u32[]{:S(2)}) collective-permute-start(bf16[64,256]{1,0:T(8,128)(2,1)S(1)} %get-tuple-element.52.u_ref), channel_id=1, source_target_pairs={{32,0},{64,32},{96,64},{128,96},{160,128},{192,160},{224,192},{256... | collective-permute-start | bytes 98312 | tf_op jit(solution)/shard_map/ppermute | solution.py:20
  97.6 1.9 collective-permute-start.12
  99.5 3.9 %collective-permute-start.13 = (bf16[64,128]{1,0:T(8,128)(2,1)S(1)}, bf16[64,128]{1,0:T(8,128)(2,1)S(1)}, u32[]{:S(2)}, u32[]{:S(2)}) collective-permute-start(bf16[64,128]{1,0:T(8,128)(2,1)S(1)} %get-tuple-element.54), channel_id=1, source_target_pairs={{0,31},{1,0},{2,1},{3,2},{4,3},{5,4},{6,5},{7,6},{8,7},{9,8},{10,9... | collective-permute-start | bytes 49160 | tf_op jit(solution)/shard_map/ppermute | solution.py:25
  103.5 14.6 %collective-permute-done.13.e_ref = bf16[64,128]{1,0:T(8,128)(2,1)S(1)} collective-permute-done((bf16[64,128]{1,0:T(8,128)(2,1)S(1)}, bf16[64,128]{1,0:T(8,128)(2,1)S(1)}, u32[]{:S(2)}, u32[]{:S(2)}) %collective-permute-start.13) | collective-permute-done | bytes 16416 | tf_op jit(solution)/shard_map/ppermute | solution.py:25
  118.1 1.0 shard_map.67
  119.1 1.9 collective-permute-start.18
  121.0 4.9 %collective-permute-start.19 = (bf16[64,256]{1,0:T(8,128)(2,1)S(1)}, bf16[64,256]{1,0:T(8,128)(2,1)S(1)}, u32[]{:S(2)}, u32[]{:S(2)}) collective-permute-start(bf16[64,256]{1,0:T(8,128)(2,1)S(1)} %get-tuple-element.57.u_ref), channel_id=1, source_target_pairs={{32,0},{64,32},{96,64},{128,96},{160,128},{192,160},{224,192},{256... | collective-permute-start | bytes 98312 | tf_op jit(solution)/shard_map/ppermute | solution.py:20
  125.9 1.9 collective-permute-start.16
  127.8 3.9 %collective-permute-start.17 = (bf16[64,128]{1,0:T(8,128)(2,1)S(1)}, bf16[64,128]{1,0:T(8,128)(2,1)S(1)}, u32[]{:S(2)}, u32[]{:S(2)}) collective-permute-start(bf16[64,128]{1,0:T(8,128)(2,1)S(1)} %get-tuple-element.59), channel_id=1, source_target_pairs={{0,31},{1,0},{2,1},{3,2},{4,3},{5,4},{6,5},{7,6},{8,7},{9,8},{10,9... | collective-permute-start | bytes 49160 | tf_op jit(solution)/shard_map/ppermute | solution.py:25
  131.8 14.6 %collective-permute-done.17.e_ref = bf16[64,128]{1,0:T(8,128)(2,1)S(1)} collective-permute-done((bf16[64,128]{1,0:T(8,128)(2,1)S(1)}, bf16[64,128]{1,0:T(8,128)(2,1)S(1)}, u32[]{:S(2)}, u32[]{:S(2)}) %collective-permute-start.17) | collective-permute-done | bytes 16416 | tf_op jit(solution)/shard_map/ppermute | solution.py:25
  146.4 1.0 shard_map.68
  147.4 1.9 collective-permute-start.22
  149.4 4.9 %collective-permute-start.23 = (bf16[64,256]{1,0:T(8,128)(2,1)S(1)}, bf16[64,256]{1,0:T(8,128)(2,1)S(1)}, u32[]{:S(2)}, u32[]{:S(2)}) collective-permute-start(bf16[64,256]{1,0:T(8,128)(2,1)S(1)} %get-tuple-element.62.u_ref), channel_id=1, source_target_pairs={{32,0},{64,32},{96,64},{128,96},{160,128},{192,160},{224,192},{256... | collective-permute-start | bytes 98312 | tf_op jit(solution)/shard_map/ppermute | solution.py:20
  154.2 1.9 collective-permute-start.20
  156.2 3.9 %collective-permute-start.21 = (bf16[64,128]{1,0:T(8,128)(2,1)S(1)}, bf16[64,128]{1,0:T(8,128)(2,1)S(1)}, u32[]{:S(2)}, u32[]{:S(2)}) collective-permute-start(bf16[64,128]{1,0:T(8,128)(2,1)S(1)} %get-tuple-element.64), channel_id=1, source_target_pairs={{0,31},{1,0},{2,1},{3,2},{4,3},{5,4},{6,5},{7,6},{8,7},{9,8},{10,9... | collective-permute-start | bytes 49160 | tf_op jit(solution)/shard_map/ppermute | solution.py:25
  160.1 14.6 %collective-permute-done.21.e_ref = bf16[64,128]{1,0:T(8,128)(2,1)S(1)} collective-permute-done((bf16[64,128]{1,0:T(8,128)(2,1)S(1)}, bf16[64,128]{1,0:T(8,128)(2,1)S(1)}, u32[]{:S(2)}, u32[]{:S(2)}) %collective-permute-start.21) | collective-permute-done | bytes 16416 | tf_op jit(solution)/shard_map/ppermute | solution.py:25
  174.7 1.0 shard_map.69
  175.8 1.9 collective-permute-start.26
  177.7 4.9 %collective-permute-start.27 = (bf16[64,256]{1,0:T(8,128)(2,1)S(1)}, bf16[64,256]{1,0:T(8,128)(2,1)S(1)}, u32[]{:S(2)}, u32[]{:S(2)}) collective-permute-start(bf16[64,256]{1,0:T(8,128)(2,1)S(1)} %get-tuple-element.67.u_ref), channel_id=1, source_target_pairs={{32,0},{64,32},{96,64},{128,96},{160,128},{192,160},{224,192},{256... | collective-permute-start | bytes 98312 | tf_op jit(solution)/shard_map/ppermute | solution.py:20
  182.5 1.9 collective-permute-start.24
  184.5 3.9 %collective-permute-start.25 = (bf16[64,128]{1,0:T(8,128)(2,1)S(1)}, bf16[64,128]{1,0:T(8,128)(2,1)S(1)}, u32[]{:S(2)}, u32[]{:S(2)}) collective-permute-start(bf16[64,128]{1,0:T(8,128)(2,1)S(1)} %get-tuple-element.69), channel_id=1, source_target_pairs={{0,31},{1,0},{2,1},{3,2},{4,3},{5,4},{6,5},{7,6},{8,7},{9,8},{10,9... | collective-permute-start | bytes 49160 | tf_op jit(solution)/shard_map/ppermute | solution.py:25
  188.4 14.6 %collective-permute-done.25.e_ref = bf16[64,128]{1,0:T(8,128)(2,1)S(1)} collective-permute-done((bf16[64,128]{1,0:T(8,128)(2,1)S(1)}, bf16[64,128]{1,0:T(8,128)(2,1)S(1)}, u32[]{:S(2)}, u32[]{:S(2)}) %collective-permute-start.25) | collective-permute-done | bytes 16416 | tf_op jit(solution)/shard_map/ppermute | solution.py:25
  203.0 1.0 shard_map.70
  204.1 1.9 collective-permute-start.30
  206.0 4.9 %collective-permute-start.31 = (bf16[64,256]{1,0:T(8,128)(2,1)S(1)}, bf16[64,256]{1,0:T(8,128)(2,1)S(1)}, u32[]{:S(2)}, u32[]{:S(2)}) collective-permute-start(bf16[64,256]{1,0:T(8,128)(2,1)S(1)} %get-tuple-element.72), channel_id=1, source_target_pairs={{32,0},{64,32},{96,64},{128,96},{160,128},{192,160},{224,192},{256... | collective-permute-start | bytes 98312 | tf_op jit(solution)/shard_map/ppermute | solution.py:20
  210.9 1.9 collective-permute-start.28
  212.8 3.9 %collective-permute-start.29 = (bf16[64,128]{1,0:T(8,128)(2,1)S(1)}, bf16[64,128]{1,0:T(8,128)(2,1)S(1)}, u32[]{:S(2)}, u32[]{:S(2)}) collective-permute-start(bf16[64,128]{1,0:T(8,128)(2,1)S(1)} %get-tuple-element.74), channel_id=1, source_target_pairs={{0,31},{1,0},{2,1},{3,2},{4,3},{5,4},{6,5},{7,6},{8,7},{9,8},{10,9... | collective-permute-start | bytes 49160 | tf_op jit(solution)/shard_map/ppermute | solution.py:25
  216.7 14.6 %collective-permute-done.29 = bf16[64,128]{1,0:T(8,128)(2,1)S(1)} collective-permute-done((bf16[64,128]{1,0:T(8,128)(2,1)S(1)}, bf16[64,128]{1,0:T(8,128)(2,1)S(1)}, u32[]{:S(2)}, u32[]{:S(2)}) %collective-permute-start.29) | collective-permute-done | bytes 16416 | tf_op jit(solution)/shard_map/ppermute | solution.py:25
  231.4 1.6 shard_map.71
  233.0 0.8 copy-done.5
  (35 shorter events, 0.1 us)
Async XLA Ops:
  0.0 29.5 %copy-start.2 = (bf16[1,1,2048,256]{3,2,1,0:T(8,128)(2,1)S(1)}, bf16[1,1,2048,256]{3,2,1,0:T(8,128)(2,1)}, u32[]{:S(2)}) copy-start(bf16[1,1,2048,256]{3,2,1,0:T(8,128)(2,1)} %param.10) | copy-start | bytes 3145732
  0.9 28.6 %collective-permute-start.2 = (bf16[64,256]{1,0:T(8,128)(2,1)S(1)}, bf16[64,256]{1,0:T(8,128)(2,1)S(1)}, u32[]{:S(2)}, u32[]{:S(2)}) collective-permute-start(bf16[64,256]{1,0:T(8,128)(2,1)S(1)} %convert_bitcast_fusion.u_ref), channel_id=1, source_target_pairs={{0,32},{32,64},{64,96},{96,128},{128,160},{160,192},{192,224},{224... | collective-permute-start | bytes 98312 | tf_op jit(solution)/shard_map/ppermute | solution.py:20
  2.9 26.7 %collective-permute-start.3 = (bf16[64,256]{1,0:T(8,128)(2,1)S(1)}, bf16[64,256]{1,0:T(8,128)(2,1)S(1)}, u32[]{:S(2)}, u32[]{:S(2)}) collective-permute-start(bf16[64,256]{1,0:T(8,128)(2,1)S(1)} %convert_bitcast_fusion.u_ref), channel_id=1, source_target_pairs={{32,0},{64,32},{96,64},{128,96},{160,128},{192,160},{224,192},{256... | collective-permute-start | bytes 98312 | tf_op jit(solution)/shard_map/ppermute | solution.py:20
  7.7 7.3 %collective-permute-start = (bf16[64,128]{1,0:T(8,128)(2,1)S(1)}, bf16[64,128]{1,0:T(8,128)(2,1)S(1)}, u32[]{:S(2)}, u32[]{:S(2)}) collective-permute-start(bf16[64,128]{1,0:T(8,128)(2,1)S(1)} %get-tuple-element.92), channel_id=1, source_target_pairs={{0,1},{1,2},{2,3},{3,4},{4,5},{5,6},{6,7},{7,8},{8,9},{9,10},{10,1... | collective-permute-start | bytes 49160 | tf_op jit(solution)/shard_map/ppermute | solution.py:25
  10.9 18.6 %collective-permute-start.1 = (bf16[64,128]{1,0:T(8,128)(2,1)S(1)}, bf16[64,128]{1,0:T(8,128)(2,1)S(1)}, u32[]{:S(2)}, u32[]{:S(2)}) collective-permute-start(bf16[64,128]{1,0:T(8,128)(2,1)S(1)} %get-tuple-element.91), channel_id=1, source_target_pairs={{0,31},{1,0},{2,1},{3,2},{4,3},{5,4},{6,5},{7,6},{8,7},{9,8},{10,9... | collective-permute-start | bytes 49160 | tf_op jit(solution)/shard_map/ppermute | solution.py:25
  29.5 1.6 copy-start
  31.1 1.0 copy-start.3
  32.2 0.9 copy-start.4
  33.1 28.3 %copy-start.1 = (bf16[1,1,16,4,128,128]{5,4,3,2,1,0:T(8,128)(2,1)S(1)}, bf16[1,1,16,4,128,128]{5,4,3,2,1,0:T(8,128)(2,1)}, u32[]{:S(2)}) copy-start(bf16[1,1,16,4,128,128]{5,4,3,2,1,0:T(8,128)(2,1)} %param.8) | copy-start | bytes 6291460
  34.1 27.3 %collective-permute-start.6 = (bf16[64,256]{1,0:T(8,128)(2,1)S(1)}, bf16[64,256]{1,0:T(8,128)(2,1)S(1)}, u32[]{:S(2)}, u32[]{:S(2)}) collective-permute-start(bf16[64,256]{1,0:T(8,128)(2,1)S(1)} %get-tuple-element.42.u_ref), channel_id=1, source_target_pairs={{0,32},{32,64},{64,96},{96,128},{128,160},{160,192},{192,224},{224... | collective-permute-start | bytes 98312 | tf_op jit(solution)/shard_map/ppermute | solution.py:20
  36.1 25.4 %collective-permute-start.7 = (bf16[64,256]{1,0:T(8,128)(2,1)S(1)}, bf16[64,256]{1,0:T(8,128)(2,1)S(1)}, u32[]{:S(2)}, u32[]{:S(2)}) collective-permute-start(bf16[64,256]{1,0:T(8,128)(2,1)S(1)} %get-tuple-element.42.u_ref), channel_id=1, source_target_pairs={{32,0},{64,32},{96,64},{128,96},{160,128},{192,160},{224,192},{256... | collective-permute-start | bytes 98312 | tf_op jit(solution)/shard_map/ppermute | solution.py:20
  40.9 5.9 %collective-permute-start.4 = (bf16[64,128]{1,0:T(8,128)(2,1)S(1)}, bf16[64,128]{1,0:T(8,128)(2,1)S(1)}, u32[]{:S(2)}, u32[]{:S(2)}) collective-permute-start(bf16[64,128]{1,0:T(8,128)(2,1)S(1)} %get-tuple-element.43), channel_id=1, source_target_pairs={{0,1},{1,2},{2,3},{3,4},{4,5},{5,6},{6,7},{7,8},{8,9},{9,10},{10,1... | collective-permute-start | bytes 49160 | tf_op jit(solution)/shard_map/ppermute | solution.py:25
  42.9 18.6 %collective-permute-start.5 = (bf16[64,128]{1,0:T(8,128)(2,1)S(1)}, bf16[64,128]{1,0:T(8,128)(2,1)S(1)}, u32[]{:S(2)}, u32[]{:S(2)}) collective-permute-start(bf16[64,128]{1,0:T(8,128)(2,1)S(1)} %get-tuple-element.44), channel_id=1, source_target_pairs={{0,31},{1,0},{2,1},{3,2},{4,3},{5,4},{6,5},{7,6},{8,7},{9,8},{10,9... | collective-permute-start | bytes 49160 | tf_op jit(solution)/shard_map/ppermute | solution.py:25
  62.5 27.3 %collective-permute-start.10 = (bf16[64,256]{1,0:T(8,128)(2,1)S(1)}, bf16[64,256]{1,0:T(8,128)(2,1)S(1)}, u32[]{:S(2)}, u32[]{:S(2)}) collective-permute-start(bf16[64,256]{1,0:T(8,128)(2,1)S(1)} %get-tuple-element.47.u_ref), channel_id=1, source_target_pairs={{0,32},{32,64},{64,96},{96,128},{128,160},{160,192},{192,224},{224... | collective-permute-start | bytes 98312 | tf_op jit(solution)/shard_map/ppermute | solution.py:20
  64.4 25.4 %collective-permute-start.11 = (bf16[64,256]{1,0:T(8,128)(2,1)S(1)}, bf16[64,256]{1,0:T(8,128)(2,1)S(1)}, u32[]{:S(2)}, u32[]{:S(2)}) collective-permute-start(bf16[64,256]{1,0:T(8,128)(2,1)S(1)} %get-tuple-element.47.u_ref), channel_id=1, source_target_pairs={{32,0},{64,32},{96,64},{128,96},{160,128},{192,160},{224,192},{256... | collective-permute-start | bytes 98312 | tf_op jit(solution)/shard_map/ppermute | solution.py:20
  69.3 5.9 %collective-permute-start.8 = (bf16[64,128]{1,0:T(8,128)(2,1)S(1)}, bf16[64,128]{1,0:T(8,128)(2,1)S(1)}, u32[]{:S(2)}, u32[]{:S(2)}) collective-permute-start(bf16[64,128]{1,0:T(8,128)(2,1)S(1)} %get-tuple-element.48), channel_id=1, source_target_pairs={{0,1},{1,2},{2,3},{3,4},{4,5},{5,6},{6,7},{7,8},{8,9},{9,10},{10,1... | collective-permute-start | bytes 49160 | tf_op jit(solution)/shard_map/ppermute | solution.py:25
  71.2 18.6 %collective-permute-start.9 = (bf16[64,128]{1,0:T(8,128)(2,1)S(1)}, bf16[64,128]{1,0:T(8,128)(2,1)S(1)}, u32[]{:S(2)}, u32[]{:S(2)}) collective-permute-start(bf16[64,128]{1,0:T(8,128)(2,1)S(1)} %get-tuple-element.49), channel_id=1, source_target_pairs={{0,31},{1,0},{2,1},{3,2},{4,3},{5,4},{6,5},{7,6},{8,7},{9,8},{10,9... | collective-permute-start | bytes 49160 | tf_op jit(solution)/shard_map/ppermute | solution.py:25
  90.8 27.3 %collective-permute-start.14 = (bf16[64,256]{1,0:T(8,128)(2,1)S(1)}, bf16[64,256]{1,0:T(8,128)(2,1)S(1)}, u32[]{:S(2)}, u32[]{:S(2)}) collective-permute-start(bf16[64,256]{1,0:T(8,128)(2,1)S(1)} %get-tuple-element.52.u_ref), channel_id=1, source_target_pairs={{0,32},{32,64},{64,96},{96,128},{128,160},{160,192},{192,224},{224... | collective-permute-start | bytes 98312 | tf_op jit(solution)/shard_map/ppermute | solution.py:20
  92.7 25.4 %collective-permute-start.15 = (bf16[64,256]{1,0:T(8,128)(2,1)S(1)}, bf16[64,256]{1,0:T(8,128)(2,1)S(1)}, u32[]{:S(2)}, u32[]{:S(2)}) collective-permute-start(bf16[64,256]{1,0:T(8,128)(2,1)S(1)} %get-tuple-element.52.u_ref), channel_id=1, source_target_pairs={{32,0},{64,32},{96,64},{128,96},{160,128},{192,160},{224,192},{256... | collective-permute-start | bytes 98312 | tf_op jit(solution)/shard_map/ppermute | solution.py:20
  97.6 5.9 %collective-permute-start.12 = (bf16[64,128]{1,0:T(8,128)(2,1)S(1)}, bf16[64,128]{1,0:T(8,128)(2,1)S(1)}, u32[]{:S(2)}, u32[]{:S(2)}) collective-permute-start(bf16[64,128]{1,0:T(8,128)(2,1)S(1)} %get-tuple-element.53), channel_id=1, source_target_pairs={{0,1},{1,2},{2,3},{3,4},{4,5},{5,6},{6,7},{7,8},{8,9},{9,10},{10,1... | collective-permute-start | bytes 49160 | tf_op jit(solution)/shard_map/ppermute | solution.py:25
  99.5 18.6 %collective-permute-start.13 = (bf16[64,128]{1,0:T(8,128)(2,1)S(1)}, bf16[64,128]{1,0:T(8,128)(2,1)S(1)}, u32[]{:S(2)}, u32[]{:S(2)}) collective-permute-start(bf16[64,128]{1,0:T(8,128)(2,1)S(1)} %get-tuple-element.54), channel_id=1, source_target_pairs={{0,31},{1,0},{2,1},{3,2},{4,3},{5,4},{6,5},{7,6},{8,7},{9,8},{10,9... | collective-permute-start | bytes 49160 | tf_op jit(solution)/shard_map/ppermute | solution.py:25
  119.1 27.3 %collective-permute-start.18 = (bf16[64,256]{1,0:T(8,128)(2,1)S(1)}, bf16[64,256]{1,0:T(8,128)(2,1)S(1)}, u32[]{:S(2)}, u32[]{:S(2)}) collective-permute-start(bf16[64,256]{1,0:T(8,128)(2,1)S(1)} %get-tuple-element.57.u_ref), channel_id=1, source_target_pairs={{0,32},{32,64},{64,96},{96,128},{128,160},{160,192},{192,224},{224... | collective-permute-start | bytes 98312 | tf_op jit(solution)/shard_map/ppermute | solution.py:20
  121.0 25.4 %collective-permute-start.19 = (bf16[64,256]{1,0:T(8,128)(2,1)S(1)}, bf16[64,256]{1,0:T(8,128)(2,1)S(1)}, u32[]{:S(2)}, u32[]{:S(2)}) collective-permute-start(bf16[64,256]{1,0:T(8,128)(2,1)S(1)} %get-tuple-element.57.u_ref), channel_id=1, source_target_pairs={{32,0},{64,32},{96,64},{128,96},{160,128},{192,160},{224,192},{256... | collective-permute-start | bytes 98312 | tf_op jit(solution)/shard_map/ppermute | solution.py:20
  125.9 5.9 %collective-permute-start.16 = (bf16[64,128]{1,0:T(8,128)(2,1)S(1)}, bf16[64,128]{1,0:T(8,128)(2,1)S(1)}, u32[]{:S(2)}, u32[]{:S(2)}) collective-permute-start(bf16[64,128]{1,0:T(8,128)(2,1)S(1)} %get-tuple-element.58), channel_id=1, source_target_pairs={{0,1},{1,2},{2,3},{3,4},{4,5},{5,6},{6,7},{7,8},{8,9},{9,10},{10,1... | collective-permute-start | bytes 49160 | tf_op jit(solution)/shard_map/ppermute | solution.py:25
  127.8 18.6 %collective-permute-start.17 = (bf16[64,128]{1,0:T(8,128)(2,1)S(1)}, bf16[64,128]{1,0:T(8,128)(2,1)S(1)}, u32[]{:S(2)}, u32[]{:S(2)}) collective-permute-start(bf16[64,128]{1,0:T(8,128)(2,1)S(1)} %get-tuple-element.59), channel_id=1, source_target_pairs={{0,31},{1,0},{2,1},{3,2},{4,3},{5,4},{6,5},{7,6},{8,7},{9,8},{10,9... | collective-permute-start | bytes 49160 | tf_op jit(solution)/shard_map/ppermute | solution.py:25
  147.4 27.3 %collective-permute-start.22 = (bf16[64,256]{1,0:T(8,128)(2,1)S(1)}, bf16[64,256]{1,0:T(8,128)(2,1)S(1)}, u32[]{:S(2)}, u32[]{:S(2)}) collective-permute-start(bf16[64,256]{1,0:T(8,128)(2,1)S(1)} %get-tuple-element.62.u_ref), channel_id=1, source_target_pairs={{0,32},{32,64},{64,96},{96,128},{128,160},{160,192},{192,224},{224... | collective-permute-start | bytes 98312 | tf_op jit(solution)/shard_map/ppermute | solution.py:20
  149.4 25.4 %collective-permute-start.23 = (bf16[64,256]{1,0:T(8,128)(2,1)S(1)}, bf16[64,256]{1,0:T(8,128)(2,1)S(1)}, u32[]{:S(2)}, u32[]{:S(2)}) collective-permute-start(bf16[64,256]{1,0:T(8,128)(2,1)S(1)} %get-tuple-element.62.u_ref), channel_id=1, source_target_pairs={{32,0},{64,32},{96,64},{128,96},{160,128},{192,160},{224,192},{256... | collective-permute-start | bytes 98312 | tf_op jit(solution)/shard_map/ppermute | solution.py:20
  154.2 5.9 %collective-permute-start.20 = (bf16[64,128]{1,0:T(8,128)(2,1)S(1)}, bf16[64,128]{1,0:T(8,128)(2,1)S(1)}, u32[]{:S(2)}, u32[]{:S(2)}) collective-permute-start(bf16[64,128]{1,0:T(8,128)(2,1)S(1)} %get-tuple-element.63), channel_id=1, source_target_pairs={{0,1},{1,2},{2,3},{3,4},{4,5},{5,6},{6,7},{7,8},{8,9},{9,10},{10,1... | collective-permute-start | bytes 49160 | tf_op jit(solution)/shard_map/ppermute | solution.py:25
  156.2 18.6 %collective-permute-start.21 = (bf16[64,128]{1,0:T(8,128)(2,1)S(1)}, bf16[64,128]{1,0:T(8,128)(2,1)S(1)}, u32[]{:S(2)}, u32[]{:S(2)}) collective-permute-start(bf16[64,128]{1,0:T(8,128)(2,1)S(1)} %get-tuple-element.64), channel_id=1, source_target_pairs={{0,31},{1,0},{2,1},{3,2},{4,3},{5,4},{6,5},{7,6},{8,7},{9,8},{10,9... | collective-permute-start | bytes 49160 | tf_op jit(solution)/shard_map/ppermute | solution.py:25
  175.8 27.3 %collective-permute-start.26 = (bf16[64,256]{1,0:T(8,128)(2,1)S(1)}, bf16[64,256]{1,0:T(8,128)(2,1)S(1)}, u32[]{:S(2)}, u32[]{:S(2)}) collective-permute-start(bf16[64,256]{1,0:T(8,128)(2,1)S(1)} %get-tuple-element.67.u_ref), channel_id=1, source_target_pairs={{0,32},{32,64},{64,96},{96,128},{128,160},{160,192},{192,224},{224... | collective-permute-start | bytes 98312 | tf_op jit(solution)/shard_map/ppermute | solution.py:20
  177.7 25.4 %collective-permute-start.27 = (bf16[64,256]{1,0:T(8,128)(2,1)S(1)}, bf16[64,256]{1,0:T(8,128)(2,1)S(1)}, u32[]{:S(2)}, u32[]{:S(2)}) collective-permute-start(bf16[64,256]{1,0:T(8,128)(2,1)S(1)} %get-tuple-element.67.u_ref), channel_id=1, source_target_pairs={{32,0},{64,32},{96,64},{128,96},{160,128},{192,160},{224,192},{256... | collective-permute-start | bytes 98312 | tf_op jit(solution)/shard_map/ppermute | solution.py:20
  182.5 5.9 %collective-permute-start.24 = (bf16[64,128]{1,0:T(8,128)(2,1)S(1)}, bf16[64,128]{1,0:T(8,128)(2,1)S(1)}, u32[]{:S(2)}, u32[]{:S(2)}) collective-permute-start(bf16[64,128]{1,0:T(8,128)(2,1)S(1)} %get-tuple-element.68), channel_id=1, source_target_pairs={{0,1},{1,2},{2,3},{3,4},{4,5},{5,6},{6,7},{7,8},{8,9},{9,10},{10,1... | collective-permute-start | bytes 49160 | tf_op jit(solution)/shard_map/ppermute | solution.py:25
  184.5 18.6 %collective-permute-start.25 = (bf16[64,128]{1,0:T(8,128)(2,1)S(1)}, bf16[64,128]{1,0:T(8,128)(2,1)S(1)}, u32[]{:S(2)}, u32[]{:S(2)}) collective-permute-start(bf16[64,128]{1,0:T(8,128)(2,1)S(1)} %get-tuple-element.69), channel_id=1, source_target_pairs={{0,31},{1,0},{2,1},{3,2},{4,3},{5,4},{6,5},{7,6},{8,7},{9,8},{10,9... | collective-permute-start | bytes 49160 | tf_op jit(solution)/shard_map/ppermute | solution.py:25
  204.1 27.3 %collective-permute-start.30 = (bf16[64,256]{1,0:T(8,128)(2,1)S(1)}, bf16[64,256]{1,0:T(8,128)(2,1)S(1)}, u32[]{:S(2)}, u32[]{:S(2)}) collective-permute-start(bf16[64,256]{1,0:T(8,128)(2,1)S(1)} %get-tuple-element.72), channel_id=1, source_target_pairs={{0,32},{32,64},{64,96},{96,128},{128,160},{160,192},{192,224},{224... | collective-permute-start | bytes 98312 | tf_op jit(solution)/shard_map/ppermute | solution.py:20
  206.0 25.4 %collective-permute-start.31 = (bf16[64,256]{1,0:T(8,128)(2,1)S(1)}, bf16[64,256]{1,0:T(8,128)(2,1)S(1)}, u32[]{:S(2)}, u32[]{:S(2)}) collective-permute-start(bf16[64,256]{1,0:T(8,128)(2,1)S(1)} %get-tuple-element.72), channel_id=1, source_target_pairs={{32,0},{64,32},{96,64},{128,96},{160,128},{192,160},{224,192},{256... | collective-permute-start | bytes 98312 | tf_op jit(solution)/shard_map/ppermute | solution.py:20
  210.9 5.9 %collective-permute-start.28 = (bf16[64,128]{1,0:T(8,128)(2,1)S(1)}, bf16[64,128]{1,0:T(8,128)(2,1)S(1)}, u32[]{:S(2)}, u32[]{:S(2)}) collective-permute-start(bf16[64,128]{1,0:T(8,128)(2,1)S(1)} %get-tuple-element.73), channel_id=1, source_target_pairs={{0,1},{1,2},{2,3},{3,4},{4,5},{5,6},{6,7},{7,8},{8,9},{9,10},{10,1... | collective-permute-start | bytes 49160 | tf_op jit(solution)/shard_map/ppermute | solution.py:25
  212.8 18.6 %collective-permute-start.29 = (bf16[64,128]{1,0:T(8,128)(2,1)S(1)}, bf16[64,128]{1,0:T(8,128)(2,1)S(1)}, u32[]{:S(2)}, u32[]{:S(2)}) collective-permute-start(bf16[64,128]{1,0:T(8,128)(2,1)S(1)} %get-tuple-element.74), channel_id=1, source_target_pairs={{0,31},{1,0},{2,1},{3,2},{4,3},{5,4},{6,5},{7,6},{8,7},{9,8},{10,9... | collective-permute-start | bytes 49160 | tf_op jit(solution)/shard_map/ppermute | solution.py:25
  233.0 0.8 copy-start.5

commit v2 on v1

--- a/solution.py
+++ b/solution.py
@@ -14,17 +14,6 @@
 PTS = 8
 
 
-def shifted(value, axis, by):
-    peers = lax.axis_size(axis)
-    pairs = [(i, i + by) for i in range(peers) if 0 <= i + by < peers]
-    return lax.ppermute(value, axis, pairs)
-
-
-def ring(value, axis, by):
-    peers = lax.axis_size(axis)
-    return lax.ppermute(value, axis, [(i, (i + by) % peers) for i in range(peers)])
-
-
 def selector(slot_list, breadth):
     onehot = (slot_list[:, None] == jnp.arange(PTS, dtype=jnp.int32)[None, :]).astype(jnp.bfloat16)
     eye = jnp.eye(VARS, dtype=jnp.bfloat16)
@@ -32,15 +21,21 @@
     return full.reshape(PTS * VARS, OV * VARS)
 
 
-def step_kernel(u_ref, w_ref, e_ref, n_ref, s_ref, sn_ref, ss_ref, r_ref, c_ref, win_ref, ro_ref,
-                f_out, u_out, lo_out, hi_out, r_out, feat_scr):
-    members, half = lo_out.shape
+def step_kernel(flag_ref, u_ref, la_ref, lb_ref, ta_ref, tb_ref, sn_ref, ss_ref, r_ref, c_ref, win_ref, ro_ref,
+                f_out, u_out, sa_out, sb_out, r_out, feat_scr):
+    members, half = sa_out.shape
     res_blocks, links, breadth, _ = c_ref.shape
+    lon_even = jnp.broadcast_to(flag_ref[0], (members, half)) == 1
+    lat_even = jnp.broadcast_to(flag_ref[1], ta_ref.shape) == 1
+    west = jnp.where(lon_even, lb_ref[...], la_ref[...])
+    east = jnp.where(lon_even, la_ref[...], lb_ref[...])
+    north_src = jnp.where(lat_even, tb_ref[...], ta_ref[...])
+    south_src = jnp.where(lat_even, ta_ref[...], tb_ref[...])
     u = u_ref[...]
-    north = jnp.dot(n_ref[...], sn_ref[...], preferred_element_type=jnp.float32).astype(jnp.bfloat16)
-    south = jnp.dot(s_ref[...], ss_ref[...], preferred_element_type=jnp.float32).astype(jnp.bfloat16)
+    north = jnp.dot(north_src, sn_ref[...], preferred_element_type=jnp.float32).astype(jnp.bfloat16)
+    south = jnp.dot(south_src, ss_ref[...], preferred_element_type=jnp.float32).astype(jnp.bfloat16)
     pieces = [u[:, j * breadth:(j + 1) * breadth] for j in range(u.shape[1] // breadth)]
-    pieces += [w_ref[...], e_ref[...], north, south]
+    pieces += [west, east, north, south]
     r = r_ref[...]
     even = lax.broadcasted_iota(jnp.int32, (members, breadth), 1) % 2 == 0
     for b in range(res_blocks):
@@ -57,16 +52,17 @@
     f_out[...] = f
     ub = f.astype(jnp.bfloat16)
     u_out[...] = ub
-    lo_out[...] = ub[:, :half]
-    hi_out[...] = ub[:, half:]
+    lo = ub[:, :half]
+    hi = ub[:, half:]
+    sa_out[...] = jnp.where(lon_even, hi, lo)
+    sb_out[...] = jnp.where(lon_even, lo, hi)
 
 
-def step_call(u, west, east, north_src, south_src, sel_n, sel_s, reservoir, block_weight, entry_weight, read_weight):
+def step_call(flags, u, lon_a, lon_b, lat_a, lat_b, sel_n, sel_s, reservoir, block_weight, entry_weight, read_weight):
     members, feats = u.shape
     nodes = reservoir.shape[1]
     half = feats // LONC
-    vmem = pltpu.MemorySpace.VMEM
-    spec = pl.BlockSpec(memory_space=vmem)
+    spec = pl.BlockSpec(memory_space=pltpu.MemorySpace.VMEM)
     out_shape = (
         jax.ShapeDtypeStruct((members, feats), jnp.float32),
         jax.ShapeDtypeStruct((members, feats), jnp.bfloat16),
@@ -77,11 +73,22 @@
     return pl.pallas_call(
         step_kernel,
         out_shape=out_shape,
-        in_specs=[spec] * 11,
+        in_specs=[pl.BlockSpec(memory_space=pltpu.MemorySpace.SMEM)] + [spec] * 11,
         out_specs=tuple([spec] * 5),
         scratch_shapes=[pltpu.VMEM((members, nodes), jnp.bfloat16)],
         compiler_params=pltpu.CompilerParams(vmem_limit_bytes=32 * 1024 * 1024),
-    )(u, west, east, north_src, south_src, sel_n, sel_s, reservoir, block_weight, entry_weight, read_weight)
+    )(flags, u, lon_a, lon_b, lat_a, lat_b, sel_n, sel_s, reservoir, block_weight, entry_weight, read_weight)
+
+
+def swaps(peers, odd_first, wrap):
+    pairs = []
+    for i in range(peers):
+        partner = i + 1 if (i % 2 == 1) == odd_first else i - 1
+        if wrap:
+            partner %= peers
+        if 0 <= partner < peers:
+            pairs.append((i, partner))
+    return pairs
 
 
 def per_device(initial_state, initial_reservoir, coupling, input_weight, readout, intersection):
@@ -95,17 +102,28 @@
     half = current.shape[1] // LONC
     sel_n = selector(lists[0], breadth)
     sel_s = selector(lists[1], breadth)
+    lon_even = (lax.axis_index("lon") % 2 == 0).astype(jnp.int32)
+    lat_even = (lax.axis_index("lat") % 2 == 0).astype(jnp.int32)
+    flags = jnp.stack([lon_even, lat_even])
+    lon_peers = lax.axis_size("lon")
+    lat_peers = lax.axis_size("lat")
+    lon_pairs_a = swaps(lon_peers, False, True)
+    lon_pairs_b = swaps(lon_peers, True, True)
+    lat_pairs_a = swaps(lat_peers, False, False)
+    lat_pairs_b = swaps(lat_peers, True, False)
     rounded = current.astype(jnp.bfloat16)
     low = rounded[:, :half]
     high = rounded[:, half:]
+    send_a = jnp.where(lon_even == 1, high, low)
+    send_b = jnp.where(lon_even == 1, low, high)
     outputs = []
     for moment in range(STEPS):
-        west = ring(high, "lon", 1)
-        east = ring(low, "lon", -1)
-        from_north = shifted(rounded, "lat", 1)
-        from_south = shifted(rounded, "lat", -1)
-        current, rounded, low, high, reservoir = step_call(
-            rounded, west, east, from_north, from_south, sel_n, sel_s,
+        lon_b = lax.ppermute(send_b, "lon", lon_pairs_b)
+        lon_a = lax.ppermute(send_a, "lon", lon_pairs_a)
+        lat_b = lax.ppermute(rounded, "lat", lat_pairs_b)
+        lat_a = lax.ppermute(rounded, "lat", lat_pairs_a)
+        current, rounded, send_a, send_b, reservoir = step_call(
+            flags, rounded, lon_a, lon_b, lat_a, lat_b, sel_n, sel_s,
             reservoir, block_weight, entry_weight, read_weight)
         outputs.append(current)
     return jnp.stack(outputs)[:, None, None]

time: 235 us -> 227 us (0.966)
  the two profiles are of different devices: /device:TPU:414 before, /device:TPU:1 now
where the time goes in v2:
time: 227 us; the launch traced here: 226 us
  starting transfers between devices  193 us (85%)
  waiting for transfers between devices  12.5 us (6%)
  Pallas kernels  11 us (5%)
  local copies, waits for them, and re-layouts  7.71 us (3%)
    ppermute x8, starting transfers between devices, per_device(): lon_b = lax.ppermute(send_b, 'lon', lon_pairs_b)  126 us
    ppermute x8, starting transfers between devices, per_device(): lat_b = lax.ppermute(rounded, 'lat', lat_pairs_b)  29.5 us
    ppermute x8, starting transfers between devices, per_device(): lat_a = lax.ppermute(rounded, 'lat', lat_pairs_a)  22.2 us
    ppermute x8, starting transfers between devices, per_device(): lon_a = lax.ppermute(send_a, 'lon', lon_pairs_a)  15.4 us
    ppermute x8, waiting for transfers between devices, per_device(): lon_b = lax.ppermute(send_b, 'lon', lon_pairs_b)  12.4 us
    pallas_call x7, Pallas kernels, step_call(): pl.pallas_call(step_kernel, out_shape=out_shape, in_specs=[pl.BlockSpec(m...  11 us
  transfers between devices with their start and end apart: 32, of which 7 were waited for; matrix products, arithmetic and copies ran while one was open for 1% of the time, Pallas kernels for 0%

profile of v2, /device:TPU:1, one launch (start us, length us, event | category | flops | bytes accessed | tf_op | source)
XLA Modules:
  0.0 225.6 jit_solution(11497711510819735487)
XLA Ops:
  0.0 0.9 convert_bitcast_fusion.u_ref
  0.9 8.7 %collective-permute-start.2 = (bf16[64,256]{1,0:T(8,128)(2,1)S(1)}, bf16[64,256]{1,0:T(8,128)(2,1)S(1)}, u32[]{:S(2)}, u32[]{:S(2)}) collective-permute-start(bf16[64,256]{1,0:T(8,128)(2,1)S(1)} %convert_bitcast_fusion.u_ref), channel_id=1, source_target_pairs={{0,32},{32,0},{64,96},{96,64},{128,160},{160,128},{192,224},{224,1... | collective-permute-start | bytes 98312 | tf_op jit(solution)/shard_map/ppermute | solution.py:124
  9.7 1.9 collective-permute-start.3
  11.6 1.9 collective-permute-start
  13.6 15.9 %collective-permute-start.1 = (bf16[64,128]{1,0:T(8,128)(2,1)S(1)}, bf16[64,128]{1,0:T(8,128)(2,1)S(1)}, u32[]{:S(2)}, u32[]{:S(2)}) collective-permute-start(bf16[64,128]{1,0:T(8,128)(2,1)S(1)} %get-tuple-element.91), channel_id=1, source_target_pairs={{0,31},{1,2},{2,1},{3,4},{4,3},{5,6},{6,5},{7,8},{8,7},{9,10},{10,... | collective-permute-start | bytes 49160 | tf_op jit(solution)/shard_map/ppermute | solution.py:121
  29.5 0.8 slice_bitcast_fusion
  30.3 0.3 broadcast_multiply_fusion
  30.5 0.1 pad_add_fusion.flag_ref
  30.6 0.2 mul.37.sn_ref
  30.8 0.2 mul.40.ss_ref
  31.0 0.0 collective-permute-done.la_ref
  31.0 0.0 collective-permute-done.3.tb_ref
  31.0 0.0 copy-start
  31.0 1.6 copy-done
  32.6 1.0 copy-done.3
  33.7 0.9 copy-done.4
  34.6 1.6 shard_map.64
  36.2 1.9 collective-permute-start.6
  38.1 4.8 %collective-permute-start.7 = (bf16[64,256]{1,0:T(8,128)(2,1)S(1)}, bf16[64,256]{1,0:T(8,128)(2,1)S(1)}, u32[]{:S(2)}, u32[]{:S(2)}) collective-permute-start(bf16[64,256]{1,0:T(8,128)(2,1)S(1)} %get-tuple-element.42.u_ref), channel_id=1, source_target_pairs={{32,64},{64,32},{96,128},{128,96},{160,192},{192,160},{224,256},{2... | collective-permute-start | bytes 98312 | tf_op jit(solution)/shard_map/ppermute | solution.py:123
  43.0 1.9 collective-permute-start.4
  44.9 15.5 %collective-permute-start.5 = (bf16[64,128]{1,0:T(8,128)(2,1)S(1)}, bf16[64,128]{1,0:T(8,128)(2,1)S(1)}, u32[]{:S(2)}, u32[]{:S(2)}) collective-permute-start(bf16[64,128]{1,0:T(8,128)(2,1)S(1)} %get-tuple-element.44), channel_id=1, source_target_pairs={{0,31},{1,2},{2,1},{3,4},{4,3},{5,6},{6,5},{7,8},{8,7},{9,10},{10,... | collective-permute-start | bytes 49160 | tf_op jit(solution)/shard_map/ppermute | solution.py:121
  60.4 0.0 collective-permute-done.4.la_ref
  60.4 1.9 collective-permute-done.5.lb_ref
  62.3 0.0 collective-permute-done.6.ta_ref
  62.3 0.0 collective-permute-done.7.tb_ref
  62.3 1.6 shard_map.65
  63.9 1.9 collective-permute-start.10
  65.8 3.2 %collective-permute-start.11 = (bf16[64,256]{1,0:T(8,128)(2,1)S(1)}, bf16[64,256]{1,0:T(8,128)(2,1)S(1)}, u32[]{:S(2)}, u32[]{:S(2)}) collective-permute-start(bf16[64,256]{1,0:T(8,128)(2,1)S(1)} %get-tuple-element.47.u_ref), channel_id=1, source_target_pairs={{32,64},{64,32},{96,128},{128,96},{160,192},{192,160},{224,256},{2... | collective-permute-start | bytes 98312 | tf_op jit(solution)/shard_map/ppermute | solution.py:123
  69.0 1.9 collective-permute-start.8
  70.9 15.5 %collective-permute-start.9 = (bf16[64,128]{1,0:T(8,128)(2,1)S(1)}, bf16[64,128]{1,0:T(8,128)(2,1)S(1)}, u32[]{:S(2)}, u32[]{:S(2)}) collective-permute-start(bf16[64,128]{1,0:T(8,128)(2,1)S(1)} %get-tuple-element.49), channel_id=1, source_target_pairs={{0,31},{1,2},{2,1},{3,4},{4,3},{5,6},{6,5},{7,8},{8,7},{9,10},{10,... | collective-permute-start | bytes 49160 | tf_op jit(solution)/shard_map/ppermute | solution.py:121
  86.5 0.0 collective-permute-done.8.la_ref
  86.5 1.9 collective-permute-done.9.lb_ref
  88.4 1.6 shard_map.66
  89.9 1.9 collective-permute-start.14
  91.9 4.1 %collective-permute-start.15 = (bf16[64,256]{1,0:T(8,128)(2,1)S(1)}, bf16[64,256]{1,0:T(8,128)(2,1)S(1)}, u32[]{:S(2)}, u32[]{:S(2)}) collective-permute-start(bf16[64,256]{1,0:T(8,128)(2,1)S(1)} %get-tuple-element.52.u_ref), channel_id=1, source_target_pairs={{32,64},{64,32},{96,128},{128,96},{160,192},{192,160},{224,256},{2... | collective-permute-start | bytes 98312 | tf_op jit(solution)/shard_map/ppermute | solution.py:123
  96.0 1.9 collective-permute-start.12
  97.9 15.5 %collective-permute-start.13 = (bf16[64,128]{1,0:T(8,128)(2,1)S(1)}, bf16[64,128]{1,0:T(8,128)(2,1)S(1)}, u32[]{:S(2)}, u32[]{:S(2)}) collective-permute-start(bf16[64,128]{1,0:T(8,128)(2,1)S(1)} %get-tuple-element.54), channel_id=1, source_target_pairs={{0,31},{1,2},{2,1},{3,4},{4,3},{5,6},{6,5},{7,8},{8,7},{9,10},{10,... | collective-permute-start | bytes 49160 | tf_op jit(solution)/shard_map/ppermute | solution.py:121
  113.5 1.9 collective-permute-done.13.lb_ref
  115.4 1.6 shard_map.67
  116.9 1.9 collective-permute-start.18
  118.9 3.2 %collective-permute-start.19 = (bf16[64,256]{1,0:T(8,128)(2,1)S(1)}, bf16[64,256]{1,0:T(8,128)(2,1)S(1)}, u32[]{:S(2)}, u32[]{:S(2)}) collective-permute-start(bf16[64,256]{1,0:T(8,128)(2,1)S(1)} %get-tuple-element.57.u_ref), channel_id=1, source_target_pairs={{32,64},{64,32},{96,128},{128,96},{160,192},{192,160},{224,256},{2... | collective-permute-start | bytes 98312 | tf_op jit(solution)/shard_map/ppermute | solution.py:123
  122.0 1.9 collective-permute-start.16
  124.0 15.6 %collective-permute-start.17 = (bf16[64,128]{1,0:T(8,128)(2,1)S(1)}, bf16[64,128]{1,0:T(8,128)(2,1)S(1)}, u32[]{:S(2)}, u32[]{:S(2)}) collective-permute-start(bf16[64,128]{1,0:T(8,128)(2,1)S(1)} %get-tuple-element.59), channel_id=1, source_target_pairs={{0,31},{1,2},{2,1},{3,4},{4,3},{5,6},{6,5},{7,8},{8,7},{9,10},{10,... | collective-permute-start | bytes 49160 | tf_op jit(solution)/shard_map/ppermute | solution.py:121
  139.6 1.9 collective-permute-done.17.lb_ref
  141.6 1.6 shard_map.68
  143.1 1.9 collective-permute-start.22
  145.1 3.9 %collective-permute-start.23 = (bf16[64,256]{1,0:T(8,128)(2,1)S(1)}, bf16[64,256]{1,0:T(8,128)(2,1)S(1)}, u32[]{:S(2)}, u32[]{:S(2)}) collective-permute-start(bf16[64,256]{1,0:T(8,128)(2,1)S(1)} %get-tuple-element.62.u_ref), channel_id=1, source_target_pairs={{32,64},{64,32},{96,128},{128,96},{160,192},{192,160},{224,256},{2... | collective-permute-start | bytes 98312 | tf_op jit(solution)/shard_map/ppermute | solution.py:123
  148.9 1.9 collective-permute-start.20
  150.9 15.7 %collective-permute-start.21 = (bf16[64,128]{1,0:T(8,128)(2,1)S(1)}, bf16[64,128]{1,0:T(8,128)(2,1)S(1)}, u32[]{:S(2)}, u32[]{:S(2)}) collective-permute-start(bf16[64,128]{1,0:T(8,128)(2,1)S(1)} %get-tuple-element.64), channel_id=1, source_target_pairs={{0,31},{1,2},{2,1},{3,4},{4,3},{5,6},{6,5},{7,8},{8,7},{9,10},{10,... | collective-permute-start | bytes 49160 | tf_op jit(solution)/shard_map/ppermute | solution.py:121
  166.6 1.7 collective-permute-done.21.lb_ref
  168.3 1.6 shard_map.69
  169.9 1.9 collective-permute-start.26
  171.8 3.7 %collective-permute-start.27 = (bf16[64,256]{1,0:T(8,128)(2,1)S(1)}, bf16[64,256]{1,0:T(8,128)(2,1)S(1)}, u32[]{:S(2)}, u32[]{:S(2)}) collective-permute-start(bf16[64,256]{1,0:T(8,128)(2,1)S(1)} %get-tuple-element.67.u_ref), channel_id=1, source_target_pairs={{32,64},{64,32},{96,128},{128,96},{160,192},{192,160},{224,256},{2... | collective-permute-start | bytes 98312 | tf_op jit(solution)/shard_map/ppermute | solution.py:123
  175.5 1.9 collective-permute-start.24
  177.4 16.3 %collective-permute-start.25 = (bf16[64,128]{1,0:T(8,128)(2,1)S(1)}, bf16[64,128]{1,0:T(8,128)(2,1)S(1)}, u32[]{:S(2)}, u32[]{:S(2)}) collective-permute-start(bf16[64,128]{1,0:T(8,128)(2,1)S(1)} %get-tuple-element.69), channel_id=1, source_target_pairs={{0,31},{1,2},{2,1},{3,4},{4,3},{5,6},{6,5},{7,8},{8,7},{9,10},{10,... | collective-permute-start | bytes 49160 | tf_op jit(solution)/shard_map/ppermute | solution.py:121
  193.7 1.2 collective-permute-done.25.lb_ref
  194.9 1.6 shard_map.70
  196.5 1.9 collective-permute-start.30
  198.4 4.8 %collective-permute-start.31 = (bf16[64,256]{1,0:T(8,128)(2,1)S(1)}, bf16[64,256]{1,0:T(8,128)(2,1)S(1)}, u32[]{:S(2)}, u32[]{:S(2)}) collective-permute-start(bf16[64,256]{1,0:T(8,128)(2,1)S(1)} %get-tuple-element.72), channel_id=1, source_target_pairs={{32,64},{64,32},{96,128},{128,96},{160,192},{192,160},{224,256},{2... | collective-permute-start | bytes 98312 | tf_op jit(solution)/shard_map/ppermute | solution.py:123
  203.2 1.9 collective-permute-start.28
  205.1 15.6 %collective-permute-start.29 = (bf16[64,128]{1,0:T(8,128)(2,1)S(1)}, bf16[64,128]{1,0:T(8,128)(2,1)S(1)}, u32[]{:S(2)}, u32[]{:S(2)}) collective-permute-start(bf16[64,128]{1,0:T(8,128)(2,1)S(1)} %get-tuple-element.74), channel_id=1, source_target_pairs={{0,31},{1,2},{2,1},{3,4},{4,3},{5,6},{6,5},{7,8},{8,7},{9,10},{10,... | collective-permute-start | bytes 49160 | tf_op jit(solution)/shard_map/ppermute | solution.py:121
  220.7 1.9 collective-permute-done.29
  222.6 2.2 shard_map.71
  224.8 0.8 copy-done.5
  (36 shorter events, 0.1 us)
Async XLA Ops:
  0.0 31.0 %copy-start.2 = (bf16[1,1,2048,256]{3,2,1,0:T(8,128)(2,1)S(1)}, bf16[1,1,2048,256]{3,2,1,0:T(8,128)(2,1)}, u32[]{:S(2)}) copy-start(bf16[1,1,2048,256]{3,2,1,0:T(8,128)(2,1)} %param.10) | copy-start | bytes 3145732
  0.9 30.1 %collective-permute-start.2 = (bf16[64,256]{1,0:T(8,128)(2,1)S(1)}, bf16[64,256]{1,0:T(8,128)(2,1)S(1)}, u32[]{:S(2)}, u32[]{:S(2)}) collective-permute-start(bf16[64,256]{1,0:T(8,128)(2,1)S(1)} %convert_bitcast_fusion.u_ref), channel_id=1, source_target_pairs={{0,32},{32,0},{64,96},{96,64},{128,160},{160,128},{192,224},{224,1... | collective-permute-start | bytes 98312 | tf_op jit(solution)/shard_map/ppermute | solution.py:124
  9.7 21.3 %collective-permute-start.3 = (bf16[64,256]{1,0:T(8,128)(2,1)S(1)}, bf16[64,256]{1,0:T(8,128)(2,1)S(1)}, u32[]{:S(2)}, u32[]{:S(2)}) collective-permute-start(bf16[64,256]{1,0:T(8,128)(2,1)S(1)} %convert_bitcast_fusion.u_ref), channel_id=1, source_target_pairs={{32,64},{64,32},{96,128},{128,96},{160,192},{192,160},{224,256},{2... | collective-permute-start | bytes 98312 | tf_op jit(solution)/shard_map/ppermute | solution.py:123
  11.6 19.3 %collective-permute-start = (bf16[64,128]{1,0:T(8,128)(2,1)S(1)}, bf16[64,128]{1,0:T(8,128)(2,1)S(1)}, u32[]{:S(2)}, u32[]{:S(2)}) collective-permute-start(bf16[64,128]{1,0:T(8,128)(2,1)S(1)} %get-tuple-element.92), channel_id=1, source_target_pairs={{0,1},{1,0},{2,3},{3,2},{4,5},{5,4},{6,7},{7,6},{8,9},{9,8},{10,11... | collective-permute-start | bytes 49160 | tf_op jit(solution)/shard_map/ppermute | solution.py:122
  13.6 17.4 %collective-permute-start.1 = (bf16[64,128]{1,0:T(8,128)(2,1)S(1)}, bf16[64,128]{1,0:T(8,128)(2,1)S(1)}, u32[]{:S(2)}, u32[]{:S(2)}) collective-permute-start(bf16[64,128]{1,0:T(8,128)(2,1)S(1)} %get-tuple-element.91), channel_id=1, source_target_pairs={{0,31},{1,2},{2,1},{3,4},{4,3},{5,6},{6,5},{7,8},{8,7},{9,10},{10,... | collective-permute-start | bytes 49160 | tf_op jit(solution)/shard_map/ppermute | solution.py:121
  31.0 1.6 copy-start
  32.6 1.0 copy-start.3
  33.7 0.9 copy-start.4
  34.6 27.7 %copy-start.1 = (bf16[1,1,16,4,128,128]{5,4,3,2,1,0:T(8,128)(2,1)S(1)}, bf16[1,1,16,4,128,128]{5,4,3,2,1,0:T(8,128)(2,1)}, u32[]{:S(2)}) copy-start(bf16[1,1,16,4,128,128]{5,4,3,2,1,0:T(8,128)(2,1)} %param.8) | copy-start | bytes 6291460
  36.2 26.1 %collective-permute-start.6 = (bf16[64,256]{1,0:T(8,128)(2,1)S(1)}, bf16[64,256]{1,0:T(8,128)(2,1)S(1)}, u32[]{:S(2)}, u32[]{:S(2)}) collective-permute-start(bf16[64,256]{1,0:T(8,128)(2,1)S(1)} %get-tuple-element.42.u_ref), channel_id=1, source_target_pairs={{0,32},{32,0},{64,96},{96,64},{128,160},{160,128},{192,224},{224,1... | collective-permute-start | bytes 98312 | tf_op jit(solution)/shard_map/ppermute | solution.py:124
  38.1 24.2 %collective-permute-start.7 = (bf16[64,256]{1,0:T(8,128)(2,1)S(1)}, bf16[64,256]{1,0:T(8,128)(2,1)S(1)}, u32[]{:S(2)}, u32[]{:S(2)}) collective-permute-start(bf16[64,256]{1,0:T(8,128)(2,1)S(1)} %get-tuple-element.42.u_ref), channel_id=1, source_target_pairs={{32,64},{64,32},{96,128},{128,96},{160,192},{192,160},{224,256},{2... | collective-permute-start | bytes 98312 | tf_op jit(solution)/shard_map/ppermute | solution.py:123
  43.0 17.4 %collective-permute-start.4 = (bf16[64,128]{1,0:T(8,128)(2,1)S(1)}, bf16[64,128]{1,0:T(8,128)(2,1)S(1)}, u32[]{:S(2)}, u32[]{:S(2)}) collective-permute-start(bf16[64,128]{1,0:T(8,128)(2,1)S(1)} %get-tuple-element.43), channel_id=1, source_target_pairs={{0,1},{1,0},{2,3},{3,2},{4,5},{5,4},{6,7},{7,6},{8,9},{9,8},{10,11... | collective-permute-start | bytes 49160 | tf_op jit(solution)/shard_map/ppermute | solution.py:122
  44.9 17.4 %collective-permute-start.5 = (bf16[64,128]{1,0:T(8,128)(2,1)S(1)}, bf16[64,128]{1,0:T(8,128)(2,1)S(1)}, u32[]{:S(2)}, u32[]{:S(2)}) collective-permute-start(bf16[64,128]{1,0:T(8,128)(2,1)S(1)} %get-tuple-element.44), channel_id=1, source_target_pairs={{0,31},{1,2},{2,1},{3,4},{4,3},{5,6},{6,5},{7,8},{8,7},{9,10},{10,... | collective-permute-start | bytes 49160 | tf_op jit(solution)/shard_map/ppermute | solution.py:121
  63.9 24.4 %collective-permute-start.10 = (bf16[64,256]{1,0:T(8,128)(2,1)S(1)}, bf16[64,256]{1,0:T(8,128)(2,1)S(1)}, u32[]{:S(2)}, u32[]{:S(2)}) collective-permute-start(bf16[64,256]{1,0:T(8,128)(2,1)S(1)} %get-tuple-element.47.u_ref), channel_id=1, source_target_pairs={{0,32},{32,0},{64,96},{96,64},{128,160},{160,128},{192,224},{224,1... | collective-permute-start | bytes 98312 | tf_op jit(solution)/shard_map/ppermute | solution.py:124
  65.8 22.5 %collective-permute-start.11 = (bf16[64,256]{1,0:T(8,128)(2,1)S(1)}, bf16[64,256]{1,0:T(8,128)(2,1)S(1)}, u32[]{:S(2)}, u32[]{:S(2)}) collective-permute-start(bf16[64,256]{1,0:T(8,128)(2,1)S(1)} %get-tuple-element.47.u_ref), channel_id=1, source_target_pairs={{32,64},{64,32},{96,128},{128,96},{160,192},{192,160},{224,256},{2... | collective-permute-start | bytes 98312 | tf_op jit(solution)/shard_map/ppermute | solution.py:123
  69.0 17.5 %collective-permute-start.8 = (bf16[64,128]{1,0:T(8,128)(2,1)S(1)}, bf16[64,128]{1,0:T(8,128)(2,1)S(1)}, u32[]{:S(2)}, u32[]{:S(2)}) collective-permute-start(bf16[64,128]{1,0:T(8,128)(2,1)S(1)} %get-tuple-element.48), channel_id=1, source_target_pairs={{0,1},{1,0},{2,3},{3,2},{4,5},{5,4},{6,7},{7,6},{8,9},{9,8},{10,11... | collective-permute-start | bytes 49160 | tf_op jit(solution)/shard_map/ppermute | solution.py:122
  70.9 17.4 %collective-permute-start.9 = (bf16[64,128]{1,0:T(8,128)(2,1)S(1)}, bf16[64,128]{1,0:T(8,128)(2,1)S(1)}, u32[]{:S(2)}, u32[]{:S(2)}) collective-permute-start(bf16[64,128]{1,0:T(8,128)(2,1)S(1)} %get-tuple-element.49), channel_id=1, source_target_pairs={{0,31},{1,2},{2,1},{3,4},{4,3},{5,6},{6,5},{7,8},{8,7},{9,10},{10,... | collective-permute-start | bytes 49160 | tf_op jit(solution)/shard_map/ppermute | solution.py:121
  89.9 25.4 %collective-permute-start.14 = (bf16[64,256]{1,0:T(8,128)(2,1)S(1)}, bf16[64,256]{1,0:T(8,128)(2,1)S(1)}, u32[]{:S(2)}, u32[]{:S(2)}) collective-permute-start(bf16[64,256]{1,0:T(8,128)(2,1)S(1)} %get-tuple-element.52.u_ref), channel_id=1, source_target_pairs={{0,32},{32,0},{64,96},{96,64},{128,160},{160,128},{192,224},{224,1... | collective-permute-start | bytes 98312 | tf_op jit(solution)/shard_map/ppermute | solution.py:124
  91.9 23.5 %collective-permute-start.15 = (bf16[64,256]{1,0:T(8,128)(2,1)S(1)}, bf16[64,256]{1,0:T(8,128)(2,1)S(1)}, u32[]{:S(2)}, u32[]{:S(2)}) collective-permute-start(bf16[64,256]{1,0:T(8,128)(2,1)S(1)} %get-tuple-element.52.u_ref), channel_id=1, source_target_pairs={{32,64},{64,32},{96,128},{128,96},{160,192},{192,160},{224,256},{2... | collective-permute-start | bytes 98312 | tf_op jit(solution)/shard_map/ppermute | solution.py:123
  96.0 17.4 %collective-permute-start.12 = (bf16[64,128]{1,0:T(8,128)(2,1)S(1)}, bf16[64,128]{1,0:T(8,128)(2,1)S(1)}, u32[]{:S(2)}, u32[]{:S(2)}) collective-permute-start(bf16[64,128]{1,0:T(8,128)(2,1)S(1)} %get-tuple-element.53), channel_id=1, source_target_pairs={{0,1},{1,0},{2,3},{3,2},{4,5},{5,4},{6,7},{7,6},{8,9},{9,8},{10,11... | collective-permute-start | bytes 49160 | tf_op jit(solution)/shard_map/ppermute | solution.py:122
  97.9 17.4 %collective-permute-start.13 = (bf16[64,128]{1,0:T(8,128)(2,1)S(1)}, bf16[64,128]{1,0:T(8,128)(2,1)S(1)}, u32[]{:S(2)}, u32[]{:S(2)}) collective-permute-start(bf16[64,128]{1,0:T(8,128)(2,1)S(1)} %get-tuple-element.54), channel_id=1, source_target_pairs={{0,31},{1,2},{2,1},{3,4},{4,3},{5,6},{6,5},{7,8},{8,7},{9,10},{10,... | collective-permute-start | bytes 49160 | tf_op jit(solution)/shard_map/ppermute | solution.py:121
  116.9 24.6 %collective-permute-start.18 = (bf16[64,256]{1,0:T(8,128)(2,1)S(1)}, bf16[64,256]{1,0:T(8,128)(2,1)S(1)}, u32[]{:S(2)}, u32[]{:S(2)}) collective-permute-start(bf16[64,256]{1,0:T(8,128)(2,1)S(1)} %get-tuple-element.57.u_ref), channel_id=1, source_target_pairs={{0,32},{32,0},{64,96},{96,64},{128,160},{160,128},{192,224},{224,1... | collective-permute-start | bytes 98312 | tf_op jit(solution)/shard_map/ppermute | solution.py:124
  118.9 22.7 %collective-permute-start.19 = (bf16[64,256]{1,0:T(8,128)(2,1)S(1)}, bf16[64,256]{1,0:T(8,128)(2,1)S(1)}, u32[]{:S(2)}, u32[]{:S(2)}) collective-permute-start(bf16[64,256]{1,0:T(8,128)(2,1)S(1)} %get-tuple-element.57.u_ref), channel_id=1, source_target_pairs={{32,64},{64,32},{96,128},{128,96},{160,192},{192,160},{224,256},{2... | collective-permute-start | bytes 98312 | tf_op jit(solution)/shard_map/ppermute | solution.py:123
  122.0 17.6 %collective-permute-start.16 = (bf16[64,128]{1,0:T(8,128)(2,1)S(1)}, bf16[64,128]{1,0:T(8,128)(2,1)S(1)}, u32[]{:S(2)}, u32[]{:S(2)}) collective-permute-start(bf16[64,128]{1,0:T(8,128)(2,1)S(1)} %get-tuple-element.58), channel_id=1, source_target_pairs={{0,1},{1,0},{2,3},{3,2},{4,5},{5,4},{6,7},{7,6},{8,9},{9,8},{10,11... | collective-permute-start | bytes 49160 | tf_op jit(solution)/shard_map/ppermute | solution.py:122
  124.0 17.6 %collective-permute-start.17 = (bf16[64,128]{1,0:T(8,128)(2,1)S(1)}, bf16[64,128]{1,0:T(8,128)(2,1)S(1)}, u32[]{:S(2)}, u32[]{:S(2)}) collective-permute-start(bf16[64,128]{1,0:T(8,128)(2,1)S(1)} %get-tuple-element.59), channel_id=1, source_target_pairs={{0,31},{1,2},{2,1},{3,4},{4,3},{5,6},{6,5},{7,8},{8,7},{9,10},{10,... | collective-permute-start | bytes 49160 | tf_op jit(solution)/shard_map/ppermute | solution.py:121
  143.1 25.2 %collective-permute-start.22 = (bf16[64,256]{1,0:T(8,128)(2,1)S(1)}, bf16[64,256]{1,0:T(8,128)(2,1)S(1)}, u32[]{:S(2)}, u32[]{:S(2)}) collective-permute-start(bf16[64,256]{1,0:T(8,128)(2,1)S(1)} %get-tuple-element.62.u_ref), channel_id=1, source_target_pairs={{0,32},{32,0},{64,96},{96,64},{128,160},{160,128},{192,224},{224,1... | collective-permute-start | bytes 98312 | tf_op jit(solution)/shard_map/ppermute | solution.py:124
  145.1 23.2 %collective-permute-start.23 = (bf16[64,256]{1,0:T(8,128)(2,1)S(1)}, bf16[64,256]{1,0:T(8,128)(2,1)S(1)}, u32[]{:S(2)}, u32[]{:S(2)}) collective-permute-start(bf16[64,256]{1,0:T(8,128)(2,1)S(1)} %get-tuple-element.62.u_ref), channel_id=1, source_target_pairs={{32,64},{64,32},{96,128},{128,96},{160,192},{192,160},{224,256},{2... | collective-permute-start | bytes 98312 | tf_op jit(solution)/shard_map/ppermute | solution.py:123
  148.9 17.6 %collective-permute-start.20 = (bf16[64,128]{1,0:T(8,128)(2,1)S(1)}, bf16[64,128]{1,0:T(8,128)(2,1)S(1)}, u32[]{:S(2)}, u32[]{:S(2)}) collective-permute-start(bf16[64,128]{1,0:T(8,128)(2,1)S(1)} %get-tuple-element.63), channel_id=1, source_target_pairs={{0,1},{1,0},{2,3},{3,2},{4,5},{5,4},{6,7},{7,6},{8,9},{9,8},{10,11... | collective-permute-start | bytes 49160 | tf_op jit(solution)/shard_map/ppermute | solution.py:122
  150.9 17.4 %collective-permute-start.21 = (bf16[64,128]{1,0:T(8,128)(2,1)S(1)}, bf16[64,128]{1,0:T(8,128)(2,1)S(1)}, u32[]{:S(2)}, u32[]{:S(2)}) collective-permute-start(bf16[64,128]{1,0:T(8,128)(2,1)S(1)} %get-tuple-element.64), channel_id=1, source_target_pairs={{0,31},{1,2},{2,1},{3,4},{4,3},{5,6},{6,5},{7,8},{8,7},{9,10},{10,... | collective-permute-start | bytes 49160 | tf_op jit(solution)/shard_map/ppermute | solution.py:121
  169.9 25.0 %collective-permute-start.26 = (bf16[64,256]{1,0:T(8,128)(2,1)S(1)}, bf16[64,256]{1,0:T(8,128)(2,1)S(1)}, u32[]{:S(2)}, u32[]{:S(2)}) collective-permute-start(bf16[64,256]{1,0:T(8,128)(2,1)S(1)} %get-tuple-element.67.u_ref), channel_id=1, source_target_pairs={{0,32},{32,0},{64,96},{96,64},{128,160},{160,128},{192,224},{224,1... | collective-permute-start | bytes 98312 | tf_op jit(solution)/shard_map/ppermute | solution.py:124
  171.8 23.1 %collective-permute-start.27 = (bf16[64,256]{1,0:T(8,128)(2,1)S(1)}, bf16[64,256]{1,0:T(8,128)(2,1)S(1)}, u32[]{:S(2)}, u32[]{:S(2)}) collective-permute-start(bf16[64,256]{1,0:T(8,128)(2,1)S(1)} %get-tuple-element.67.u_ref), channel_id=1, source_target_pairs={{32,64},{64,32},{96,128},{128,96},{160,192},{192,160},{224,256},{2... | collective-permute-start | bytes 98312 | tf_op jit(solution)/shard_map/ppermute | solution.py:123
  175.5 18.2 %collective-permute-start.24 = (bf16[64,128]{1,0:T(8,128)(2,1)S(1)}, bf16[64,128]{1,0:T(8,128)(2,1)S(1)}, u32[]{:S(2)}, u32[]{:S(2)}) collective-permute-start(bf16[64,128]{1,0:T(8,128)(2,1)S(1)} %get-tuple-element.68), channel_id=1, source_target_pairs={{0,1},{1,0},{2,3},{3,2},{4,5},{5,4},{6,7},{7,6},{8,9},{9,8},{10,11... | collective-permute-start | bytes 49160 | tf_op jit(solution)/shard_map/ppermute | solution.py:122
  177.4 17.5 %collective-permute-start.25 = (bf16[64,128]{1,0:T(8,128)(2,1)S(1)}, bf16[64,128]{1,0:T(8,128)(2,1)S(1)}, u32[]{:S(2)}, u32[]{:S(2)}) collective-permute-start(bf16[64,128]{1,0:T(8,128)(2,1)S(1)} %get-tuple-element.69), channel_id=1, source_target_pairs={{0,31},{1,2},{2,1},{3,4},{4,3},{5,6},{6,5},{7,8},{8,7},{9,10},{10,... | collective-permute-start | bytes 49160 | tf_op jit(solution)/shard_map/ppermute | solution.py:121
  196.5 26.1 %collective-permute-start.30 = (bf16[64,256]{1,0:T(8,128)(2,1)S(1)}, bf16[64,256]{1,0:T(8,128)(2,1)S(1)}, u32[]{:S(2)}, u32[]{:S(2)}) collective-permute-start(bf16[64,256]{1,0:T(8,128)(2,1)S(1)} %get-tuple-element.72), channel_id=1, source_target_pairs={{0,32},{32,0},{64,96},{96,64},{128,160},{160,128},{192,224},{224,1... | collective-permute-start | bytes 98312 | tf_op jit(solution)/shard_map/ppermute | solution.py:124
  198.4 24.2 %collective-permute-start.31 = (bf16[64,256]{1,0:T(8,128)(2,1)S(1)}, bf16[64,256]{1,0:T(8,128)(2,1)S(1)}, u32[]{:S(2)}, u32[]{:S(2)}) collective-permute-start(bf16[64,256]{1,0:T(8,128)(2,1)S(1)} %get-tuple-element.72), channel_id=1, source_target_pairs={{32,64},{64,32},{96,128},{128,96},{160,192},{192,160},{224,256},{2... | collective-permute-start | bytes 98312 | tf_op jit(solution)/shard_map/ppermute | solution.py:123
  203.2 17.5 %collective-permute-start.28 = (bf16[64,128]{1,0:T(8,128)(2,1)S(1)}, bf16[64,128]{1,0:T(8,128)(2,1)S(1)}, u32[]{:S(2)}, u32[]{:S(2)}) collective-permute-start(bf16[64,128]{1,0:T(8,128)(2,1)S(1)} %get-tuple-element.73), channel_id=1, source_target_pairs={{0,1},{1,0},{2,3},{3,2},{4,5},{5,4},{6,7},{7,6},{8,9},{9,8},{10,11... | collective-permute-start | bytes 49160 | tf_op jit(solution)/shard_map/ppermute | solution.py:122
  205.1 17.5 %collective-permute-start.29 = (bf16[64,128]{1,0:T(8,128)(2,1)S(1)}, bf16[64,128]{1,0:T(8,128)(2,1)S(1)}, u32[]{:S(2)}, u32[]{:S(2)}) collective-permute-start(bf16[64,128]{1,0:T(8,128)(2,1)S(1)} %get-tuple-element.74), channel_id=1, source_target_pairs={{0,31},{1,2},{2,1},{3,4},{4,3},{5,6},{6,5},{7,8},{8,7},{9,10},{10,... | collective-permute-start | bytes 49160 | tf_op jit(solution)/shard_map/ppermute | solution.py:121
  224.8 0.8 copy-start.5

commit v3 on v2

--- a/solution.py
+++ b/solution.py
@@ -1,20 +1,19 @@
 import jax
 import jax.numpy as jnp
-import numpy as np
 from jax import lax
 from jax.experimental import pallas as pl
 from jax.experimental.pallas import tpu as pltpu
 from jax.sharding import PartitionSpec as P
 
+
 VARS = 32
-LATR = 4
 LONC = 2
 OV = 4
 STEPS = 8
 PTS = 8
 
 
-def selector(slot_list, breadth):
+def selector(slot_list):
     onehot = (slot_list[:, None] == jnp.arange(PTS, dtype=jnp.int32)[None, :]).astype(jnp.bfloat16)
     eye = jnp.eye(VARS, dtype=jnp.bfloat16)
     full = onehot.T[:, None, :, None] * eye[None, :, None, :]
@@ -98,10 +97,9 @@
     entry_weight = input_weight[0, 0]
     read_weight = readout[0, 0]
     lists = intersection[0, 0]
-    breadth = block_weight.shape[2]
     half = current.shape[1] // LONC
-    sel_n = selector(lists[0], breadth)
-    sel_s = selector(lists[1], breadth)
+    sel_n = selector(lists[0])
+    sel_s = selector(lists[1])
     lon_even = (lax.axis_index("lon") % 2 == 0).astype(jnp.int32)
     lat_even = (lax.axis_index("lat") % 2 == 0).astype(jnp.int32)
     flags = jnp.stack([lon_even, lat_even])
@@ -117,7 +115,7 @@
     send_a = jnp.where(lon_even == 1, high, low)
     send_b = jnp.where(lon_even == 1, low, high)
     outputs = []
-    for moment in range(STEPS):
+    for _ in range(STEPS):
         lon_b = lax.ppermute(send_b, "lon", lon_pairs_b)
         lon_a = lax.ppermute(send_a, "lon", lon_pairs_a)
         lat_b = lax.ppermute(rounded, "lat", lat_pairs_b)

time: 227 us -> 227 us (level)
  no operation moved by 1% of the time
where the time goes in v3:
time: 227 us; the launch traced here: 226 us
  starting transfers between devices  193 us (85%)
  waiting for transfers between devices  12.5 us (6%)
  Pallas kernels  11 us (5%)
  local copies, waits for them, and re-layouts  7.71 us (3%)
    ppermute x8, starting transfers between devices, per_device(): lon_b = lax.ppermute(send_b, 'lon', lon_pairs_b)  126 us
    ppermute x8, starting transfers between devices, per_device(): lat_b = lax.ppermute(rounded, 'lat', lat_pairs_b)  29.5 us
    ppermute x8, starting transfers between devices, per_device(): lat_a = lax.ppermute(rounded, 'lat', lat_pairs_a)  22.2 us
    ppermute x8, starting transfers between devices, per_device(): lon_a = lax.ppermute(send_a, 'lon', lon_pairs_a)  15.4 us
    ppermute x8, waiting for transfers between devices, per_device(): lon_b = lax.ppermute(send_b, 'lon', lon_pairs_b)  12.4 us
    pallas_call x7, Pallas kernels, step_call(): pl.pallas_call(step_kernel, out_shape=out_shape, in_specs=[pl.BlockSpec(m...  11 us
  transfers between devices with their start and end apart: 32, of which 7 were waited for; matrix products, arithmetic and copies ran while one was open for 1% of the time, Pallas kernels for 0%

profile of v3, /device:TPU:1, one launch (start us, length us, event | category | flops | bytes accessed | tf_op | source)
XLA Modules:
  0.0 225.6 jit_solution(11497711510819735487)
XLA Ops:
  0.0 0.9 convert_bitcast_fusion.u_ref
  0.9 8.7 %collective-permute-start.2 = (bf16[64,256]{1,0:T(8,128)(2,1)S(1)}, bf16[64,256]{1,0:T(8,128)(2,1)S(1)}, u32[]{:S(2)}, u32[]{:S(2)}) collective-permute-start(bf16[64,256]{1,0:T(8,128)(2,1)S(1)} %convert_bitcast_fusion.u_ref), channel_id=1, source_target_pairs={{0,32},{32,0},{64,96},{96,64},{128,160},{160,128},{192,224},{224,1... | collective-permute-start | bytes 98312 | tf_op jit(solution)/shard_map/ppermute | solution.py:122
  9.7 1.9 collective-permute-start.3
  11.6 1.9 collective-permute-start
  13.6 15.9 %collective-permute-start.1 = (bf16[64,128]{1,0:T(8,128)(2,1)S(1)}, bf16[64,128]{1,0:T(8,128)(2,1)S(1)}, u32[]{:S(2)}, u32[]{:S(2)}) collective-permute-start(bf16[64,128]{1,0:T(8,128)(2,1)S(1)} %get-tuple-element.91), channel_id=1, source_target_pairs={{0,31},{1,2},{2,1},{3,4},{4,3},{5,6},{6,5},{7,8},{8,7},{9,10},{10,... | collective-permute-start | bytes 49160 | tf_op jit(solution)/shard_map/ppermute | solution.py:119
  29.5 0.8 slice_bitcast_fusion
  30.3 0.3 broadcast_multiply_fusion
  30.5 0.1 pad_add_fusion.flag_ref
  30.6 0.2 mul.37.sn_ref
  30.8 0.2 mul.40.ss_ref
  31.0 0.0 collective-permute-done.la_ref
  31.0 0.0 collective-permute-done.3.tb_ref
  31.0 0.0 copy-start
  31.0 1.6 copy-done
  32.6 1.0 copy-done.3
  33.7 0.9 copy-done.4
  34.6 1.6 shard_map.64
  36.2 1.9 collective-permute-start.6
  38.1 4.8 %collective-permute-start.7 = (bf16[64,256]{1,0:T(8,128)(2,1)S(1)}, bf16[64,256]{1,0:T(8,128)(2,1)S(1)}, u32[]{:S(2)}, u32[]{:S(2)}) collective-permute-start(bf16[64,256]{1,0:T(8,128)(2,1)S(1)} %get-tuple-element.42.u_ref), channel_id=1, source_target_pairs={{32,64},{64,32},{96,128},{128,96},{160,192},{192,160},{224,256},{2... | collective-permute-start | bytes 98312 | tf_op jit(solution)/shard_map/ppermute | solution.py:121
  43.0 1.9 collective-permute-start.4
  44.9 15.5 %collective-permute-start.5 = (bf16[64,128]{1,0:T(8,128)(2,1)S(1)}, bf16[64,128]{1,0:T(8,128)(2,1)S(1)}, u32[]{:S(2)}, u32[]{:S(2)}) collective-permute-start(bf16[64,128]{1,0:T(8,128)(2,1)S(1)} %get-tuple-element.44), channel_id=1, source_target_pairs={{0,31},{1,2},{2,1},{3,4},{4,3},{5,6},{6,5},{7,8},{8,7},{9,10},{10,... | collective-permute-start | bytes 49160 | tf_op jit(solution)/shard_map/ppermute | solution.py:119
  60.4 0.0 collective-permute-done.4.la_ref
  60.4 1.9 collective-permute-done.5.lb_ref
  62.3 0.0 collective-permute-done.6.ta_ref
  62.3 0.0 collective-permute-done.7.tb_ref
  62.3 1.6 shard_map.65
  63.9 1.9 collective-permute-start.10
  65.8 3.2 %collective-permute-start.11 = (bf16[64,256]{1,0:T(8,128)(2,1)S(1)}, bf16[64,256]{1,0:T(8,128)(2,1)S(1)}, u32[]{:S(2)}, u32[]{:S(2)}) collective-permute-start(bf16[64,256]{1,0:T(8,128)(2,1)S(1)} %get-tuple-element.47.u_ref), channel_id=1, source_target_pairs={{32,64},{64,32},{96,128},{128,96},{160,192},{192,160},{224,256},{2... | collective-permute-start | bytes 98312 | tf_op jit(solution)/shard_map/ppermute | solution.py:121
  69.0 1.9 collective-permute-start.8
  70.9 15.5 %collective-permute-start.9 = (bf16[64,128]{1,0:T(8,128)(2,1)S(1)}, bf16[64,128]{1,0:T(8,128)(2,1)S(1)}, u32[]{:S(2)}, u32[]{:S(2)}) collective-permute-start(bf16[64,128]{1,0:T(8,128)(2,1)S(1)} %get-tuple-element.49), channel_id=1, source_target_pairs={{0,31},{1,2},{2,1},{3,4},{4,3},{5,6},{6,5},{7,8},{8,7},{9,10},{10,... | collective-permute-start | bytes 49160 | tf_op jit(solution)/shard_map/ppermute | solution.py:119
  86.5 0.0 collective-permute-done.8.la_ref
  86.5 1.9 collective-permute-done.9.lb_ref
  88.4 1.6 shard_map.66
  89.9 1.9 collective-permute-start.14
  91.9 4.1 %collective-permute-start.15 = (bf16[64,256]{1,0:T(8,128)(2,1)S(1)}, bf16[64,256]{1,0:T(8,128)(2,1)S(1)}, u32[]{:S(2)}, u32[]{:S(2)}) collective-permute-start(bf16[64,256]{1,0:T(8,128)(2,1)S(1)} %get-tuple-element.52.u_ref), channel_id=1, source_target_pairs={{32,64},{64,32},{96,128},{128,96},{160,192},{192,160},{224,256},{2... | collective-permute-start | bytes 98312 | tf_op jit(solution)/shard_map/ppermute | solution.py:121
  96.0 1.9 collective-permute-start.12
  97.9 15.5 %collective-permute-start.13 = (bf16[64,128]{1,0:T(8,128)(2,1)S(1)}, bf16[64,128]{1,0:T(8,128)(2,1)S(1)}, u32[]{:S(2)}, u32[]{:S(2)}) collective-permute-start(bf16[64,128]{1,0:T(8,128)(2,1)S(1)} %get-tuple-element.54), channel_id=1, source_target_pairs={{0,31},{1,2},{2,1},{3,4},{4,3},{5,6},{6,5},{7,8},{8,7},{9,10},{10,... | collective-permute-start | bytes 49160 | tf_op jit(solution)/shard_map/ppermute | solution.py:119
  113.5 1.9 collective-permute-done.13.lb_ref
  115.4 1.6 shard_map.67
  116.9 1.9 collective-permute-start.18
  118.9 3.2 %collective-permute-start.19 = (bf16[64,256]{1,0:T(8,128)(2,1)S(1)}, bf16[64,256]{1,0:T(8,128)(2,1)S(1)}, u32[]{:S(2)}, u32[]{:S(2)}) collective-permute-start(bf16[64,256]{1,0:T(8,128)(2,1)S(1)} %get-tuple-element.57.u_ref), channel_id=1, source_target_pairs={{32,64},{64,32},{96,128},{128,96},{160,192},{192,160},{224,256},{2... | collective-permute-start | bytes 98312 | tf_op jit(solution)/shard_map/ppermute | solution.py:121
  122.0 1.9 collective-permute-start.16
  124.0 15.6 %collective-permute-start.17 = (bf16[64,128]{1,0:T(8,128)(2,1)S(1)}, bf16[64,128]{1,0:T(8,128)(2,1)S(1)}, u32[]{:S(2)}, u32[]{:S(2)}) collective-permute-start(bf16[64,128]{1,0:T(8,128)(2,1)S(1)} %get-tuple-element.59), channel_id=1, source_target_pairs={{0,31},{1,2},{2,1},{3,4},{4,3},{5,6},{6,5},{7,8},{8,7},{9,10},{10,... | collective-permute-start | bytes 49160 | tf_op jit(solution)/shard_map/ppermute | solution.py:119
  139.6 1.9 collective-permute-done.17.lb_ref
  141.6 1.6 shard_map.68
  143.1 1.9 collective-permute-start.22
  145.1 3.9 %collective-permute-start.23 = (bf16[64,256]{1,0:T(8,128)(2,1)S(1)}, bf16[64,256]{1,0:T(8,128)(2,1)S(1)}, u32[]{:S(2)}, u32[]{:S(2)}) collective-permute-start(bf16[64,256]{1,0:T(8,128)(2,1)S(1)} %get-tuple-element.62.u_ref), channel_id=1, source_target_pairs={{32,64},{64,32},{96,128},{128,96},{160,192},{192,160},{224,256},{2... | collective-permute-start | bytes 98312 | tf_op jit(solution)/shard_map/ppermute | solution.py:121
  148.9 1.9 collective-permute-start.20
  150.9 15.7 %collective-permute-start.21 = (bf16[64,128]{1,0:T(8,128)(2,1)S(1)}, bf16[64,128]{1,0:T(8,128)(2,1)S(1)}, u32[]{:S(2)}, u32[]{:S(2)}) collective-permute-start(bf16[64,128]{1,0:T(8,128)(2,1)S(1)} %get-tuple-element.64), channel_id=1, source_target_pairs={{0,31},{1,2},{2,1},{3,4},{4,3},{5,6},{6,5},{7,8},{8,7},{9,10},{10,... | collective-permute-start | bytes 49160 | tf_op jit(solution)/shard_map/ppermute | solution.py:119
  166.6 1.7 collective-permute-done.21.lb_ref
  168.3 1.6 shard_map.69
  169.9 1.9 collective-permute-start.26
  171.8 3.7 %collective-permute-start.27 = (bf16[64,256]{1,0:T(8,128)(2,1)S(1)}, bf16[64,256]{1,0:T(8,128)(2,1)S(1)}, u32[]{:S(2)}, u32[]{:S(2)}) collective-permute-start(bf16[64,256]{1,0:T(8,128)(2,1)S(1)} %get-tuple-element.67.u_ref), channel_id=1, source_target_pairs={{32,64},{64,32},{96,128},{128,96},{160,192},{192,160},{224,256},{2... | collective-permute-start | bytes 98312 | tf_op jit(solution)/shard_map/ppermute | solution.py:121
  175.5 1.9 collective-permute-start.24
  177.4 16.3 %collective-permute-start.25 = (bf16[64,128]{1,0:T(8,128)(2,1)S(1)}, bf16[64,128]{1,0:T(8,128)(2,1)S(1)}, u32[]{:S(2)}, u32[]{:S(2)}) collective-permute-start(bf16[64,128]{1,0:T(8,128)(2,1)S(1)} %get-tuple-element.69), channel_id=1, source_target_pairs={{0,31},{1,2},{2,1},{3,4},{4,3},{5,6},{6,5},{7,8},{8,7},{9,10},{10,... | collective-permute-start | bytes 49160 | tf_op jit(solution)/shard_map/ppermute | solution.py:119
  193.7 1.2 collective-permute-done.25.lb_ref
  194.9 1.6 shard_map.70
  196.5 1.9 collective-permute-start.30
  198.4 4.8 %collective-permute-start.31 = (bf16[64,256]{1,0:T(8,128)(2,1)S(1)}, bf16[64,256]{1,0:T(8,128)(2,1)S(1)}, u32[]{:S(2)}, u32[]{:S(2)}) collective-permute-start(bf16[64,256]{1,0:T(8,128)(2,1)S(1)} %get-tuple-element.72), channel_id=1, source_target_pairs={{32,64},{64,32},{96,128},{128,96},{160,192},{192,160},{224,256},{2... | collective-permute-start | bytes 98312 | tf_op jit(solution)/shard_map/ppermute | solution.py:121
  203.2 1.9 collective-permute-start.28
  205.1 15.6 %collective-permute-start.29 = (bf16[64,128]{1,0:T(8,128)(2,1)S(1)}, bf16[64,128]{1,0:T(8,128)(2,1)S(1)}, u32[]{:S(2)}, u32[]{:S(2)}) collective-permute-start(bf16[64,128]{1,0:T(8,128)(2,1)S(1)} %get-tuple-element.74), channel_id=1, source_target_pairs={{0,31},{1,2},{2,1},{3,4},{4,3},{5,6},{6,5},{7,8},{8,7},{9,10},{10,... | collective-permute-start | bytes 49160 | tf_op jit(solution)/shard_map/ppermute | solution.py:119
  220.7 1.9 collective-permute-done.29
  222.6 2.2 shard_map.71
  224.8 0.8 copy-done.5
  (36 shorter events, 0.1 us)
Async XLA Ops:
  0.0 31.0 %copy-start.2 = (bf16[1,1,2048,256]{3,2,1,0:T(8,128)(2,1)S(1)}, bf16[1,1,2048,256]{3,2,1,0:T(8,128)(2,1)}, u32[]{:S(2)}) copy-start(bf16[1,1,2048,256]{3,2,1,0:T(8,128)(2,1)} %param.10) | copy-start | bytes 3145732
  0.9 30.1 %collective-permute-start.2 = (bf16[64,256]{1,0:T(8,128)(2,1)S(1)}, bf16[64,256]{1,0:T(8,128)(2,1)S(1)}, u32[]{:S(2)}, u32[]{:S(2)}) collective-permute-start(bf16[64,256]{1,0:T(8,128)(2,1)S(1)} %convert_bitcast_fusion.u_ref), channel_id=1, source_target_pairs={{0,32},{32,0},{64,96},{96,64},{128,160},{160,128},{192,224},{224,1... | collective-permute-start | bytes 98312 | tf_op jit(solution)/shard_map/ppermute | solution.py:122
  9.7 21.3 %collective-permute-start.3 = (bf16[64,256]{1,0:T(8,128)(2,1)S(1)}, bf16[64,256]{1,0:T(8,128)(2,1)S(1)}, u32[]{:S(2)}, u32[]{:S(2)}) collective-permute-start(bf16[64,256]{1,0:T(8,128)(2,1)S(1)} %convert_bitcast_fusion.u_ref), channel_id=1, source_target_pairs={{32,64},{64,32},{96,128},{128,96},{160,192},{192,160},{224,256},{2... | collective-permute-start | bytes 98312 | tf_op jit(solution)/shard_map/ppermute | solution.py:121
  11.6 19.3 %collective-permute-start = (bf16[64,128]{1,0:T(8,128)(2,1)S(1)}, bf16[64,128]{1,0:T(8,128)(2,1)S(1)}, u32[]{:S(2)}, u32[]{:S(2)}) collective-permute-start(bf16[64,128]{1,0:T(8,128)(2,1)S(1)} %get-tuple-element.92), channel_id=1, source_target_pairs={{0,1},{1,0},{2,3},{3,2},{4,5},{5,4},{6,7},{7,6},{8,9},{9,8},{10,11... | collective-permute-start | bytes 49160 | tf_op jit(solution)/shard_map/ppermute | solution.py:120
  13.6 17.4 %collective-permute-start.1 = (bf16[64,128]{1,0:T(8,128)(2,1)S(1)}, bf16[64,128]{1,0:T(8,128)(2,1)S(1)}, u32[]{:S(2)}, u32[]{:S(2)}) collective-permute-start(bf16[64,128]{1,0:T(8,128)(2,1)S(1)} %get-tuple-element.91), channel_id=1, source_target_pairs={{0,31},{1,2},{2,1},{3,4},{4,3},{5,6},{6,5},{7,8},{8,7},{9,10},{10,... | collective-permute-start | bytes 49160 | tf_op jit(solution)/shard_map/ppermute | solution.py:119
  31.0 1.6 copy-start
  32.6 1.0 copy-start.3
  33.7 0.9 copy-start.4
  34.6 27.7 %copy-start.1 = (bf16[1,1,16,4,128,128]{5,4,3,2,1,0:T(8,128)(2,1)S(1)}, bf16[1,1,16,4,128,128]{5,4,3,2,1,0:T(8,128)(2,1)}, u32[]{:S(2)}) copy-start(bf16[1,1,16,4,128,128]{5,4,3,2,1,0:T(8,128)(2,1)} %param.8) | copy-start | bytes 6291460
  36.2 26.1 %collective-permute-start.6 = (bf16[64,256]{1,0:T(8,128)(2,1)S(1)}, bf16[64,256]{1,0:T(8,128)(2,1)S(1)}, u32[]{:S(2)}, u32[]{:S(2)}) collective-permute-start(bf16[64,256]{1,0:T(8,128)(2,1)S(1)} %get-tuple-element.42.u_ref), channel_id=1, source_target_pairs={{0,32},{32,0},{64,96},{96,64},{128,160},{160,128},{192,224},{224,1... | collective-permute-start | bytes 98312 | tf_op jit(solution)/shard_map/ppermute | solution.py:122
  38.1 24.2 %collective-permute-start.7 = (bf16[64,256]{1,0:T(8,128)(2,1)S(1)}, bf16[64,256]{1,0:T(8,128)(2,1)S(1)}, u32[]{:S(2)}, u32[]{:S(2)}) collective-permute-start(bf16[64,256]{1,0:T(8,128)(2,1)S(1)} %get-tuple-element.42.u_ref), channel_id=1, source_target_pairs={{32,64},{64,32},{96,128},{128,96},{160,192},{192,160},{224,256},{2... | collective-permute-start | bytes 98312 | tf_op jit(solution)/shard_map/ppermute | solution.py:121
  43.0 17.4 %collective-permute-start.4 = (bf16[64,128]{1,0:T(8,128)(2,1)S(1)}, bf16[64,128]{1,0:T(8,128)(2,1)S(1)}, u32[]{:S(2)}, u32[]{:S(2)}) collective-permute-start(bf16[64,128]{1,0:T(8,128)(2,1)S(1)} %get-tuple-element.43), channel_id=1, source_target_pairs={{0,1},{1,0},{2,3},{3,2},{4,5},{5,4},{6,7},{7,6},{8,9},{9,8},{10,11... | collective-permute-start | bytes 49160 | tf_op jit(solution)/shard_map/ppermute | solution.py:120
  44.9 17.4 %collective-permute-start.5 = (bf16[64,128]{1,0:T(8,128)(2,1)S(1)}, bf16[64,128]{1,0:T(8,128)(2,1)S(1)}, u32[]{:S(2)}, u32[]{:S(2)}) collective-permute-start(bf16[64,128]{1,0:T(8,128)(2,1)S(1)} %get-tuple-element.44), channel_id=1, source_target_pairs={{0,31},{1,2},{2,1},{3,4},{4,3},{5,6},{6,5},{7,8},{8,7},{9,10},{10,... | collective-permute-start | bytes 49160 | tf_op jit(solution)/shard_map/ppermute | solution.py:119
  63.9 24.4 %collective-permute-start.10 = (bf16[64,256]{1,0:T(8,128)(2,1)S(1)}, bf16[64,256]{1,0:T(8,128)(2,1)S(1)}, u32[]{:S(2)}, u32[]{:S(2)}) collective-permute-start(bf16[64,256]{1,0:T(8,128)(2,1)S(1)} %get-tuple-element.47.u_ref), channel_id=1, source_target_pairs={{0,32},{32,0},{64,96},{96,64},{128,160},{160,128},{192,224},{224,1... | collective-permute-start | bytes 98312 | tf_op jit(solution)/shard_map/ppermute | solution.py:122
  65.8 22.5 %collective-permute-start.11 = (bf16[64,256]{1,0:T(8,128)(2,1)S(1)}, bf16[64,256]{1,0:T(8,128)(2,1)S(1)}, u32[]{:S(2)}, u32[]{:S(2)}) collective-permute-start(bf16[64,256]{1,0:T(8,128)(2,1)S(1)} %get-tuple-element.47.u_ref), channel_id=1, source_target_pairs={{32,64},{64,32},{96,128},{128,96},{160,192},{192,160},{224,256},{2... | collective-permute-start | bytes 98312 | tf_op jit(solution)/shard_map/ppermute | solution.py:121
  69.0 17.5 %collective-permute-start.8 = (bf16[64,128]{1,0:T(8,128)(2,1)S(1)}, bf16[64,128]{1,0:T(8,128)(2,1)S(1)}, u32[]{:S(2)}, u32[]{:S(2)}) collective-permute-start(bf16[64,128]{1,0:T(8,128)(2,1)S(1)} %get-tuple-element.48), channel_id=1, source_target_pairs={{0,1},{1,0},{2,3},{3,2},{4,5},{5,4},{6,7},{7,6},{8,9},{9,8},{10,11... | collective-permute-start | bytes 49160 | tf_op jit(solution)/shard_map/ppermute | solution.py:120
  70.9 17.4 %collective-permute-start.9 = (bf16[64,128]{1,0:T(8,128)(2,1)S(1)}, bf16[64,128]{1,0:T(8,128)(2,1)S(1)}, u32[]{:S(2)}, u32[]{:S(2)}) collective-permute-start(bf16[64,128]{1,0:T(8,128)(2,1)S(1)} %get-tuple-element.49), channel_id=1, source_target_pairs={{0,31},{1,2},{2,1},{3,4},{4,3},{5,6},{6,5},{7,8},{8,7},{9,10},{10,... | collective-permute-start | bytes 49160 | tf_op jit(solution)/shard_map/ppermute | solution.py:119
  89.9 25.4 %collective-permute-start.14 = (bf16[64,256]{1,0:T(8,128)(2,1)S(1)}, bf16[64,256]{1,0:T(8,128)(2,1)S(1)}, u32[]{:S(2)}, u32[]{:S(2)}) collective-permute-start(bf16[64,256]{1,0:T(8,128)(2,1)S(1)} %get-tuple-element.52.u_ref), channel_id=1, source_target_pairs={{0,32},{32,0},{64,96},{96,64},{128,160},{160,128},{192,224},{224,1... | collective-permute-start | bytes 98312 | tf_op jit(solution)/shard_map/ppermute | solution.py:122
  91.9 23.5 %collective-permute-start.15 = (bf16[64,256]{1,0:T(8,128)(2,1)S(1)}, bf16[64,256]{1,0:T(8,128)(2,1)S(1)}, u32[]{:S(2)}, u32[]{:S(2)}) collective-permute-start(bf16[64,256]{1,0:T(8,128)(2,1)S(1)} %get-tuple-element.52.u_ref), channel_id=1, source_target_pairs={{32,64},{64,32},{96,128},{128,96},{160,192},{192,160},{224,256},{2... | collective-permute-start | bytes 98312 | tf_op jit(solution)/shard_map/ppermute | solution.py:121
  96.0 17.4 %collective-permute-start.12 = (bf16[64,128]{1,0:T(8,128)(2,1)S(1)}, bf16[64,128]{1,0:T(8,128)(2,1)S(1)}, u32[]{:S(2)}, u32[]{:S(2)}) collective-permute-start(bf16[64,128]{1,0:T(8,128)(2,1)S(1)} %get-tuple-element.53), channel_id=1, source_target_pairs={{0,1},{1,0},{2,3},{3,2},{4,5},{5,4},{6,7},{7,6},{8,9},{9,8},{10,11... | collective-permute-start | bytes 49160 | tf_op jit(solution)/shard_map/ppermute | solution.py:120
  97.9 17.4 %collective-permute-start.13 = (bf16[64,128]{1,0:T(8,128)(2,1)S(1)}, bf16[64,128]{1,0:T(8,128)(2,1)S(1)}, u32[]{:S(2)}, u32[]{:S(2)}) collective-permute-start(bf16[64,128]{1,0:T(8,128)(2,1)S(1)} %get-tuple-element.54), channel_id=1, source_target_pairs={{0,31},{1,2},{2,1},{3,4},{4,3},{5,6},{6,5},{7,8},{8,7},{9,10},{10,... | collective-permute-start | bytes 49160 | tf_op jit(solution)/shard_map/ppermute | solution.py:119
  116.9 24.6 %collective-permute-start.18 = (bf16[64,256]{1,0:T(8,128)(2,1)S(1)}, bf16[64,256]{1,0:T(8,128)(2,1)S(1)}, u32[]{:S(2)}, u32[]{:S(2)}) collective-permute-start(bf16[64,256]{1,0:T(8,128)(2,1)S(1)} %get-tuple-element.57.u_ref), channel_id=1, source_target_pairs={{0,32},{32,0},{64,96},{96,64},{128,160},{160,128},{192,224},{224,1... | collective-permute-start | bytes 98312 | tf_op jit(solution)/shard_map/ppermute | solution.py:122
  118.9 22.7 %collective-permute-start.19 = (bf16[64,256]{1,0:T(8,128)(2,1)S(1)}, bf16[64,256]{1,0:T(8,128)(2,1)S(1)}, u32[]{:S(2)}, u32[]{:S(2)}) collective-permute-start(bf16[64,256]{1,0:T(8,128)(2,1)S(1)} %get-tuple-element.57.u_ref), channel_id=1, source_target_pairs={{32,64},{64,32},{96,128},{128,96},{160,192},{192,160},{224,256},{2... | collective-permute-start | bytes 98312 | tf_op jit(solution)/shard_map/ppermute | solution.py:121
  122.0 17.6 %collective-permute-start.16 = (bf16[64,128]{1,0:T(8,128)(2,1)S(1)}, bf16[64,128]{1,0:T(8,128)(2,1)S(1)}, u32[]{:S(2)}, u32[]{:S(2)}) collective-permute-start(bf16[64,128]{1,0:T(8,128)(2,1)S(1)} %get-tuple-element.58), channel_id=1, source_target_pairs={{0,1},{1,0},{2,3},{3,2},{4,5},{5,4},{6,7},{7,6},{8,9},{9,8},{10,11... | collective-permute-start | bytes 49160 | tf_op jit(solution)/shard_map/ppermute | solution.py:120
  124.0 17.6 %collective-permute-start.17 = (bf16[64,128]{1,0:T(8,128)(2,1)S(1)}, bf16[64,128]{1,0:T(8,128)(2,1)S(1)}, u32[]{:S(2)}, u32[]{:S(2)}) collective-permute-start(bf16[64,128]{1,0:T(8,128)(2,1)S(1)} %get-tuple-element.59), channel_id=1, source_target_pairs={{0,31},{1,2},{2,1},{3,4},{4,3},{5,6},{6,5},{7,8},{8,7},{9,10},{10,... | collective-permute-start | bytes 49160 | tf_op jit(solution)/shard_map/ppermute | solution.py:119
  143.1 25.2 %collective-permute-start.22 = (bf16[64,256]{1,0:T(8,128)(2,1)S(1)}, bf16[64,256]{1,0:T(8,128)(2,1)S(1)}, u32[]{:S(2)}, u32[]{:S(2)}) collective-permute-start(bf16[64,256]{1,0:T(8,128)(2,1)S(1)} %get-tuple-element.62.u_ref), channel_id=1, source_target_pairs={{0,32},{32,0},{64,96},{96,64},{128,160},{160,128},{192,224},{224,1... | collective-permute-start | bytes 98312 | tf_op jit(solution)/shard_map/ppermute | solution.py:122
  145.1 23.2 %collective-permute-start.23 = (bf16[64,256]{1,0:T(8,128)(2,1)S(1)}, bf16[64,256]{1,0:T(8,128)(2,1)S(1)}, u32[]{:S(2)}, u32[]{:S(2)}) collective-permute-start(bf16[64,256]{1,0:T(8,128)(2,1)S(1)} %get-tuple-element.62.u_ref), channel_id=1, source_target_pairs={{32,64},{64,32},{96,128},{128,96},{160,192},{192,160},{224,256},{2... | collective-permute-start | bytes 98312 | tf_op jit(solution)/shard_map/ppermute | solution.py:121
  148.9 17.6 %collective-permute-start.20 = (bf16[64,128]{1,0:T(8,128)(2,1)S(1)}, bf16[64,128]{1,0:T(8,128)(2,1)S(1)}, u32[]{:S(2)}, u32[]{:S(2)}) collective-permute-start(bf16[64,128]{1,0:T(8,128)(2,1)S(1)} %get-tuple-element.63), channel_id=1, source_target_pairs={{0,1},{1,0},{2,3},{3,2},{4,5},{5,4},{6,7},{7,6},{8,9},{9,8},{10,11... | collective-permute-start | bytes 49160 | tf_op jit(solution)/shard_map/ppermute | solution.py:120
  150.9 17.4 %collective-permute-start.21 = (bf16[64,128]{1,0:T(8,128)(2,1)S(1)}, bf16[64,128]{1,0:T(8,128)(2,1)S(1)}, u32[]{:S(2)}, u32[]{:S(2)}) collective-permute-start(bf16[64,128]{1,0:T(8,128)(2,1)S(1)} %get-tuple-element.64), channel_id=1, source_target_pairs={{0,31},{1,2},{2,1},{3,4},{4,3},{5,6},{6,5},{7,8},{8,7},{9,10},{10,... | collective-permute-start | bytes 49160 | tf_op jit(solution)/shard_map/ppermute | solution.py:119
  169.9 25.0 %collective-permute-start.26 = (bf16[64,256]{1,0:T(8,128)(2,1)S(1)}, bf16[64,256]{1,0:T(8,128)(2,1)S(1)}, u32[]{:S(2)}, u32[]{:S(2)}) collective-permute-start(bf16[64,256]{1,0:T(8,128)(2,1)S(1)} %get-tuple-element.67.u_ref), channel_id=1, source_target_pairs={{0,32},{32,0},{64,96},{96,64},{128,160},{160,128},{192,224},{224,1... | collective-permute-start | bytes 98312 | tf_op jit(solution)/shard_map/ppermute | solution.py:122
  171.8 23.1 %collective-permute-start.27 = (bf16[64,256]{1,0:T(8,128)(2,1)S(1)}, bf16[64,256]{1,0:T(8,128)(2,1)S(1)}, u32[]{:S(2)}, u32[]{:S(2)}) collective-permute-start(bf16[64,256]{1,0:T(8,128)(2,1)S(1)} %get-tuple-element.67.u_ref), channel_id=1, source_target_pairs={{32,64},{64,32},{96,128},{128,96},{160,192},{192,160},{224,256},{2... | collective-permute-start | bytes 98312 | tf_op jit(solution)/shard_map/ppermute | solution.py:121
  175.5 18.2 %collective-permute-start.24 = (bf16[64,128]{1,0:T(8,128)(2,1)S(1)}, bf16[64,128]{1,0:T(8,128)(2,1)S(1)}, u32[]{:S(2)}, u32[]{:S(2)}) collective-permute-start(bf16[64,128]{1,0:T(8,128)(2,1)S(1)} %get-tuple-element.68), channel_id=1, source_target_pairs={{0,1},{1,0},{2,3},{3,2},{4,5},{5,4},{6,7},{7,6},{8,9},{9,8},{10,11... | collective-permute-start | bytes 49160 | tf_op jit(solution)/shard_map/ppermute | solution.py:120
  177.4 17.5 %collective-permute-start.25 = (bf16[64,128]{1,0:T(8,128)(2,1)S(1)}, bf16[64,128]{1,0:T(8,128)(2,1)S(1)}, u32[]{:S(2)}, u32[]{:S(2)}) collective-permute-start(bf16[64,128]{1,0:T(8,128)(2,1)S(1)} %get-tuple-element.69), channel_id=1, source_target_pairs={{0,31},{1,2},{2,1},{3,4},{4,3},{5,6},{6,5},{7,8},{8,7},{9,10},{10,... | collective-permute-start | bytes 49160 | tf_op jit(solution)/shard_map/ppermute | solution.py:119
  196.5 26.1 %collective-permute-start.30 = (bf16[64,256]{1,0:T(8,128)(2,1)S(1)}, bf16[64,256]{1,0:T(8,128)(2,1)S(1)}, u32[]{:S(2)}, u32[]{:S(2)}) collective-permute-start(bf16[64,256]{1,0:T(8,128)(2,1)S(1)} %get-tuple-element.72), channel_id=1, source_target_pairs={{0,32},{32,0},{64,96},{96,64},{128,160},{160,128},{192,224},{224,1... | collective-permute-start | bytes 98312 | tf_op jit(solution)/shard_map/ppermute | solution.py:122
  198.4 24.2 %collective-permute-start.31 = (bf16[64,256]{1,0:T(8,128)(2,1)S(1)}, bf16[64,256]{1,0:T(8,128)(2,1)S(1)}, u32[]{:S(2)}, u32[]{:S(2)}) collective-permute-start(bf16[64,256]{1,0:T(8,128)(2,1)S(1)} %get-tuple-element.72), channel_id=1, source_target_pairs={{32,64},{64,32},{96,128},{128,96},{160,192},{192,160},{224,256},{2... | collective-permute-start | bytes 98312 | tf_op jit(solution)/shard_map/ppermute | solution.py:121
  203.2 17.5 %collective-permute-start.28 = (bf16[64,128]{1,0:T(8,128)(2,1)S(1)}, bf16[64,128]{1,0:T(8,128)(2,1)S(1)}, u32[]{:S(2)}, u32[]{:S(2)}) collective-permute-start(bf16[64,128]{1,0:T(8,128)(2,1)S(1)} %get-tuple-element.73), channel_id=1, source_target_pairs={{0,1},{1,0},{2,3},{3,2},{4,5},{5,4},{6,7},{7,6},{8,9},{9,8},{10,11... | collective-permute-start | bytes 49160 | tf_op jit(solution)/shard_map/ppermute | solution.py:120
  205.1 17.5 %collective-permute-start.29 = (bf16[64,128]{1,0:T(8,128)(2,1)S(1)}, bf16[64,128]{1,0:T(8,128)(2,1)S(1)}, u32[]{:S(2)}, u32[]{:S(2)}) collective-permute-start(bf16[64,128]{1,0:T(8,128)(2,1)S(1)} %get-tuple-element.74), channel_id=1, source_target_pairs={{0,31},{1,2},{2,1},{3,4},{4,3},{5,6},{6,5},{7,8},{8,7},{9,10},{10,... | collective-permute-start | bytes 49160 | tf_op jit(solution)/shard_map/ppermute | solution.py:119
  224.8 0.8 copy-start.5

commit v4 on v3

--- a/solution.py
+++ b/solution.py
@@ -11,6 +11,7 @@
 OV = 4
 STEPS = 8
 PTS = 8
+IN_BLOCKS = 6
 
 
 def selector(slot_list):
@@ -20,29 +21,42 @@
     return full.reshape(PTS * VARS, OV * VARS)
 
 
-def step_kernel(flag_ref, u_ref, la_ref, lb_ref, ta_ref, tb_ref, sn_ref, ss_ref, r_ref, c_ref, win_ref, ro_ref,
+def couple_kernel(u_ref, r_ref, c_ref, win_ref, acc_out):
+    res_blocks, links, breadth, _ = c_ref.shape
+    u = u_ref[...]
+    own = u.shape[1] // breadth
+    r = r_ref[...]
+    for b in range(res_blocks):
+        acc = jnp.zeros((r.shape[0], breadth), jnp.float32)
+        if b % IN_BLOCKS < own:
+            j = b % IN_BLOCKS
+            acc = jnp.dot(u[:, j * breadth:(j + 1) * breadth], win_ref[b], preferred_element_type=jnp.float32)
+        for k in range(links):
+            blk = (b + k) % res_blocks
+            acc = acc + jnp.dot(r[:, blk * breadth:(blk + 1) * breadth], c_ref[b, k],
+                                preferred_element_type=jnp.float32)
+        acc_out[:, b * breadth:(b + 1) * breadth] = acc
+
+
+def step_kernel(flag_ref, acc_ref, la_ref, lb_ref, ta_ref, tb_ref, sn_ref, ss_ref, win_ref, ro_ref,
                 f_out, u_out, sa_out, sb_out, r_out, feat_scr):
     members, half = sa_out.shape
-    res_blocks, links, breadth, _ = c_ref.shape
+    res_blocks, breadth, _ = win_ref.shape
     lon_even = jnp.broadcast_to(flag_ref[0], (members, half)) == 1
     lat_even = jnp.broadcast_to(flag_ref[1], ta_ref.shape) == 1
     west = jnp.where(lon_even, lb_ref[...], la_ref[...])
     east = jnp.where(lon_even, la_ref[...], lb_ref[...])
     north_src = jnp.where(lat_even, tb_ref[...], ta_ref[...])
     south_src = jnp.where(lat_even, ta_ref[...], tb_ref[...])
-    u = u_ref[...]
     north = jnp.dot(north_src, sn_ref[...], preferred_element_type=jnp.float32).astype(jnp.bfloat16)
     south = jnp.dot(south_src, ss_ref[...], preferred_element_type=jnp.float32).astype(jnp.bfloat16)
-    pieces = [u[:, j * breadth:(j + 1) * breadth] for j in range(u.shape[1] // breadth)]
-    pieces += [west, east, north, south]
-    r = r_ref[...]
+    pieces = [west, east, north, south]
+    own = IN_BLOCKS - len(pieces)
     even = lax.broadcasted_iota(jnp.int32, (members, breadth), 1) % 2 == 0
     for b in range(res_blocks):
-        acc = jnp.dot(pieces[b % len(pieces)], win_ref[b], preferred_element_type=jnp.float32)
-        for k in range(links):
-            blk = (b + k) % res_blocks
-            acc = acc + jnp.dot(r[:, blk * breadth:(blk + 1) * breadth], c_ref[b, k],
-                                preferred_element_type=jnp.float32)
+        acc = acc_ref[:, b * breadth:(b + 1) * breadth]
+        if b % IN_BLOCKS >= own:
+            acc = acc + jnp.dot(pieces[b % IN_BLOCKS - own], win_ref[b], preferred_element_type=jnp.float32)
         rb = jnp.tanh(acc).astype(jnp.bfloat16)
         r_out[:, b * breadth:(b + 1) * breadth] = rb
         wide = rb.astype(jnp.float32)
@@ -57,11 +71,24 @@
     sb_out[...] = jnp.where(lon_even, lo, hi)
 
 
-def step_call(flags, u, lon_a, lon_b, lat_a, lat_b, sel_n, sel_s, reservoir, block_weight, entry_weight, read_weight):
-    members, feats = u.shape
-    nodes = reservoir.shape[1]
+VMEM_SPEC = pl.BlockSpec(memory_space=pltpu.MemorySpace.VMEM)
+
+
+def couple_call(u, reservoir, block_weight, entry_weight):
+    members, nodes = reservoir.shape
+    return pl.pallas_call(
+        couple_kernel,
+        out_shape=jax.ShapeDtypeStruct((members, nodes), jnp.float32),
+        in_specs=[VMEM_SPEC] * 4,
+        out_specs=VMEM_SPEC,
+        compiler_params=pltpu.CompilerParams(vmem_limit_bytes=32 * 1024 * 1024),
+    )(u, reservoir, block_weight, entry_weight)
+
+
+def step_call(flags, acc, lon_a, lon_b, lat_a, lat_b, sel_n, sel_s, entry_weight, read_weight):
+    members, nodes = acc.shape
+    feats = read_weight.shape[1]
     half = feats // LONC
-    spec = pl.BlockSpec(memory_space=pltpu.MemorySpace.VMEM)
     out_shape = (
         jax.ShapeDtypeStruct((members, feats), jnp.float32),
         jax.ShapeDtypeStruct((members, feats), jnp.bfloat16),
@@ -72,11 +99,11 @@
     return pl.pallas_call(
         step_kernel,
         out_shape=out_shape,
-        in_specs=[pl.BlockSpec(memory_space=pltpu.MemorySpace.SMEM)] + [spec] * 11,
-        out_specs=tuple([spec] * 5),
+        in_specs=[pl.BlockSpec(memory_space=pltpu.MemorySpace.SMEM)] + [VMEM_SPEC] * 9,
+        out_specs=tuple([VMEM_SPEC] * 5),
         scratch_shapes=[pltpu.VMEM((members, nodes), jnp.bfloat16)],
         compiler_params=pltpu.CompilerParams(vmem_limit_bytes=32 * 1024 * 1024),
-    )(flags, u, lon_a, lon_b, lat_a, lat_b, sel_n, sel_s, reservoir, block_weight, entry_weight, read_weight)
+    )(flags, acc, lon_a, lon_b, lat_a, lat_b, sel_n, sel_s, entry_weight, read_weight)
 
 
 def swaps(peers, odd_first, wrap):
@@ -120,9 +147,9 @@
         lon_a = lax.ppermute(send_a, "lon", lon_pairs_a)
         lat_b = lax.ppermute(rounded, "lat", lat_pairs_b)
         lat_a = lax.ppermute(rounded, "lat", lat_pairs_a)
+        acc = couple_call(rounded, reservoir, block_weight, entry_weight)
         current, rounded, send_a, send_b, reservoir = step_call(
-            flags, rounded, lon_a, lon_b, lat_a, lat_b, sel_n, sel_s,
-            reservoir, block_weight, entry_weight, read_weight)
+            flags, acc, lon_a, lon_b, lat_a, lat_b, sel_n, sel_s, entry_weight, read_weight)
         outputs.append(current)
     return jnp.stack(outputs)[:, None, None]
 

time: 227 us -> 227 us (level)
  starting transfers between devices: 193 us -> 144 us
  waiting for transfers between devices: 12.5 us -> 58 us
  Pallas kernels: 11 us -> 13.7 us
    ppermute x8, starting transfers between devices: 126 us -> 74.2 us  [per_device(): lon_b = lax.ppermute(send_b, 'lon', lon_pairs_b)]
    ppermute x8, waiting for transfers between devices: 12.4 us -> 58 us  [per_device(): lon_b = lax.ppermute(send_b, 'lon', lon_pairs_b)]
    pallas_call x0 -> x8, Pallas kernels: none -> 5.81 us  [couple_call(): pl.pallas_call(couple_kernel, out_shape=jax.ShapeDtypeStruct((members, no...]
    pallas_call x7, Pallas kernels: 11 us -> 7.89 us  [step_call(): pl.pallas_call(step_kernel, out_shape=out_shape, in_specs=[pl.BlockSpec(m...]
    unnamed x19 -> x21, local copies, waits for them, and re-layouts: 4.42 us -> 4.88 us
  transfers between devices with their start and end apart: 32 -> 32, of which waited for: 7 -> 7; matrix products, arithmetic and copies ran while one was open for 1% -> 1% of each run, Pallas kernels for 0% -> 3%
where the time goes in v4:
time: 227 us; the launch traced here: 225 us
  starting transfers between devices  144 us (63%)
  waiting for transfers between devices  58 us (26%)
  Pallas kernels  13.7 us (6%)
  local copies, waits for them, and re-layouts  7.72 us (3%)
    ppermute x8, starting transfers between devices, per_device(): lon_b = lax.ppermute(send_b, 'lon', lon_pairs_b)  74.2 us
    ppermute x8, waiting for transfers between devices, per_device(): lon_b = lax.ppermute(send_b, 'lon', lon_pairs_b)  58 us
    ppermute x8, starting transfers between devices, per_device(): lat_b = lax.ppermute(rounded, 'lat', lat_pairs_b)  30.8 us
    ppermute x8, starting transfers between devices, per_device(): lat_a = lax.ppermute(rounded, 'lat', lat_pairs_a)  22.2 us
    ppermute x8, starting transfers between devices, per_device(): lon_a = lax.ppermute(send_a, 'lon', lon_pairs_a)  17.1 us
    pallas_call x7, Pallas kernels, step_call(): pl.pallas_call(step_kernel, out_shape=out_shape, in_specs=[pl.BlockSpec(m...  7.89 us
    pallas_call x8, Pallas kernels, couple_call(): pl.pallas_call(couple_kernel, out_shape=jax.ShapeDtypeStruct((members, no...  5.81 us
    unnamed x21, local copies, waits for them, and re-layouts  4.88 us
  transfers between devices with their start and end apart: 32, of which 7 were waited for; matrix products, arithmetic and copies ran while one was open for 1% of the time, Pallas kernels for 3%

profile of v4, /device:TPU:1, one launch (start us, length us, event | category | flops | bytes accessed | tf_op | source)
XLA Modules:
  0.0 225.4 jit_solution(4176435394035148794)
XLA Ops:
  0.0 0.8 convert_bitcast_fusion.u_ref
  0.8 8.7 %collective-permute-start.2 = (bf16[64,256]{1,0:T(8,128)(2,1)S(1)}, bf16[64,256]{1,0:T(8,128)(2,1)S(1)}, u32[]{:S(2)}, u32[]{:S(2)}) collective-permute-start(bf16[64,256]{1,0:T(8,128)(2,1)S(1)} %convert_bitcast_fusion.u_ref), channel_id=1, source_target_pairs={{0,32},{32,0},{64,96},{96,64},{128,160},{160,128},{192,224},{224,1... | collective-permute-start | bytes 98312 | tf_op jit(solution)/shard_map/ppermute | solution.py:149
  9.6 1.9 collective-permute-start.3
  11.5 15.4 %collective-permute-start.1 = (bf16[64,128]{1,0:T(8,128)(2,1)S(1)}, bf16[64,128]{1,0:T(8,128)(2,1)S(1)}, u32[]{:S(2)}, u32[]{:S(2)}) collective-permute-start(bf16[64,128]{1,0:T(8,128)(2,1)S(1)} %get-tuple-element.91), channel_id=1, source_target_pairs={{0,31},{1,2},{2,1},{3,4},{4,3},{5,6},{6,5},{7,8},{8,7},{9,10},{10,... | collective-permute-start | bytes 49160 | tf_op jit(solution)/shard_map/ppermute | solution.py:146
  26.9 1.9 collective-permute-start
  28.9 0.8 slice_bitcast_fusion
  29.6 0.3 broadcast_multiply_fusion
  30.2 0.2 mul.37.sn_ref
  30.4 1.6 copy-done
  32.0 1.0 copy-done.2
  33.0 0.9 copy-done.5
  34.0 0.7 shard_map.64.acc_ref
  34.7 0.4 copy-done.4
  35.2 1.1 shard_map.65
  36.3 3.3 %collective-permute-start.7 = (bf16[64,256]{1,0:T(8,128)(2,1)S(1)}, bf16[64,256]{1,0:T(8,128)(2,1)S(1)}, u32[]{:S(2)}, u32[]{:S(2)}) collective-permute-start(bf16[64,256]{1,0:T(8,128)(2,1)S(1)} %get-tuple-element.42.u_ref), channel_id=1, source_target_pairs={{32,64},{64,32},{96,128},{128,96},{160,192},{192,160},{224,256},{2... | collective-permute-start | bytes 98312 | tf_op jit(solution)/shard_map/ppermute | solution.py:148
  39.6 1.9 collective-permute-start.6
  41.5 3.6 %collective-permute-start.4 = (bf16[64,128]{1,0:T(8,128)(2,1)S(1)}, bf16[64,128]{1,0:T(8,128)(2,1)S(1)}, u32[]{:S(2)}, u32[]{:S(2)}) collective-permute-start(bf16[64,128]{1,0:T(8,128)(2,1)S(1)} %get-tuple-element.44), channel_id=1, source_target_pairs={{0,1},{1,0},{2,3},{3,2},{4,5},{5,4},{6,7},{7,6},{8,9},{9,8},{10,11... | collective-permute-start | bytes 49160 | tf_op jit(solution)/shard_map/ppermute | solution.py:147
  45.2 8.6 %collective-permute-start.5 = (bf16[64,128]{1,0:T(8,128)(2,1)S(1)}, bf16[64,128]{1,0:T(8,128)(2,1)S(1)}, u32[]{:S(2)}, u32[]{:S(2)}) collective-permute-start(bf16[64,128]{1,0:T(8,128)(2,1)S(1)} %get-tuple-element.45), channel_id=1, source_target_pairs={{0,31},{1,2},{2,1},{3,4},{4,3},{5,6},{6,5},{7,8},{8,7},{9,10},{10,... | collective-permute-start | bytes 49160 | tf_op jit(solution)/shard_map/ppermute | solution.py:146
  53.8 0.7 shard_map.66.acc_ref
  54.5 8.2 %collective-permute-done.5.lb_ref = bf16[64,128]{1,0:T(8,128)(2,1)S(1)} collective-permute-done((bf16[64,128]{1,0:T(8,128)(2,1)S(1)}, bf16[64,128]{1,0:T(8,128)(2,1)S(1)}, u32[]{:S(2)}, u32[]{:S(2)}) %collective-permute-start.5) | collective-permute-done | bytes 16416 | tf_op jit(solution)/shard_map/ppermute | solution.py:146
  62.8 1.1 shard_map.67
  63.9 4.3 %collective-permute-start.11 = (bf16[64,256]{1,0:T(8,128)(2,1)S(1)}, bf16[64,256]{1,0:T(8,128)(2,1)S(1)}, u32[]{:S(2)}, u32[]{:S(2)}) collective-permute-start(bf16[64,256]{1,0:T(8,128)(2,1)S(1)} %get-tuple-element.47.u_ref), channel_id=1, source_target_pairs={{32,64},{64,32},{96,128},{128,96},{160,192},{192,160},{224,256},{2... | collective-permute-start | bytes 98312 | tf_op jit(solution)/shard_map/ppermute | solution.py:148
  68.2 1.9 collective-permute-start.10
  70.1 1.9 collective-permute-start.8
  72.1 8.2 %collective-permute-start.9 = (bf16[64,128]{1,0:T(8,128)(2,1)S(1)}, bf16[64,128]{1,0:T(8,128)(2,1)S(1)}, u32[]{:S(2)}, u32[]{:S(2)}) collective-permute-start(bf16[64,128]{1,0:T(8,128)(2,1)S(1)} %get-tuple-element.50), channel_id=1, source_target_pairs={{0,31},{1,2},{2,1},{3,4},{4,3},{5,6},{6,5},{7,8},{8,7},{9,10},{10,... | collective-permute-start | bytes 49160 | tf_op jit(solution)/shard_map/ppermute | solution.py:146
  80.3 0.7 shard_map.68.acc_ref
  81.0 8.5 %collective-permute-done.9.lb_ref = bf16[64,128]{1,0:T(8,128)(2,1)S(1)} collective-permute-done((bf16[64,128]{1,0:T(8,128)(2,1)S(1)}, bf16[64,128]{1,0:T(8,128)(2,1)S(1)}, u32[]{:S(2)}, u32[]{:S(2)}) %collective-permute-start.9) | collective-permute-done | bytes 16416 | tf_op jit(solution)/shard_map/ppermute | solution.py:146
  89.5 1.1 shard_map.69
  90.6 4.2 %collective-permute-start.15 = (bf16[64,256]{1,0:T(8,128)(2,1)S(1)}, bf16[64,256]{1,0:T(8,128)(2,1)S(1)}, u32[]{:S(2)}, u32[]{:S(2)}) collective-permute-start(bf16[64,256]{1,0:T(8,128)(2,1)S(1)} %get-tuple-element.52.u_ref), channel_id=1, source_target_pairs={{32,64},{64,32},{96,128},{128,96},{160,192},{192,160},{224,256},{2... | collective-permute-start | bytes 98312 | tf_op jit(solution)/shard_map/ppermute | solution.py:148
  94.8 1.9 collective-permute-start.14
  96.7 1.9 collective-permute-start.12
  98.7 8.6 %collective-permute-start.13 = (bf16[64,128]{1,0:T(8,128)(2,1)S(1)}, bf16[64,128]{1,0:T(8,128)(2,1)S(1)}, u32[]{:S(2)}, u32[]{:S(2)}) collective-permute-start(bf16[64,128]{1,0:T(8,128)(2,1)S(1)} %get-tuple-element.55), channel_id=1, source_target_pairs={{0,31},{1,2},{2,1},{3,4},{4,3},{5,6},{6,5},{7,8},{8,7},{9,10},{10,... | collective-permute-start | bytes 49160 | tf_op jit(solution)/shard_map/ppermute | solution.py:146
  107.3 0.7 shard_map.70.acc_ref
  108.0 8.1 %collective-permute-done.13.lb_ref = bf16[64,128]{1,0:T(8,128)(2,1)S(1)} collective-permute-done((bf16[64,128]{1,0:T(8,128)(2,1)S(1)}, bf16[64,128]{1,0:T(8,128)(2,1)S(1)}, u32[]{:S(2)}, u32[]{:S(2)}) %collective-permute-start.13) | collective-permute-done | bytes 16416 | tf_op jit(solution)/shard_map/ppermute | solution.py:146
  116.1 1.1 shard_map.71
  117.2 5.7 %collective-permute-start.19 = (bf16[64,256]{1,0:T(8,128)(2,1)S(1)}, bf16[64,256]{1,0:T(8,128)(2,1)S(1)}, u32[]{:S(2)}, u32[]{:S(2)}) collective-permute-start(bf16[64,256]{1,0:T(8,128)(2,1)S(1)} %get-tuple-element.57.u_ref), channel_id=1, source_target_pairs={{32,64},{64,32},{96,128},{128,96},{160,192},{192,160},{224,256},{2... | collective-permute-start | bytes 98312 | tf_op jit(solution)/shard_map/ppermute | solution.py:148
  122.9 1.9 collective-permute-start.18
  124.9 1.9 collective-permute-start.16
  126.8 8.1 %collective-permute-start.17 = (bf16[64,128]{1,0:T(8,128)(2,1)S(1)}, bf16[64,128]{1,0:T(8,128)(2,1)S(1)}, u32[]{:S(2)}, u32[]{:S(2)}) collective-permute-start(bf16[64,128]{1,0:T(8,128)(2,1)S(1)} %get-tuple-element.60), channel_id=1, source_target_pairs={{0,31},{1,2},{2,1},{3,4},{4,3},{5,6},{6,5},{7,8},{8,7},{9,10},{10,... | collective-permute-start | bytes 49160 | tf_op jit(solution)/shard_map/ppermute | solution.py:146
  135.0 0.7 shard_map.72.acc_ref
  135.7 8.5 %collective-permute-done.17.lb_ref = bf16[64,128]{1,0:T(8,128)(2,1)S(1)} collective-permute-done((bf16[64,128]{1,0:T(8,128)(2,1)S(1)}, bf16[64,128]{1,0:T(8,128)(2,1)S(1)}, u32[]{:S(2)}, u32[]{:S(2)}) %collective-permute-start.17) | collective-permute-done | bytes 16416 | tf_op jit(solution)/shard_map/ppermute | solution.py:146
  144.2 1.1 shard_map.73
  145.4 3.3 %collective-permute-start.23 = (bf16[64,256]{1,0:T(8,128)(2,1)S(1)}, bf16[64,256]{1,0:T(8,128)(2,1)S(1)}, u32[]{:S(2)}, u32[]{:S(2)}) collective-permute-start(bf16[64,256]{1,0:T(8,128)(2,1)S(1)} %get-tuple-element.62.u_ref), channel_id=1, source_target_pairs={{32,64},{64,32},{96,128},{128,96},{160,192},{192,160},{224,256},{2... | collective-permute-start | bytes 98312 | tf_op jit(solution)/shard_map/ppermute | solution.py:148
  148.7 1.9 collective-permute-start.22
  150.6 1.9 collective-permute-start.20
  152.5 8.4 %collective-permute-start.21 = (bf16[64,128]{1,0:T(8,128)(2,1)S(1)}, bf16[64,128]{1,0:T(8,128)(2,1)S(1)}, u32[]{:S(2)}, u32[]{:S(2)}) collective-permute-start(bf16[64,128]{1,0:T(8,128)(2,1)S(1)} %get-tuple-element.65), channel_id=1, source_target_pairs={{0,31},{1,2},{2,1},{3,4},{4,3},{5,6},{6,5},{7,8},{8,7},{9,10},{10,... | collective-permute-start | bytes 49160 | tf_op jit(solution)/shard_map/ppermute | solution.py:146
  160.9 0.7 shard_map.74.acc_ref
  161.7 8.3 %collective-permute-done.21.lb_ref = bf16[64,128]{1,0:T(8,128)(2,1)S(1)} collective-permute-done((bf16[64,128]{1,0:T(8,128)(2,1)S(1)}, bf16[64,128]{1,0:T(8,128)(2,1)S(1)}, u32[]{:S(2)}, u32[]{:S(2)}) %collective-permute-start.21) | collective-permute-done | bytes 16416 | tf_op jit(solution)/shard_map/ppermute | solution.py:146
  169.9 1.1 shard_map.75
  171.1 4.3 %collective-permute-start.27 = (bf16[64,256]{1,0:T(8,128)(2,1)S(1)}, bf16[64,256]{1,0:T(8,128)(2,1)S(1)}, u32[]{:S(2)}, u32[]{:S(2)}) collective-permute-start(bf16[64,256]{1,0:T(8,128)(2,1)S(1)} %get-tuple-element.67.u_ref), channel_id=1, source_target_pairs={{32,64},{64,32},{96,128},{128,96},{160,192},{192,160},{224,256},{2... | collective-permute-start | bytes 98312 | tf_op jit(solution)/shard_map/ppermute | solution.py:148
  175.4 1.9 collective-permute-start.26
  177.3 1.9 collective-permute-start.24
  179.3 8.6 %collective-permute-start.25 = (bf16[64,128]{1,0:T(8,128)(2,1)S(1)}, bf16[64,128]{1,0:T(8,128)(2,1)S(1)}, u32[]{:S(2)}, u32[]{:S(2)}) collective-permute-start(bf16[64,128]{1,0:T(8,128)(2,1)S(1)} %get-tuple-element.70), channel_id=1, source_target_pairs={{0,31},{1,2},{2,1},{3,4},{4,3},{5,6},{6,5},{7,8},{8,7},{9,10},{10,... | collective-permute-start | bytes 49160 | tf_op jit(solution)/shard_map/ppermute | solution.py:146
  187.9 0.7 shard_map.76.acc_ref
  188.6 8.1 %collective-permute-done.25.lb_ref = bf16[64,128]{1,0:T(8,128)(2,1)S(1)} collective-permute-done((bf16[64,128]{1,0:T(8,128)(2,1)S(1)}, bf16[64,128]{1,0:T(8,128)(2,1)S(1)}, u32[]{:S(2)}, u32[]{:S(2)}) %collective-permute-start.25) | collective-permute-done | bytes 16416 | tf_op jit(solution)/shard_map/ppermute | solution.py:146
  196.7 1.1 shard_map.77
  197.8 3.8 %collective-permute-start.31 = (bf16[64,256]{1,0:T(8,128)(2,1)S(1)}, bf16[64,256]{1,0:T(8,128)(2,1)S(1)}, u32[]{:S(2)}, u32[]{:S(2)}) collective-permute-start(bf16[64,256]{1,0:T(8,128)(2,1)S(1)} %get-tuple-element.72.u_ref), channel_id=1, source_target_pairs={{32,64},{64,32},{96,128},{128,96},{160,192},{192,160},{224,256},{2... | collective-permute-start | bytes 98312 | tf_op jit(solution)/shard_map/ppermute | solution.py:148
  201.6 1.9 collective-permute-start.30
  203.6 1.9 collective-permute-start.28
  205.5 8.3 %collective-permute-start.29 = (bf16[64,128]{1,0:T(8,128)(2,1)S(1)}, bf16[64,128]{1,0:T(8,128)(2,1)S(1)}, u32[]{:S(2)}, u32[]{:S(2)}) collective-permute-start(bf16[64,128]{1,0:T(8,128)(2,1)S(1)} %get-tuple-element.75), channel_id=1, source_target_pairs={{0,31},{1,2},{2,1},{3,4},{4,3},{5,6},{6,5},{7,8},{8,7},{9,10},{10,... | collective-permute-start | bytes 49160 | tf_op jit(solution)/shard_map/ppermute | solution.py:146
  213.8 0.7 shard_map.78
  214.6 8.3 %collective-permute-done.29 = bf16[64,128]{1,0:T(8,128)(2,1)S(1)} collective-permute-done((bf16[64,128]{1,0:T(8,128)(2,1)S(1)}, bf16[64,128]{1,0:T(8,128)(2,1)S(1)}, u32[]{:S(2)}, u32[]{:S(2)}) %collective-permute-start.29) | collective-permute-done | bytes 16416 | tf_op jit(solution)/shard_map/ppermute | solution.py:146
  222.9 1.7 shard_map.79
  224.7 0.8 copy-done.6
  (46 shorter events, 0.4 us)
Async XLA Ops:
  0.8 33.9 %collective-permute-start.2 = (bf16[64,256]{1,0:T(8,128)(2,1)S(1)}, bf16[64,256]{1,0:T(8,128)(2,1)S(1)}, u32[]{:S(2)}, u32[]{:S(2)}) collective-permute-start(bf16[64,256]{1,0:T(8,128)(2,1)S(1)} %convert_bitcast_fusion.u_ref), channel_id=1, source_target_pairs={{0,32},{32,0},{64,96},{96,64},{128,160},{160,128},{192,224},{224,1... | collective-permute-start | bytes 98312 | tf_op jit(solution)/shard_map/ppermute | solution.py:149
  9.6 25.1 %collective-permute-start.3 = (bf16[64,256]{1,0:T(8,128)(2,1)S(1)}, bf16[64,256]{1,0:T(8,128)(2,1)S(1)}, u32[]{:S(2)}, u32[]{:S(2)}) collective-permute-start(bf16[64,256]{1,0:T(8,128)(2,1)S(1)} %convert_bitcast_fusion.u_ref), channel_id=1, source_target_pairs={{32,64},{64,32},{96,128},{128,96},{160,192},{192,160},{224,256},{2... | collective-permute-start | bytes 98312 | tf_op jit(solution)/shard_map/ppermute | solution.py:148
  11.5 23.1 %collective-permute-start.1 = (bf16[64,128]{1,0:T(8,128)(2,1)S(1)}, bf16[64,128]{1,0:T(8,128)(2,1)S(1)}, u32[]{:S(2)}, u32[]{:S(2)}) collective-permute-start(bf16[64,128]{1,0:T(8,128)(2,1)S(1)} %get-tuple-element.91), channel_id=1, source_target_pairs={{0,31},{1,2},{2,1},{3,4},{4,3},{5,6},{6,5},{7,8},{8,7},{9,10},{10,... | collective-permute-start | bytes 49160 | tf_op jit(solution)/shard_map/ppermute | solution.py:146
  26.9 7.8 %collective-permute-start = (bf16[64,128]{1,0:T(8,128)(2,1)S(1)}, bf16[64,128]{1,0:T(8,128)(2,1)S(1)}, u32[]{:S(2)}, u32[]{:S(2)}) collective-permute-start(bf16[64,128]{1,0:T(8,128)(2,1)S(1)} %get-tuple-element.92), channel_id=1, source_target_pairs={{0,1},{1,0},{2,3},{3,2},{4,5},{5,4},{6,7},{7,6},{8,9},{9,8},{10,11... | collective-permute-start | bytes 49160 | tf_op jit(solution)/shard_map/ppermute | solution.py:147
  29.9 4.8 %copy-start.3 = (bf16[1,1,16,128,128]{4,3,2,1,0:T(8,128)(2,1)S(1)}, bf16[1,1,16,128,128]{4,3,2,1,0:T(8,128)(2,1)}, u32[]{:S(2)}) copy-start(bf16[1,1,16,128,128]{4,3,2,1,0:T(8,128)(2,1)} %param.9) | copy-start | bytes 1572868
  30.4 1.6 copy-start
  32.0 1.0 copy-start.2
  33.0 0.9 copy-start.5
  33.9 1.2 copy-start.4
  34.0 19.9 %copy-start.1 = (bf16[1,1,16,4,128,128]{5,4,3,2,1,0:T(8,128)(2,1)S(1)}, bf16[1,1,16,4,128,128]{5,4,3,2,1,0:T(8,128)(2,1)}, u32[]{:S(2)}) copy-start(bf16[1,1,16,4,128,128]{5,4,3,2,1,0:T(8,128)(2,1)} %param.8) | copy-start | bytes 6291460
  36.3 26.5 %collective-permute-start.7 = (bf16[64,256]{1,0:T(8,128)(2,1)S(1)}, bf16[64,256]{1,0:T(8,128)(2,1)S(1)}, u32[]{:S(2)}, u32[]{:S(2)}) collective-permute-start(bf16[64,256]{1,0:T(8,128)(2,1)S(1)} %get-tuple-element.42.u_ref), channel_id=1, source_target_pairs={{32,64},{64,32},{96,128},{128,96},{160,192},{192,160},{224,256},{2... | collective-permute-start | bytes 98312 | tf_op jit(solution)/shard_map/ppermute | solution.py:148
  39.6 23.2 %collective-permute-start.6 = (bf16[64,256]{1,0:T(8,128)(2,1)S(1)}, bf16[64,256]{1,0:T(8,128)(2,1)S(1)}, u32[]{:S(2)}, u32[]{:S(2)}) collective-permute-start(bf16[64,256]{1,0:T(8,128)(2,1)S(1)} %get-tuple-element.42.u_ref), channel_id=1, source_target_pairs={{0,32},{32,0},{64,96},{96,64},{128,160},{160,128},{192,224},{224,1... | collective-permute-start | bytes 98312 | tf_op jit(solution)/shard_map/ppermute | solution.py:149
  41.5 13.0 %collective-permute-start.4 = (bf16[64,128]{1,0:T(8,128)(2,1)S(1)}, bf16[64,128]{1,0:T(8,128)(2,1)S(1)}, u32[]{:S(2)}, u32[]{:S(2)}) collective-permute-start(bf16[64,128]{1,0:T(8,128)(2,1)S(1)} %get-tuple-element.44), channel_id=1, source_target_pairs={{0,1},{1,0},{2,3},{3,2},{4,5},{5,4},{6,7},{7,6},{8,9},{9,8},{10,11... | collective-permute-start | bytes 49160 | tf_op jit(solution)/shard_map/ppermute | solution.py:147
  45.2 17.6 %collective-permute-start.5 = (bf16[64,128]{1,0:T(8,128)(2,1)S(1)}, bf16[64,128]{1,0:T(8,128)(2,1)S(1)}, u32[]{:S(2)}, u32[]{:S(2)}) collective-permute-start(bf16[64,128]{1,0:T(8,128)(2,1)S(1)} %get-tuple-element.45), channel_id=1, source_target_pairs={{0,31},{1,2},{2,1},{3,4},{4,3},{5,6},{6,5},{7,8},{8,7},{9,10},{10,... | collective-permute-start | bytes 49160 | tf_op jit(solution)/shard_map/ppermute | solution.py:146
  63.9 25.6 %collective-permute-start.11 = (bf16[64,256]{1,0:T(8,128)(2,1)S(1)}, bf16[64,256]{1,0:T(8,128)(2,1)S(1)}, u32[]{:S(2)}, u32[]{:S(2)}) collective-permute-start(bf16[64,256]{1,0:T(8,128)(2,1)S(1)} %get-tuple-element.47.u_ref), channel_id=1, source_target_pairs={{32,64},{64,32},{96,128},{128,96},{160,192},{192,160},{224,256},{2... | collective-permute-start | bytes 98312 | tf_op jit(solution)/shard_map/ppermute | solution.py:148
  68.2 21.3 %collective-permute-start.10 = (bf16[64,256]{1,0:T(8,128)(2,1)S(1)}, bf16[64,256]{1,0:T(8,128)(2,1)S(1)}, u32[]{:S(2)}, u32[]{:S(2)}) collective-permute-start(bf16[64,256]{1,0:T(8,128)(2,1)S(1)} %get-tuple-element.47.u_ref), channel_id=1, source_target_pairs={{0,32},{32,0},{64,96},{96,64},{128,160},{160,128},{192,224},{224,1... | collective-permute-start | bytes 98312 | tf_op jit(solution)/shard_map/ppermute | solution.py:149
  70.1 10.9 %collective-permute-start.8 = (bf16[64,128]{1,0:T(8,128)(2,1)S(1)}, bf16[64,128]{1,0:T(8,128)(2,1)S(1)}, u32[]{:S(2)}, u32[]{:S(2)}) collective-permute-start(bf16[64,128]{1,0:T(8,128)(2,1)S(1)} %get-tuple-element.49), channel_id=1, source_target_pairs={{0,1},{1,0},{2,3},{3,2},{4,5},{5,4},{6,7},{7,6},{8,9},{9,8},{10,11... | collective-permute-start | bytes 49160 | tf_op jit(solution)/shard_map/ppermute | solution.py:147
  72.1 17.4 %collective-permute-start.9 = (bf16[64,128]{1,0:T(8,128)(2,1)S(1)}, bf16[64,128]{1,0:T(8,128)(2,1)S(1)}, u32[]{:S(2)}, u32[]{:S(2)}) collective-permute-start(bf16[64,128]{1,0:T(8,128)(2,1)S(1)} %get-tuple-element.50), channel_id=1, source_target_pairs={{0,31},{1,2},{2,1},{3,4},{4,3},{5,6},{6,5},{7,8},{8,7},{9,10},{10,... | collective-permute-start | bytes 49160 | tf_op jit(solution)/shard_map/ppermute | solution.py:146
  90.6 25.5 %collective-permute-start.15 = (bf16[64,256]{1,0:T(8,128)(2,1)S(1)}, bf16[64,256]{1,0:T(8,128)(2,1)S(1)}, u32[]{:S(2)}, u32[]{:S(2)}) collective-permute-start(bf16[64,256]{1,0:T(8,128)(2,1)S(1)} %get-tuple-element.52.u_ref), channel_id=1, source_target_pairs={{32,64},{64,32},{96,128},{128,96},{160,192},{192,160},{224,256},{2... | collective-permute-start | bytes 98312 | tf_op jit(solution)/shard_map/ppermute | solution.py:148
  94.8 21.3 %collective-permute-start.14 = (bf16[64,256]{1,0:T(8,128)(2,1)S(1)}, bf16[64,256]{1,0:T(8,128)(2,1)S(1)}, u32[]{:S(2)}, u32[]{:S(2)}) collective-permute-start(bf16[64,256]{1,0:T(8,128)(2,1)S(1)} %get-tuple-element.52.u_ref), channel_id=1, source_target_pairs={{0,32},{32,0},{64,96},{96,64},{128,160},{160,128},{192,224},{224,1... | collective-permute-start | bytes 98312 | tf_op jit(solution)/shard_map/ppermute | solution.py:149
  96.7 11.3 %collective-permute-start.12 = (bf16[64,128]{1,0:T(8,128)(2,1)S(1)}, bf16[64,128]{1,0:T(8,128)(2,1)S(1)}, u32[]{:S(2)}, u32[]{:S(2)}) collective-permute-start(bf16[64,128]{1,0:T(8,128)(2,1)S(1)} %get-tuple-element.54), channel_id=1, source_target_pairs={{0,1},{1,0},{2,3},{3,2},{4,5},{5,4},{6,7},{7,6},{8,9},{9,8},{10,11... | collective-permute-start | bytes 49160 | tf_op jit(solution)/shard_map/ppermute | solution.py:147
  98.7 17.4 %collective-permute-start.13 = (bf16[64,128]{1,0:T(8,128)(2,1)S(1)}, bf16[64,128]{1,0:T(8,128)(2,1)S(1)}, u32[]{:S(2)}, u32[]{:S(2)}) collective-permute-start(bf16[64,128]{1,0:T(8,128)(2,1)S(1)} %get-tuple-element.55), channel_id=1, source_target_pairs={{0,31},{1,2},{2,1},{3,4},{4,3},{5,6},{6,5},{7,8},{8,7},{9,10},{10,... | collective-permute-start | bytes 49160 | tf_op jit(solution)/shard_map/ppermute | solution.py:146
  117.2 27.0 %collective-permute-start.19 = (bf16[64,256]{1,0:T(8,128)(2,1)S(1)}, bf16[64,256]{1,0:T(8,128)(2,1)S(1)}, u32[]{:S(2)}, u32[]{:S(2)}) collective-permute-start(bf16[64,256]{1,0:T(8,128)(2,1)S(1)} %get-tuple-element.57.u_ref), channel_id=1, source_target_pairs={{32,64},{64,32},{96,128},{128,96},{160,192},{192,160},{224,256},{2... | collective-permute-start | bytes 98312 | tf_op jit(solution)/shard_map/ppermute | solution.py:148
  122.9 21.3 %collective-permute-start.18 = (bf16[64,256]{1,0:T(8,128)(2,1)S(1)}, bf16[64,256]{1,0:T(8,128)(2,1)S(1)}, u32[]{:S(2)}, u32[]{:S(2)}) collective-permute-start(bf16[64,256]{1,0:T(8,128)(2,1)S(1)} %get-tuple-element.57.u_ref), channel_id=1, source_target_pairs={{0,32},{32,0},{64,96},{96,64},{128,160},{160,128},{192,224},{224,1... | collective-permute-start | bytes 98312 | tf_op jit(solution)/shard_map/ppermute | solution.py:149
  124.9 10.8 %collective-permute-start.16 = (bf16[64,128]{1,0:T(8,128)(2,1)S(1)}, bf16[64,128]{1,0:T(8,128)(2,1)S(1)}, u32[]{:S(2)}, u32[]{:S(2)}) collective-permute-start(bf16[64,128]{1,0:T(8,128)(2,1)S(1)} %get-tuple-element.59), channel_id=1, source_target_pairs={{0,1},{1,0},{2,3},{3,2},{4,5},{5,4},{6,7},{7,6},{8,9},{9,8},{10,11... | collective-permute-start | bytes 49160 | tf_op jit(solution)/shard_map/ppermute | solution.py:147
  126.8 17.4 %collective-permute-start.17 = (bf16[64,128]{1,0:T(8,128)(2,1)S(1)}, bf16[64,128]{1,0:T(8,128)(2,1)S(1)}, u32[]{:S(2)}, u32[]{:S(2)}) collective-permute-start(bf16[64,128]{1,0:T(8,128)(2,1)S(1)} %get-tuple-element.60), channel_id=1, source_target_pairs={{0,31},{1,2},{2,1},{3,4},{4,3},{5,6},{6,5},{7,8},{8,7},{9,10},{10,... | collective-permute-start | bytes 49160 | tf_op jit(solution)/shard_map/ppermute | solution.py:146
  145.4 24.6 %collective-permute-start.23 = (bf16[64,256]{1,0:T(8,128)(2,1)S(1)}, bf16[64,256]{1,0:T(8,128)(2,1)S(1)}, u32[]{:S(2)}, u32[]{:S(2)}) collective-permute-start(bf16[64,256]{1,0:T(8,128)(2,1)S(1)} %get-tuple-element.62.u_ref), channel_id=1, source_target_pairs={{32,64},{64,32},{96,128},{128,96},{160,192},{192,160},{224,256},{2... | collective-permute-start | bytes 98312 | tf_op jit(solution)/shard_map/ppermute | solution.py:148
  148.7 21.3 %collective-permute-start.22 = (bf16[64,256]{1,0:T(8,128)(2,1)S(1)}, bf16[64,256]{1,0:T(8,128)(2,1)S(1)}, u32[]{:S(2)}, u32[]{:S(2)}) collective-permute-start(bf16[64,256]{1,0:T(8,128)(2,1)S(1)} %get-tuple-element.62.u_ref), channel_id=1, source_target_pairs={{0,32},{32,0},{64,96},{96,64},{128,160},{160,128},{192,224},{224,1... | collective-permute-start | bytes 98312 | tf_op jit(solution)/shard_map/ppermute | solution.py:149
  150.6 11.1 %collective-permute-start.20 = (bf16[64,128]{1,0:T(8,128)(2,1)S(1)}, bf16[64,128]{1,0:T(8,128)(2,1)S(1)}, u32[]{:S(2)}, u32[]{:S(2)}) collective-permute-start(bf16[64,128]{1,0:T(8,128)(2,1)S(1)} %get-tuple-element.64), channel_id=1, source_target_pairs={{0,1},{1,0},{2,3},{3,2},{4,5},{5,4},{6,7},{7,6},{8,9},{9,8},{10,11... | collective-permute-start | bytes 49160 | tf_op jit(solution)/shard_map/ppermute | solution.py:147
  152.5 17.4 %collective-permute-start.21 = (bf16[64,128]{1,0:T(8,128)(2,1)S(1)}, bf16[64,128]{1,0:T(8,128)(2,1)S(1)}, u32[]{:S(2)}, u32[]{:S(2)}) collective-permute-start(bf16[64,128]{1,0:T(8,128)(2,1)S(1)} %get-tuple-element.65), channel_id=1, source_target_pairs={{0,31},{1,2},{2,1},{3,4},{4,3},{5,6},{6,5},{7,8},{8,7},{9,10},{10,... | collective-permute-start | bytes 49160 | tf_op jit(solution)/shard_map/ppermute | solution.py:146
  171.1 25.6 %collective-permute-start.27 = (bf16[64,256]{1,0:T(8,128)(2,1)S(1)}, bf16[64,256]{1,0:T(8,128)(2,1)S(1)}, u32[]{:S(2)}, u32[]{:S(2)}) collective-permute-start(bf16[64,256]{1,0:T(8,128)(2,1)S(1)} %get-tuple-element.67.u_ref), channel_id=1, source_target_pairs={{32,64},{64,32},{96,128},{128,96},{160,192},{192,160},{224,256},{2... | collective-permute-start | bytes 98312 | tf_op jit(solution)/shard_map/ppermute | solution.py:148
  175.4 21.3 %collective-permute-start.26 = (bf16[64,256]{1,0:T(8,128)(2,1)S(1)}, bf16[64,256]{1,0:T(8,128)(2,1)S(1)}, u32[]{:S(2)}, u32[]{:S(2)}) collective-permute-start(bf16[64,256]{1,0:T(8,128)(2,1)S(1)} %get-tuple-element.67.u_ref), channel_id=1, source_target_pairs={{0,32},{32,0},{64,96},{96,64},{128,160},{160,128},{192,224},{224,1... | collective-permute-start | bytes 98312 | tf_op jit(solution)/shard_map/ppermute | solution.py:149
  177.3 11.3 %collective-permute-start.24 = (bf16[64,128]{1,0:T(8,128)(2,1)S(1)}, bf16[64,128]{1,0:T(8,128)(2,1)S(1)}, u32[]{:S(2)}, u32[]{:S(2)}) collective-permute-start(bf16[64,128]{1,0:T(8,128)(2,1)S(1)} %get-tuple-element.69), channel_id=1, source_target_pairs={{0,1},{1,0},{2,3},{3,2},{4,5},{5,4},{6,7},{7,6},{8,9},{9,8},{10,11... | collective-permute-start | bytes 49160 | tf_op jit(solution)/shard_map/ppermute | solution.py:147
  179.3 17.4 %collective-permute-start.25 = (bf16[64,128]{1,0:T(8,128)(2,1)S(1)}, bf16[64,128]{1,0:T(8,128)(2,1)S(1)}, u32[]{:S(2)}, u32[]{:S(2)}) collective-permute-start(bf16[64,128]{1,0:T(8,128)(2,1)S(1)} %get-tuple-element.70), channel_id=1, source_target_pairs={{0,31},{1,2},{2,1},{3,4},{4,3},{5,6},{6,5},{7,8},{8,7},{9,10},{10,... | collective-permute-start | bytes 49160 | tf_op jit(solution)/shard_map/ppermute | solution.py:146
  197.8 25.1 %collective-permute-start.31 = (bf16[64,256]{1,0:T(8,128)(2,1)S(1)}, bf16[64,256]{1,0:T(8,128)(2,1)S(1)}, u32[]{:S(2)}, u32[]{:S(2)}) collective-permute-start(bf16[64,256]{1,0:T(8,128)(2,1)S(1)} %get-tuple-element.72.u_ref), channel_id=1, source_target_pairs={{32,64},{64,32},{96,128},{128,96},{160,192},{192,160},{224,256},{2... | collective-permute-start | bytes 98312 | tf_op jit(solution)/shard_map/ppermute | solution.py:148
  201.6 21.3 %collective-permute-start.30 = (bf16[64,256]{1,0:T(8,128)(2,1)S(1)}, bf16[64,256]{1,0:T(8,128)(2,1)S(1)}, u32[]{:S(2)}, u32[]{:S(2)}) collective-permute-start(bf16[64,256]{1,0:T(8,128)(2,1)S(1)} %get-tuple-element.72.u_ref), channel_id=1, source_target_pairs={{0,32},{32,0},{64,96},{96,64},{128,160},{160,128},{192,224},{224,1... | collective-permute-start | bytes 98312 | tf_op jit(solution)/shard_map/ppermute | solution.py:149
  203.6 11.0 %collective-permute-start.28 = (bf16[64,128]{1,0:T(8,128)(2,1)S(1)}, bf16[64,128]{1,0:T(8,128)(2,1)S(1)}, u32[]{:S(2)}, u32[]{:S(2)}) collective-permute-start(bf16[64,128]{1,0:T(8,128)(2,1)S(1)} %get-tuple-element.74), channel_id=1, source_target_pairs={{0,1},{1,0},{2,3},{3,2},{4,5},{5,4},{6,7},{7,6},{8,9},{9,8},{10,11... | collective-permute-start | bytes 49160 | tf_op jit(solution)/shard_map/ppermute | solution.py:147
  205.5 17.4 %collective-permute-start.29 = (bf16[64,128]{1,0:T(8,128)(2,1)S(1)}, bf16[64,128]{1,0:T(8,128)(2,1)S(1)}, u32[]{:S(2)}, u32[]{:S(2)}) collective-permute-start(bf16[64,128]{1,0:T(8,128)(2,1)S(1)} %get-tuple-element.75), channel_id=1, source_target_pairs={{0,31},{1,2},{2,1},{3,4},{4,3},{5,6},{6,5},{7,8},{8,7},{9,10},{10,... | collective-permute-start | bytes 49160 | tf_op jit(solution)/shard_map/ppermute | solution.py:146
  224.7 0.8 copy-start.6

commit v5 on v3

--- a/solution.py
+++ b/solution.py
@@ -11,6 +11,7 @@
 OV = 4
 STEPS = 8
 PTS = 8
+IN_BLOCKS = 6
 
 
 def selector(slot_list):
@@ -20,34 +21,82 @@
     return full.reshape(PTS * VARS, OV * VARS)
 
 
-def step_kernel(flag_ref, u_ref, la_ref, lb_ref, ta_ref, tb_ref, sn_ref, ss_ref, r_ref, c_ref, win_ref, ro_ref,
-                f_out, u_out, sa_out, sb_out, r_out, feat_scr):
-    members, half = sa_out.shape
+def lon_blocks(res_blocks):
+    return [b for b in range(res_blocks) if b % IN_BLOCKS in (2, 3)]
+
+
+def spans(blocks):
+    runs = []
+    for b in blocks:
+        if runs and runs[-1][0] + runs[-1][1] == b:
+            runs[-1] = (runs[-1][0], runs[-1][1] + 1)
+        else:
+            runs.append((b, 1))
+    return runs
+
+
+def couple_kernel(flag_ref, u_ref, ta_ref, tb_ref, sn_ref, ss_ref, r_ref, c_ref, win_ref, ro_ref,
+                  acc_out, r_out, f_out, feat_scr):
     res_blocks, links, breadth, _ = c_ref.shape
-    lon_even = jnp.broadcast_to(flag_ref[0], (members, half)) == 1
+    members = r_ref.shape[0]
     lat_even = jnp.broadcast_to(flag_ref[1], ta_ref.shape) == 1
-    west = jnp.where(lon_even, lb_ref[...], la_ref[...])
-    east = jnp.where(lon_even, la_ref[...], lb_ref[...])
     north_src = jnp.where(lat_even, tb_ref[...], ta_ref[...])
     south_src = jnp.where(lat_even, ta_ref[...], tb_ref[...])
-    u = u_ref[...]
     north = jnp.dot(north_src, sn_ref[...], preferred_element_type=jnp.float32).astype(jnp.bfloat16)
     south = jnp.dot(south_src, ss_ref[...], preferred_element_type=jnp.float32).astype(jnp.bfloat16)
-    pieces = [u[:, j * breadth:(j + 1) * breadth] for j in range(u.shape[1] // breadth)]
-    pieces += [west, east, north, south]
+    u = u_ref[...]
+    pieces = {0: u[:, :breadth], 1: u[:, breadth:2 * breadth], 4: north, 5: south}
     r = r_ref[...]
     even = lax.broadcasted_iota(jnp.int32, (members, breadth), 1) % 2 == 0
+    later = lon_blocks(res_blocks)
     for b in range(res_blocks):
-        acc = jnp.dot(pieces[b % len(pieces)], win_ref[b], preferred_element_type=jnp.float32)
+        acc = jnp.zeros((members, breadth), jnp.float32)
+        if b % IN_BLOCKS in pieces:
+            acc = jnp.dot(pieces[b % IN_BLOCKS], win_ref[b], preferred_element_type=jnp.float32)
         for k in range(links):
             blk = (b + k) % res_blocks
             acc = acc + jnp.dot(r[:, blk * breadth:(blk + 1) * breadth], c_ref[b, k],
                                 preferred_element_type=jnp.float32)
+        if b in later:
+            i = later.index(b)
+            acc_out[:, i * breadth:(i + 1) * breadth] = acc
+        else:
+            rb = jnp.tanh(acc).astype(jnp.bfloat16)
+            r_out[:, b * breadth:(b + 1) * breadth] = rb
+            wide = rb.astype(jnp.float32)
+            feat_scr[:, b * breadth:(b + 1) * breadth] = jnp.where(even, wide * wide, wide).astype(jnp.bfloat16)
+    f = jnp.zeros(f_out.shape, jnp.float32)
+    for first, count in spans([b for b in range(res_blocks) if b not in later]):
+        rows = slice(first * breadth, (first + count) * breadth)
+        f = f + jnp.dot(feat_scr[:, rows], ro_ref[rows, :], preferred_element_type=jnp.float32)
+    f_out[...] = f
+
+
+def step_kernel(flag_ref, acc_ref, la_ref, lb_ref, win_ref, ro_ref, rp_ref, fp_ref,
+                f_out, u_out, sa_out, sb_out, r_out, feat_scr):
+    members, half = sa_out.shape
+    res_blocks, breadth, _ = win_ref.shape
+    lon_even = jnp.broadcast_to(flag_ref[0], (members, half)) == 1
+    west = jnp.where(lon_even, lb_ref[...], la_ref[...])
+    east = jnp.where(lon_even, la_ref[...], lb_ref[...])
+    pieces = {2: west, 3: east}
+    even = lax.broadcasted_iota(jnp.int32, (members, breadth), 1) % 2 == 0
+    later = lon_blocks(res_blocks)
+    r_out[...] = rp_ref[...]
+    for i, b in enumerate(later):
+        acc = acc_ref[:, i * breadth:(i + 1) * breadth]
+        acc = acc + jnp.dot(pieces[b % IN_BLOCKS], win_ref[b], preferred_element_type=jnp.float32)
         rb = jnp.tanh(acc).astype(jnp.bfloat16)
         r_out[:, b * breadth:(b + 1) * breadth] = rb
         wide = rb.astype(jnp.float32)
-        feat_scr[:, b * breadth:(b + 1) * breadth] = jnp.where(even, wide * wide, wide).astype(jnp.bfloat16)
-    f = jnp.dot(feat_scr[...], ro_ref[...], preferred_element_type=jnp.float32)
+        feat_scr[:, i * breadth:(i + 1) * breadth] = jnp.where(even, wide * wide, wide).astype(jnp.bfloat16)
+    f = fp_ref[...]
+    done = 0
+    for first, count in spans(later):
+        rows = slice(first * breadth, (first + count) * breadth)
+        f = f + jnp.dot(feat_scr[:, done * breadth:(done + count) * breadth], ro_ref[rows, :],
+                        preferred_element_type=jnp.float32)
+        done += count
     f_out[...] = f
     ub = f.astype(jnp.bfloat16)
     u_out[...] = ub
@@ -57,11 +106,34 @@
     sb_out[...] = jnp.where(lon_even, lo, hi)
 
 
-def step_call(flags, u, lon_a, lon_b, lat_a, lat_b, sel_n, sel_s, reservoir, block_weight, entry_weight, read_weight):
-    members, feats = u.shape
-    nodes = reservoir.shape[1]
+VMEM_SPEC = pl.BlockSpec(memory_space=pltpu.MemorySpace.VMEM)
+SMEM_SPEC = pl.BlockSpec(memory_space=pltpu.MemorySpace.SMEM)
+PARAMS = pltpu.CompilerParams(vmem_limit_bytes=32 * 1024 * 1024)
+
+
+def couple_call(flags, u, lat_a, lat_b, sel_n, sel_s, reservoir, block_weight, entry_weight, read_weight):
+    members, nodes = reservoir.shape
+    breadth = block_weight.shape[2]
+    later = len(lon_blocks(block_weight.shape[0]))
+    out_shape = (
+        jax.ShapeDtypeStruct((members, later * breadth), jnp.float32),
+        jax.ShapeDtypeStruct((members, nodes), jnp.bfloat16),
+        jax.ShapeDtypeStruct((members, read_weight.shape[1]), jnp.float32),
+    )
+    return pl.pallas_call(
+        couple_kernel,
+        out_shape=out_shape,
+        in_specs=[SMEM_SPEC] + [VMEM_SPEC] * 9,
+        out_specs=tuple([VMEM_SPEC] * 3),
+        scratch_shapes=[pltpu.VMEM((members, nodes), jnp.bfloat16)],
+        compiler_params=PARAMS,
+    )(flags, u, lat_a, lat_b, sel_n, sel_s, reservoir, block_weight, entry_weight, read_weight)
+
+
+def step_call(flags, acc, lon_a, lon_b, entry_weight, read_weight, r_part, f_part):
+    members, nodes = r_part.shape
+    feats = read_weight.shape[1]
     half = feats // LONC
-    spec = pl.BlockSpec(memory_space=pltpu.MemorySpace.VMEM)
     out_shape = (
         jax.ShapeDtypeStruct((members, feats), jnp.float32),
         jax.ShapeDtypeStruct((members, feats), jnp.bfloat16),
@@ -72,11 +144,11 @@
     return pl.pallas_call(
         step_kernel,
         out_shape=out_shape,
-        in_specs=[pl.BlockSpec(memory_space=pltpu.MemorySpace.SMEM)] + [spec] * 11,
-        out_specs=tuple([spec] * 5),
-        scratch_shapes=[pltpu.VMEM((members, nodes), jnp.bfloat16)],
-        compiler_params=pltpu.CompilerParams(vmem_limit_bytes=32 * 1024 * 1024),
-    )(flags, u, lon_a, lon_b, lat_a, lat_b, sel_n, sel_s, reservoir, block_weight, entry_weight, read_weight)
+        in_specs=[SMEM_SPEC] + [VMEM_SPEC] * 7,
+        out_specs=tuple([VMEM_SPEC] * 5),
+        scratch_shapes=[pltpu.VMEM(acc.shape, jnp.bfloat16)],
+        compiler_params=PARAMS,
+    )(flags, acc, lon_a, lon_b, entry_weight, read_weight, r_part, f_part)
 
 
 def swaps(peers, odd_first, wrap):
@@ -120,9 +192,10 @@
         lon_a = lax.ppermute(send_a, "lon", lon_pairs_a)
         lat_b = lax.ppermute(rounded, "lat", lat_pairs_b)
         lat_a = lax.ppermute(rounded, "lat", lat_pairs_a)
+        acc, r_part, f_part = couple_call(flags, rounded, lat_a, lat_b, sel_n, sel_s,
+                                          reservoir, block_weight, entry_weight, read_weight)
         current, rounded, send_a, send_b, reservoir = step_call(
-            flags, rounded, lon_a, lon_b, lat_a, lat_b, sel_n, sel_s,
-            reservoir, block_weight, entry_weight, read_weight)
+            flags, acc, lon_a, lon_b, entry_weight, read_weight, r_part, f_part)
         outputs.append(current)
     return jnp.stack(outputs)[:, None, None]
 

time: 227 us -> 222 us (0.978)
  starting transfers between devices: 193 us -> 163 us
  waiting for transfers between devices: 12.5 us -> 31.2 us
  Pallas kernels: 11 us -> 18.1 us
    ppermute x8, starting transfers between devices: 126 us -> 96.7 us  [per_device(): lon_b = lax.ppermute(send_b, 'lon', lon_pairs_b)]
    ppermute x8, waiting for transfers between devices: 12.4 us -> 31.1 us  [per_device(): lon_b = lax.ppermute(send_b, 'lon', lon_pairs_b)]
    pallas_call x7 -> x15, Pallas kernels: 11 us -> 18.1 us  [the longest x8 11.7 us: couple_call(): pl.pallas_call(couple_kernel, out_shape=out_shape, in_specs=[SMEM_SPEC] +...]
  transfers between devices with their start and end apart: 32 -> 32, of which waited for: 7 -> 7; matrix products, arithmetic and copies ran while one was open for 1% -> 1% of each run, Pallas kernels for 0% -> 5%
where the time goes in v5:
time: 222 us; the launch traced here: 221 us
  starting transfers between devices  163 us (73%)
  waiting for transfers between devices  31.2 us (14%)
  Pallas kernels  18.1 us (8%)
  local copies, waits for them, and re-layouts  7.07 us (3%)
    ppermute x8, starting transfers between devices, per_device(): lon_b = lax.ppermute(send_b, 'lon', lon_pairs_b)  96.7 us
    ppermute x8, waiting for transfers between devices, per_device(): lon_b = lax.ppermute(send_b, 'lon', lon_pairs_b)  31.1 us
    ppermute x8, starting transfers between devices, per_device(): lat_b = lax.ppermute(rounded, 'lat', lat_pairs_b)  28.3 us
    ppermute x8, starting transfers between devices, per_device(): lat_a = lax.ppermute(rounded, 'lat', lat_pairs_a)  22.2 us
    ppermute x8, starting transfers between devices, per_device(): lon_a = lax.ppermute(send_a, 'lon', lon_pairs_a)  15.4 us
    pallas_call x8, Pallas kernels, couple_call(): pl.pallas_call(couple_kernel, out_shape=out_shape, in_specs=[SMEM_SPEC] +...  11.7 us
    pallas_call x7, Pallas kernels, step_call(): pl.pallas_call(step_kernel, out_shape=out_shape, in_specs=[SMEM_SPEC] + [...  6.45 us
  transfers between devices with their start and end apart: 32, of which 7 were waited for; matrix products, arithmetic and copies ran while one was open for 1% of the time, Pallas kernels for 5%

profile of v5, /device:TPU:1, one launch (start us, length us, event | category | flops | bytes accessed | tf_op | source)
XLA Modules:
  0.0 220.9 jit_solution(7821719672636351158)
XLA Ops:
  0.0 0.9 convert_bitcast_fusion.u_ref
  0.9 8.7 %collective-permute-start = (bf16[64,256]{1,0:T(8,128)(2,1)S(1)}, bf16[64,256]{1,0:T(8,128)(2,1)S(1)}, u32[]{:S(2)}, u32[]{:S(2)}) collective-permute-start(bf16[64,256]{1,0:T(8,128)(2,1)S(1)} %convert_bitcast_fusion.u_ref), channel_id=1, source_target_pairs={{0,32},{32,0},{64,96},{96,64},{128,160},{160,128},{192,224},{224,1... | collective-permute-start | bytes 98312 | tf_op jit(solution)/shard_map/ppermute | solution.py:194
  9.7 1.9 collective-permute-start.1
  11.6 1.9 collective-permute-start.2
  13.6 15.9 %collective-permute-start.3 = (bf16[64,128]{1,0:T(8,128)(2,1)S(1)}, bf16[64,128]{1,0:T(8,128)(2,1)S(1)}, u32[]{:S(2)}, u32[]{:S(2)}) collective-permute-start(bf16[64,128]{1,0:T(8,128)(2,1)S(1)} %get-tuple-element.139), channel_id=1, source_target_pairs={{0,31},{1,2},{2,1},{3,4},{4,3},{5,6},{6,5},{7,8},{8,7},{9,10},{10,... | collective-permute-start | bytes 49160 | tf_op jit(solution)/shard_map/ppermute | solution.py:191
  29.5 0.8 slice_bitcast_fusion
  30.3 0.3 broadcast_multiply_fusion
  30.6 0.2 mul.37.sn_ref
  30.8 0.2 mul.40.ss_ref
  31.0 1.0 copy-done.1
  32.1 1.6 copy-done.2
  33.6 0.9 copy-done.4
  34.6 1.5 shard_map.64
  36.1 0.9 shard_map.65
  37.0 1.9 collective-permute-start.4
  38.9 3.6 %collective-permute-start.5 = (bf16[64,256]{1,0:T(8,128)(2,1)S(1)}, bf16[64,256]{1,0:T(8,128)(2,1)S(1)}, u32[]{:S(2)}, u32[]{:S(2)}) collective-permute-start(bf16[64,256]{1,0:T(8,128)(2,1)S(1)} %get-tuple-element.69.u_ref), channel_id=1, source_target_pairs={{32,64},{64,32},{96,128},{128,96},{160,192},{192,160},{224,256},{2... | collective-permute-start | bytes 98312 | tf_op jit(solution)/shard_map/ppermute | solution.py:193
  42.5 1.9 collective-permute-start.6
  44.5 11.7 %collective-permute-start.7 = (bf16[64,128]{1,0:T(8,128)(2,1)S(1)}, bf16[64,128]{1,0:T(8,128)(2,1)S(1)}, u32[]{:S(2)}, u32[]{:S(2)}) collective-permute-start(bf16[64,128]{1,0:T(8,128)(2,1)S(1)} %get-tuple-element.73), channel_id=1, source_target_pairs={{0,31},{1,2},{2,1},{3,4},{4,3},{5,6},{6,5},{7,8},{8,7},{9,10},{10,... | collective-permute-start | bytes 49160 | tf_op jit(solution)/shard_map/ppermute | solution.py:191
  56.2 1.5 shard_map.66
  57.6 4.4 %collective-permute-done.7.lb_ref = bf16[64,128]{1,0:T(8,128)(2,1)S(1)} collective-permute-done((bf16[64,128]{1,0:T(8,128)(2,1)S(1)}, bf16[64,128]{1,0:T(8,128)(2,1)S(1)}, u32[]{:S(2)}, u32[]{:S(2)}) %collective-permute-start.7) | collective-permute-done | bytes 16416 | tf_op jit(solution)/shard_map/ppermute | solution.py:191
  62.0 0.9 shard_map.67
  62.9 1.9 collective-permute-start.8
  64.9 3.2 %collective-permute-start.9 = (bf16[64,256]{1,0:T(8,128)(2,1)S(1)}, bf16[64,256]{1,0:T(8,128)(2,1)S(1)}, u32[]{:S(2)}, u32[]{:S(2)}) collective-permute-start(bf16[64,256]{1,0:T(8,128)(2,1)S(1)} %get-tuple-element.77.u_ref), channel_id=1, source_target_pairs={{32,64},{64,32},{96,128},{128,96},{160,192},{192,160},{224,256},{2... | collective-permute-start | bytes 98312 | tf_op jit(solution)/shard_map/ppermute | solution.py:193
  68.1 1.9 collective-permute-start.10
  70.0 11.5 %collective-permute-start.11 = (bf16[64,128]{1,0:T(8,128)(2,1)S(1)}, bf16[64,128]{1,0:T(8,128)(2,1)S(1)}, u32[]{:S(2)}, u32[]{:S(2)}) collective-permute-start(bf16[64,128]{1,0:T(8,128)(2,1)S(1)} %get-tuple-element.81), channel_id=1, source_target_pairs={{0,31},{1,2},{2,1},{3,4},{4,3},{5,6},{6,5},{7,8},{8,7},{9,10},{10,... | collective-permute-start | bytes 49160 | tf_op jit(solution)/shard_map/ppermute | solution.py:191
  81.6 1.5 shard_map.68
  83.0 4.4 %collective-permute-done.11.lb_ref = bf16[64,128]{1,0:T(8,128)(2,1)S(1)} collective-permute-done((bf16[64,128]{1,0:T(8,128)(2,1)S(1)}, bf16[64,128]{1,0:T(8,128)(2,1)S(1)}, u32[]{:S(2)}, u32[]{:S(2)}) %collective-permute-start.11) | collective-permute-done | bytes 16416 | tf_op jit(solution)/shard_map/ppermute | solution.py:191
  87.4 0.9 shard_map.69
  88.3 1.9 collective-permute-start.12
  90.3 4.1 %collective-permute-start.13 = (bf16[64,256]{1,0:T(8,128)(2,1)S(1)}, bf16[64,256]{1,0:T(8,128)(2,1)S(1)}, u32[]{:S(2)}, u32[]{:S(2)}) collective-permute-start(bf16[64,256]{1,0:T(8,128)(2,1)S(1)} %get-tuple-element.85.u_ref), channel_id=1, source_target_pairs={{32,64},{64,32},{96,128},{128,96},{160,192},{192,160},{224,256},{2... | collective-permute-start | bytes 98312 | tf_op jit(solution)/shard_map/ppermute | solution.py:193
  94.4 1.9 collective-permute-start.14
  96.3 11.6 %collective-permute-start.15 = (bf16[64,128]{1,0:T(8,128)(2,1)S(1)}, bf16[64,128]{1,0:T(8,128)(2,1)S(1)}, u32[]{:S(2)}, u32[]{:S(2)}) collective-permute-start(bf16[64,128]{1,0:T(8,128)(2,1)S(1)} %get-tuple-element.89), channel_id=1, source_target_pairs={{0,31},{1,2},{2,1},{3,4},{4,3},{5,6},{6,5},{7,8},{8,7},{9,10},{10,... | collective-permute-start | bytes 49160 | tf_op jit(solution)/shard_map/ppermute | solution.py:191
  107.9 1.5 shard_map.70
  109.4 4.4 %collective-permute-done.15.lb_ref = bf16[64,128]{1,0:T(8,128)(2,1)S(1)} collective-permute-done((bf16[64,128]{1,0:T(8,128)(2,1)S(1)}, bf16[64,128]{1,0:T(8,128)(2,1)S(1)}, u32[]{:S(2)}, u32[]{:S(2)}) %collective-permute-start.15) | collective-permute-done | bytes 16416 | tf_op jit(solution)/shard_map/ppermute | solution.py:191
  113.8 0.9 shard_map.71
  114.7 1.9 collective-permute-start.16
  116.6 3.4 %collective-permute-start.17 = (bf16[64,256]{1,0:T(8,128)(2,1)S(1)}, bf16[64,256]{1,0:T(8,128)(2,1)S(1)}, u32[]{:S(2)}, u32[]{:S(2)}) collective-permute-start(bf16[64,256]{1,0:T(8,128)(2,1)S(1)} %get-tuple-element.93.u_ref), channel_id=1, source_target_pairs={{32,64},{64,32},{96,128},{128,96},{160,192},{192,160},{224,256},{2... | collective-permute-start | bytes 98312 | tf_op jit(solution)/shard_map/ppermute | solution.py:193
  120.0 1.9 collective-permute-start.18
  121.9 11.4 %collective-permute-start.19 = (bf16[64,128]{1,0:T(8,128)(2,1)S(1)}, bf16[64,128]{1,0:T(8,128)(2,1)S(1)}, u32[]{:S(2)}, u32[]{:S(2)}) collective-permute-start(bf16[64,128]{1,0:T(8,128)(2,1)S(1)} %get-tuple-element.97), channel_id=1, source_target_pairs={{0,31},{1,2},{2,1},{3,4},{4,3},{5,6},{6,5},{7,8},{8,7},{9,10},{10,... | collective-permute-start | bytes 49160 | tf_op jit(solution)/shard_map/ppermute | solution.py:191
  133.4 1.5 shard_map.72
  134.9 4.6 %collective-permute-done.19.lb_ref = bf16[64,128]{1,0:T(8,128)(2,1)S(1)} collective-permute-done((bf16[64,128]{1,0:T(8,128)(2,1)S(1)}, bf16[64,128]{1,0:T(8,128)(2,1)S(1)}, u32[]{:S(2)}, u32[]{:S(2)}) %collective-permute-start.19) | collective-permute-done | bytes 16416 | tf_op jit(solution)/shard_map/ppermute | solution.py:191
  139.4 0.9 shard_map.73
  140.4 1.9 collective-permute-start.20
  142.3 3.9 %collective-permute-start.21 = (bf16[64,256]{1,0:T(8,128)(2,1)S(1)}, bf16[64,256]{1,0:T(8,128)(2,1)S(1)}, u32[]{:S(2)}, u32[]{:S(2)}) collective-permute-start(bf16[64,256]{1,0:T(8,128)(2,1)S(1)} %get-tuple-element.101.u_ref), channel_id=1, source_target_pairs={{32,64},{64,32},{96,128},{128,96},{160,192},{192,160},{224,256},{2... | collective-permute-start | bytes 98312 | tf_op jit(solution)/shard_map/ppermute | solution.py:193
  146.2 1.9 collective-permute-start.22
  148.2 11.6 %collective-permute-start.23 = (bf16[64,128]{1,0:T(8,128)(2,1)S(1)}, bf16[64,128]{1,0:T(8,128)(2,1)S(1)}, u32[]{:S(2)}, u32[]{:S(2)}) collective-permute-start(bf16[64,128]{1,0:T(8,128)(2,1)S(1)} %get-tuple-element.105), channel_id=1, source_target_pairs={{0,31},{1,2},{2,1},{3,4},{4,3},{5,6},{6,5},{7,8},{8,7},{9,10},{10,... | collective-permute-start | bytes 49160 | tf_op jit(solution)/shard_map/ppermute | solution.py:191
  159.8 1.5 shard_map.74
  161.3 4.3 %collective-permute-done.23.lb_ref = bf16[64,128]{1,0:T(8,128)(2,1)S(1)} collective-permute-done((bf16[64,128]{1,0:T(8,128)(2,1)S(1)}, bf16[64,128]{1,0:T(8,128)(2,1)S(1)}, u32[]{:S(2)}, u32[]{:S(2)}) %collective-permute-start.23) | collective-permute-done | bytes 16416 | tf_op jit(solution)/shard_map/ppermute | solution.py:191
  165.6 0.9 shard_map.75
  166.5 1.9 collective-permute-start.24
  168.4 4.4 %collective-permute-start.25 = (bf16[64,256]{1,0:T(8,128)(2,1)S(1)}, bf16[64,256]{1,0:T(8,128)(2,1)S(1)}, u32[]{:S(2)}, u32[]{:S(2)}) collective-permute-start(bf16[64,256]{1,0:T(8,128)(2,1)S(1)} %get-tuple-element.109.u_ref), channel_id=1, source_target_pairs={{32,64},{64,32},{96,128},{128,96},{160,192},{192,160},{224,256},{2... | collective-permute-start | bytes 98312 | tf_op jit(solution)/shard_map/ppermute | solution.py:193
  172.8 1.9 collective-permute-start.26
  174.8 11.4 %collective-permute-start.27 = (bf16[64,128]{1,0:T(8,128)(2,1)S(1)}, bf16[64,128]{1,0:T(8,128)(2,1)S(1)}, u32[]{:S(2)}, u32[]{:S(2)}) collective-permute-start(bf16[64,128]{1,0:T(8,128)(2,1)S(1)} %get-tuple-element.113), channel_id=1, source_target_pairs={{0,31},{1,2},{2,1},{3,4},{4,3},{5,6},{6,5},{7,8},{8,7},{9,10},{10,... | collective-permute-start | bytes 49160 | tf_op jit(solution)/shard_map/ppermute | solution.py:191
  186.2 1.5 shard_map.76
  187.7 4.7 %collective-permute-done.27.lb_ref = bf16[64,128]{1,0:T(8,128)(2,1)S(1)} collective-permute-done((bf16[64,128]{1,0:T(8,128)(2,1)S(1)}, bf16[64,128]{1,0:T(8,128)(2,1)S(1)}, u32[]{:S(2)}, u32[]{:S(2)}) %collective-permute-start.27) | collective-permute-done | bytes 16416 | tf_op jit(solution)/shard_map/ppermute | solution.py:191
  192.4 0.9 shard_map.77
  193.3 1.9 collective-permute-start.28
  195.3 3.9 %collective-permute-start.29 = (bf16[64,256]{1,0:T(8,128)(2,1)S(1)}, bf16[64,256]{1,0:T(8,128)(2,1)S(1)}, u32[]{:S(2)}, u32[]{:S(2)}) collective-permute-start(bf16[64,256]{1,0:T(8,128)(2,1)S(1)} %get-tuple-element.117.u_ref), channel_id=1, source_target_pairs={{32,64},{64,32},{96,128},{128,96},{160,192},{192,160},{224,256},{2... | collective-permute-start | bytes 98312 | tf_op jit(solution)/shard_map/ppermute | solution.py:193
  199.1 1.9 collective-permute-start.30
  201.1 11.5 %collective-permute-start.31 = (bf16[64,128]{1,0:T(8,128)(2,1)S(1)}, bf16[64,128]{1,0:T(8,128)(2,1)S(1)}, u32[]{:S(2)}, u32[]{:S(2)}) collective-permute-start(bf16[64,128]{1,0:T(8,128)(2,1)S(1)} %get-tuple-element.121), channel_id=1, source_target_pairs={{0,31},{1,2},{2,1},{3,4},{4,3},{5,6},{6,5},{7,8},{8,7},{9,10},{10,... | collective-permute-start | bytes 49160 | tf_op jit(solution)/shard_map/ppermute | solution.py:191
  212.6 1.5 shard_map.78
  214.1 4.4 %collective-permute-done.31 = bf16[64,128]{1,0:T(8,128)(2,1)S(1)} collective-permute-done((bf16[64,128]{1,0:T(8,128)(2,1)S(1)}, bf16[64,128]{1,0:T(8,128)(2,1)S(1)}, u32[]{:S(2)}, u32[]{:S(2)}) %collective-permute-start.31) | collective-permute-done | bytes 16416 | tf_op jit(solution)/shard_map/ppermute | solution.py:191
  218.5 1.5 shard_map.79
  220.1 0.8 copy-done.5
  (44 shorter events, 0.2 us)
Async XLA Ops:
  0.0 31.0 %copy-start = (bf16[1,1,2048,256]{3,2,1,0:T(8,128)(2,1)S(1)}, bf16[1,1,2048,256]{3,2,1,0:T(8,128)(2,1)}, u32[]{:S(2)}) copy-start(bf16[1,1,2048,256]{3,2,1,0:T(8,128)(2,1)} %param.10) | copy-start | bytes 3145732
  0.9 30.0 %collective-permute-start = (bf16[64,256]{1,0:T(8,128)(2,1)S(1)}, bf16[64,256]{1,0:T(8,128)(2,1)S(1)}, u32[]{:S(2)}, u32[]{:S(2)}) collective-permute-start(bf16[64,256]{1,0:T(8,128)(2,1)S(1)} %convert_bitcast_fusion.u_ref), channel_id=1, source_target_pairs={{0,32},{32,0},{64,96},{96,64},{128,160},{160,128},{192,224},{224,1... | collective-permute-start | bytes 98312 | tf_op jit(solution)/shard_map/ppermute | solution.py:194
  9.7 21.3 %collective-permute-start.1 = (bf16[64,256]{1,0:T(8,128)(2,1)S(1)}, bf16[64,256]{1,0:T(8,128)(2,1)S(1)}, u32[]{:S(2)}, u32[]{:S(2)}) collective-permute-start(bf16[64,256]{1,0:T(8,128)(2,1)S(1)} %convert_bitcast_fusion.u_ref), channel_id=1, source_target_pairs={{32,64},{64,32},{96,128},{128,96},{160,192},{192,160},{224,256},{2... | collective-permute-start | bytes 98312 | tf_op jit(solution)/shard_map/ppermute | solution.py:193
  11.6 24.4 %collective-permute-start.2 = (bf16[64,128]{1,0:T(8,128)(2,1)S(1)}, bf16[64,128]{1,0:T(8,128)(2,1)S(1)}, u32[]{:S(2)}, u32[]{:S(2)}) collective-permute-start(bf16[64,128]{1,0:T(8,128)(2,1)S(1)} %get-tuple-element.140), channel_id=1, source_target_pairs={{0,1},{1,0},{2,3},{3,2},{4,5},{5,4},{6,7},{7,6},{8,9},{9,8},{10,11... | collective-permute-start | bytes 49160 | tf_op jit(solution)/shard_map/ppermute | solution.py:192
  13.6 22.5 %collective-permute-start.3 = (bf16[64,128]{1,0:T(8,128)(2,1)S(1)}, bf16[64,128]{1,0:T(8,128)(2,1)S(1)}, u32[]{:S(2)}, u32[]{:S(2)}) collective-permute-start(bf16[64,128]{1,0:T(8,128)(2,1)S(1)} %get-tuple-element.139), channel_id=1, source_target_pairs={{0,31},{1,2},{2,1},{3,4},{4,3},{5,6},{6,5},{7,8},{8,7},{9,10},{10,... | collective-permute-start | bytes 49160 | tf_op jit(solution)/shard_map/ppermute | solution.py:191
  31.0 1.0 copy-start.1
  32.1 1.6 copy-start.2
  33.6 0.9 copy-start.4
  36.0 20.1 %copy-start.3 = (bf16[1,1,16,4,128,128]{5,4,3,2,1,0:T(8,128)(2,1)S(1)}, bf16[1,1,16,4,128,128]{5,4,3,2,1,0:T(8,128)(2,1)}, u32[]{:S(2)}) copy-start(bf16[1,1,16,4,128,128]{5,4,3,2,1,0:T(8,128)(2,1)} %param.8) | copy-start | bytes 6291460
  37.0 19.1 %collective-permute-start.4 = (bf16[64,256]{1,0:T(8,128)(2,1)S(1)}, bf16[64,256]{1,0:T(8,128)(2,1)S(1)}, u32[]{:S(2)}, u32[]{:S(2)}) collective-permute-start(bf16[64,256]{1,0:T(8,128)(2,1)S(1)} %get-tuple-element.69.u_ref), channel_id=1, source_target_pairs={{0,32},{32,0},{64,96},{96,64},{128,160},{160,128},{192,224},{224,1... | collective-permute-start | bytes 98312 | tf_op jit(solution)/shard_map/ppermute | solution.py:194
  38.9 17.2 %collective-permute-start.5 = (bf16[64,256]{1,0:T(8,128)(2,1)S(1)}, bf16[64,256]{1,0:T(8,128)(2,1)S(1)}, u32[]{:S(2)}, u32[]{:S(2)}) collective-permute-start(bf16[64,256]{1,0:T(8,128)(2,1)S(1)} %get-tuple-element.69.u_ref), channel_id=1, source_target_pairs={{32,64},{64,32},{96,128},{128,96},{160,192},{192,160},{224,256},{2... | collective-permute-start | bytes 98312 | tf_op jit(solution)/shard_map/ppermute | solution.py:193
  42.5 15.1 %collective-permute-start.6 = (bf16[64,128]{1,0:T(8,128)(2,1)S(1)}, bf16[64,128]{1,0:T(8,128)(2,1)S(1)}, u32[]{:S(2)}, u32[]{:S(2)}) collective-permute-start(bf16[64,128]{1,0:T(8,128)(2,1)S(1)} %get-tuple-element.72), channel_id=1, source_target_pairs={{0,1},{1,0},{2,3},{3,2},{4,5},{5,4},{6,7},{7,6},{8,9},{9,8},{10,11... | collective-permute-start | bytes 49160 | tf_op jit(solution)/shard_map/ppermute | solution.py:192
  44.5 17.6 %collective-permute-start.7 = (bf16[64,128]{1,0:T(8,128)(2,1)S(1)}, bf16[64,128]{1,0:T(8,128)(2,1)S(1)}, u32[]{:S(2)}, u32[]{:S(2)}) collective-permute-start(bf16[64,128]{1,0:T(8,128)(2,1)S(1)} %get-tuple-element.73), channel_id=1, source_target_pairs={{0,31},{1,2},{2,1},{3,4},{4,3},{5,6},{6,5},{7,8},{8,7},{9,10},{10,... | collective-permute-start | bytes 49160 | tf_op jit(solution)/shard_map/ppermute | solution.py:191
  62.9 18.6 %collective-permute-start.8 = (bf16[64,256]{1,0:T(8,128)(2,1)S(1)}, bf16[64,256]{1,0:T(8,128)(2,1)S(1)}, u32[]{:S(2)}, u32[]{:S(2)}) collective-permute-start(bf16[64,256]{1,0:T(8,128)(2,1)S(1)} %get-tuple-element.77.u_ref), channel_id=1, source_target_pairs={{0,32},{32,0},{64,96},{96,64},{128,160},{160,128},{192,224},{224,1... | collective-permute-start | bytes 98312 | tf_op jit(solution)/shard_map/ppermute | solution.py:194
  64.9 16.7 %collective-permute-start.9 = (bf16[64,256]{1,0:T(8,128)(2,1)S(1)}, bf16[64,256]{1,0:T(8,128)(2,1)S(1)}, u32[]{:S(2)}, u32[]{:S(2)}) collective-permute-start(bf16[64,256]{1,0:T(8,128)(2,1)S(1)} %get-tuple-element.77.u_ref), channel_id=1, source_target_pairs={{32,64},{64,32},{96,128},{128,96},{160,192},{192,160},{224,256},{2... | collective-permute-start | bytes 98312 | tf_op jit(solution)/shard_map/ppermute | solution.py:193
  68.1 15.0 %collective-permute-start.10 = (bf16[64,128]{1,0:T(8,128)(2,1)S(1)}, bf16[64,128]{1,0:T(8,128)(2,1)S(1)}, u32[]{:S(2)}, u32[]{:S(2)}) collective-permute-start(bf16[64,128]{1,0:T(8,128)(2,1)S(1)} %get-tuple-element.80), channel_id=1, source_target_pairs={{0,1},{1,0},{2,3},{3,2},{4,5},{5,4},{6,7},{7,6},{8,9},{9,8},{10,11... | collective-permute-start | bytes 49160 | tf_op jit(solution)/shard_map/ppermute | solution.py:192
  70.0 17.4 %collective-permute-start.11 = (bf16[64,128]{1,0:T(8,128)(2,1)S(1)}, bf16[64,128]{1,0:T(8,128)(2,1)S(1)}, u32[]{:S(2)}, u32[]{:S(2)}) collective-permute-start(bf16[64,128]{1,0:T(8,128)(2,1)S(1)} %get-tuple-element.81), channel_id=1, source_target_pairs={{0,31},{1,2},{2,1},{3,4},{4,3},{5,6},{6,5},{7,8},{8,7},{9,10},{10,... | collective-permute-start | bytes 49160 | tf_op jit(solution)/shard_map/ppermute | solution.py:191
  88.3 19.5 %collective-permute-start.12 = (bf16[64,256]{1,0:T(8,128)(2,1)S(1)}, bf16[64,256]{1,0:T(8,128)(2,1)S(1)}, u32[]{:S(2)}, u32[]{:S(2)}) collective-permute-start(bf16[64,256]{1,0:T(8,128)(2,1)S(1)} %get-tuple-element.85.u_ref), channel_id=1, source_target_pairs={{0,32},{32,0},{64,96},{96,64},{128,160},{160,128},{192,224},{224,1... | collective-permute-start | bytes 98312 | tf_op jit(solution)/shard_map/ppermute | solution.py:194
  90.3 17.6 %collective-permute-start.13 = (bf16[64,256]{1,0:T(8,128)(2,1)S(1)}, bf16[64,256]{1,0:T(8,128)(2,1)S(1)}, u32[]{:S(2)}, u32[]{:S(2)}) collective-permute-start(bf16[64,256]{1,0:T(8,128)(2,1)S(1)} %get-tuple-element.85.u_ref), channel_id=1, source_target_pairs={{32,64},{64,32},{96,128},{128,96},{160,192},{192,160},{224,256},{2... | collective-permute-start | bytes 98312 | tf_op jit(solution)/shard_map/ppermute | solution.py:193
  94.4 15.0 %collective-permute-start.14 = (bf16[64,128]{1,0:T(8,128)(2,1)S(1)}, bf16[64,128]{1,0:T(8,128)(2,1)S(1)}, u32[]{:S(2)}, u32[]{:S(2)}) collective-permute-start(bf16[64,128]{1,0:T(8,128)(2,1)S(1)} %get-tuple-element.88), channel_id=1, source_target_pairs={{0,1},{1,0},{2,3},{3,2},{4,5},{5,4},{6,7},{7,6},{8,9},{9,8},{10,11... | collective-permute-start | bytes 49160 | tf_op jit(solution)/shard_map/ppermute | solution.py:192
  96.3 17.5 %collective-permute-start.15 = (bf16[64,128]{1,0:T(8,128)(2,1)S(1)}, bf16[64,128]{1,0:T(8,128)(2,1)S(1)}, u32[]{:S(2)}, u32[]{:S(2)}) collective-permute-start(bf16[64,128]{1,0:T(8,128)(2,1)S(1)} %get-tuple-element.89), channel_id=1, source_target_pairs={{0,31},{1,2},{2,1},{3,4},{4,3},{5,6},{6,5},{7,8},{8,7},{9,10},{10,... | collective-permute-start | bytes 49160 | tf_op jit(solution)/shard_map/ppermute | solution.py:191
  114.7 18.7 %collective-permute-start.16 = (bf16[64,256]{1,0:T(8,128)(2,1)S(1)}, bf16[64,256]{1,0:T(8,128)(2,1)S(1)}, u32[]{:S(2)}, u32[]{:S(2)}) collective-permute-start(bf16[64,256]{1,0:T(8,128)(2,1)S(1)} %get-tuple-element.93.u_ref), channel_id=1, source_target_pairs={{0,32},{32,0},{64,96},{96,64},{128,160},{160,128},{192,224},{224,1... | collective-permute-start | bytes 98312 | tf_op jit(solution)/shard_map/ppermute | solution.py:194
  116.6 16.8 %collective-permute-start.17 = (bf16[64,256]{1,0:T(8,128)(2,1)S(1)}, bf16[64,256]{1,0:T(8,128)(2,1)S(1)}, u32[]{:S(2)}, u32[]{:S(2)}) collective-permute-start(bf16[64,256]{1,0:T(8,128)(2,1)S(1)} %get-tuple-element.93.u_ref), channel_id=1, source_target_pairs={{32,64},{64,32},{96,128},{128,96},{160,192},{192,160},{224,256},{2... | collective-permute-start | bytes 98312 | tf_op jit(solution)/shard_map/ppermute | solution.py:193
  120.0 14.9 %collective-permute-start.18 = (bf16[64,128]{1,0:T(8,128)(2,1)S(1)}, bf16[64,128]{1,0:T(8,128)(2,1)S(1)}, u32[]{:S(2)}, u32[]{:S(2)}) collective-permute-start(bf16[64,128]{1,0:T(8,128)(2,1)S(1)} %get-tuple-element.96), channel_id=1, source_target_pairs={{0,1},{1,0},{2,3},{3,2},{4,5},{5,4},{6,7},{7,6},{8,9},{9,8},{10,11... | collective-permute-start | bytes 49160 | tf_op jit(solution)/shard_map/ppermute | solution.py:192
  121.9 17.5 %collective-permute-start.19 = (bf16[64,128]{1,0:T(8,128)(2,1)S(1)}, bf16[64,128]{1,0:T(8,128)(2,1)S(1)}, u32[]{:S(2)}, u32[]{:S(2)}) collective-permute-start(bf16[64,128]{1,0:T(8,128)(2,1)S(1)} %get-tuple-element.97), channel_id=1, source_target_pairs={{0,31},{1,2},{2,1},{3,4},{4,3},{5,6},{6,5},{7,8},{8,7},{9,10},{10,... | collective-permute-start | bytes 49160 | tf_op jit(solution)/shard_map/ppermute | solution.py:191
  140.4 19.4 %collective-permute-start.20 = (bf16[64,256]{1,0:T(8,128)(2,1)S(1)}, bf16[64,256]{1,0:T(8,128)(2,1)S(1)}, u32[]{:S(2)}, u32[]{:S(2)}) collective-permute-start(bf16[64,256]{1,0:T(8,128)(2,1)S(1)} %get-tuple-element.101.u_ref), channel_id=1, source_target_pairs={{0,32},{32,0},{64,96},{96,64},{128,160},{160,128},{192,224},{224,1... | collective-permute-start | bytes 98312 | tf_op jit(solution)/shard_map/ppermute | solution.py:194
  142.3 17.5 %collective-permute-start.21 = (bf16[64,256]{1,0:T(8,128)(2,1)S(1)}, bf16[64,256]{1,0:T(8,128)(2,1)S(1)}, u32[]{:S(2)}, u32[]{:S(2)}) collective-permute-start(bf16[64,256]{1,0:T(8,128)(2,1)S(1)} %get-tuple-element.101.u_ref), channel_id=1, source_target_pairs={{32,64},{64,32},{96,128},{128,96},{160,192},{192,160},{224,256},{2... | collective-permute-start | bytes 98312 | tf_op jit(solution)/shard_map/ppermute | solution.py:193
  146.2 15.1 %collective-permute-start.22 = (bf16[64,128]{1,0:T(8,128)(2,1)S(1)}, bf16[64,128]{1,0:T(8,128)(2,1)S(1)}, u32[]{:S(2)}, u32[]{:S(2)}) collective-permute-start(bf16[64,128]{1,0:T(8,128)(2,1)S(1)} %get-tuple-element.104), channel_id=1, source_target_pairs={{0,1},{1,0},{2,3},{3,2},{4,5},{5,4},{6,7},{7,6},{8,9},{9,8},{10,11... | collective-permute-start | bytes 49160 | tf_op jit(solution)/shard_map/ppermute | solution.py:192
  148.2 17.4 %collective-permute-start.23 = (bf16[64,128]{1,0:T(8,128)(2,1)S(1)}, bf16[64,128]{1,0:T(8,128)(2,1)S(1)}, u32[]{:S(2)}, u32[]{:S(2)}) collective-permute-start(bf16[64,128]{1,0:T(8,128)(2,1)S(1)} %get-tuple-element.105), channel_id=1, source_target_pairs={{0,31},{1,2},{2,1},{3,4},{4,3},{5,6},{6,5},{7,8},{8,7},{9,10},{10,... | collective-permute-start | bytes 49160 | tf_op jit(solution)/shard_map/ppermute | solution.py:191
  166.5 19.7 %collective-permute-start.24 = (bf16[64,256]{1,0:T(8,128)(2,1)S(1)}, bf16[64,256]{1,0:T(8,128)(2,1)S(1)}, u32[]{:S(2)}, u32[]{:S(2)}) collective-permute-start(bf16[64,256]{1,0:T(8,128)(2,1)S(1)} %get-tuple-element.109.u_ref), channel_id=1, source_target_pairs={{0,32},{32,0},{64,96},{96,64},{128,160},{160,128},{192,224},{224,1... | collective-permute-start | bytes 98312 | tf_op jit(solution)/shard_map/ppermute | solution.py:194
  168.4 17.8 %collective-permute-start.25 = (bf16[64,256]{1,0:T(8,128)(2,1)S(1)}, bf16[64,256]{1,0:T(8,128)(2,1)S(1)}, u32[]{:S(2)}, u32[]{:S(2)}) collective-permute-start(bf16[64,256]{1,0:T(8,128)(2,1)S(1)} %get-tuple-element.109.u_ref), channel_id=1, source_target_pairs={{32,64},{64,32},{96,128},{128,96},{160,192},{192,160},{224,256},{2... | collective-permute-start | bytes 98312 | tf_op jit(solution)/shard_map/ppermute | solution.py:193
  172.8 14.9 %collective-permute-start.26 = (bf16[64,128]{1,0:T(8,128)(2,1)S(1)}, bf16[64,128]{1,0:T(8,128)(2,1)S(1)}, u32[]{:S(2)}, u32[]{:S(2)}) collective-permute-start(bf16[64,128]{1,0:T(8,128)(2,1)S(1)} %get-tuple-element.112), channel_id=1, source_target_pairs={{0,1},{1,0},{2,3},{3,2},{4,5},{5,4},{6,7},{7,6},{8,9},{9,8},{10,11... | collective-permute-start | bytes 49160 | tf_op jit(solution)/shard_map/ppermute | solution.py:192
  174.8 17.7 %collective-permute-start.27 = (bf16[64,128]{1,0:T(8,128)(2,1)S(1)}, bf16[64,128]{1,0:T(8,128)(2,1)S(1)}, u32[]{:S(2)}, u32[]{:S(2)}) collective-permute-start(bf16[64,128]{1,0:T(8,128)(2,1)S(1)} %get-tuple-element.113), channel_id=1, source_target_pairs={{0,31},{1,2},{2,1},{3,4},{4,3},{5,6},{6,5},{7,8},{8,7},{9,10},{10,... | collective-permute-start | bytes 49160 | tf_op jit(solution)/shard_map/ppermute | solution.py:191
  193.3 19.3 %collective-permute-start.28 = (bf16[64,256]{1,0:T(8,128)(2,1)S(1)}, bf16[64,256]{1,0:T(8,128)(2,1)S(1)}, u32[]{:S(2)}, u32[]{:S(2)}) collective-permute-start(bf16[64,256]{1,0:T(8,128)(2,1)S(1)} %get-tuple-element.117.u_ref), channel_id=1, source_target_pairs={{0,32},{32,0},{64,96},{96,64},{128,160},{160,128},{192,224},{224,1... | collective-permute-start | bytes 98312 | tf_op jit(solution)/shard_map/ppermute | solution.py:194
  195.3 17.4 %collective-permute-start.29 = (bf16[64,256]{1,0:T(8,128)(2,1)S(1)}, bf16[64,256]{1,0:T(8,128)(2,1)S(1)}, u32[]{:S(2)}, u32[]{:S(2)}) collective-permute-start(bf16[64,256]{1,0:T(8,128)(2,1)S(1)} %get-tuple-element.117.u_ref), channel_id=1, source_target_pairs={{32,64},{64,32},{96,128},{128,96},{160,192},{192,160},{224,256},{2... | collective-permute-start | bytes 98312 | tf_op jit(solution)/shard_map/ppermute | solution.py:193
  199.1 15.0 %collective-permute-start.30 = (bf16[64,128]{1,0:T(8,128)(2,1)S(1)}, bf16[64,128]{1,0:T(8,128)(2,1)S(1)}, u32[]{:S(2)}, u32[]{:S(2)}) collective-permute-start(bf16[64,128]{1,0:T(8,128)(2,1)S(1)} %get-tuple-element.120), channel_id=1, source_target_pairs={{0,1},{1,0},{2,3},{3,2},{4,5},{5,4},{6,7},{7,6},{8,9},{9,8},{10,11... | collective-permute-start | bytes 49160 | tf_op jit(solution)/shard_map/ppermute | solution.py:192
  201.1 17.5 %collective-permute-start.31 = (bf16[64,128]{1,0:T(8,128)(2,1)S(1)}, bf16[64,128]{1,0:T(8,128)(2,1)S(1)}, u32[]{:S(2)}, u32[]{:S(2)}) collective-permute-start(bf16[64,128]{1,0:T(8,128)(2,1)S(1)} %get-tuple-element.121), channel_id=1, source_target_pairs={{0,31},{1,2},{2,1},{3,4},{4,3},{5,6},{6,5},{7,8},{8,7},{9,10},{10,... | collective-permute-start | bytes 49160 | tf_op jit(solution)/shard_map/ppermute | solution.py:191
  220.1 0.8 copy-start.5

commit v6 on v4

--- a/solution.py
+++ b/solution.py
@@ -10,19 +10,24 @@
 LONC = 2
 OV = 4
 STEPS = 8
-PTS = 8
 IN_BLOCKS = 6
 
 
-def selector(slot_list):
-    onehot = (slot_list[:, None] == jnp.arange(PTS, dtype=jnp.int32)[None, :]).astype(jnp.bfloat16)
-    eye = jnp.eye(VARS, dtype=jnp.bfloat16)
-    full = onehot.T[:, None, :, None] * eye[None, :, None, :]
-    return full.reshape(PTS * VARS, OV * VARS)
+def build_selector(lists_ref, side, shape):
+    row = lax.broadcasted_iota(jnp.int32, shape, 0)
+    col = lax.broadcasted_iota(jnp.int32, shape, 1)
+    slot = col // VARS
+    wanted = jnp.full(shape, lists_ref[side, OV - 1], jnp.int32)
+    for s in range(OV - 2, -1, -1):
+        wanted = jnp.where(slot == s, lists_ref[side, s], wanted)
+    hit = (row // VARS == wanted) & (row % VARS == col % VARS)
+    return hit.astype(jnp.bfloat16)
 
 
-def couple_kernel(u_ref, r_ref, c_ref, win_ref, acc_out):
+def couple_kernel(lists_ref, u_ref, r_ref, c_ref, win_ref, acc_out, sn_out, ss_out):
     res_blocks, links, breadth, _ = c_ref.shape
+    sn_out[...] = build_selector(lists_ref, 0, sn_out.shape)
+    ss_out[...] = build_selector(lists_ref, 1, ss_out.shape)
     u = u_ref[...]
     own = u.shape[1] // breadth
     r = r_ref[...]
@@ -74,15 +79,22 @@
 VMEM_SPEC = pl.BlockSpec(memory_space=pltpu.MemorySpace.VMEM)
 
 
-def couple_call(u, reservoir, block_weight, entry_weight):
+def couple_call(lists, u, reservoir, block_weight, entry_weight):
     members, nodes = reservoir.shape
+    feats = u.shape[1]
+    picked = OV * VARS
+    out_shape = (
+        jax.ShapeDtypeStruct((members, nodes), jnp.float32),
+        jax.ShapeDtypeStruct((feats, picked), jnp.bfloat16),
+        jax.ShapeDtypeStruct((feats, picked), jnp.bfloat16),
+    )
     return pl.pallas_call(
         couple_kernel,
-        out_shape=jax.ShapeDtypeStruct((members, nodes), jnp.float32),
-        in_specs=[VMEM_SPEC] * 4,
-        out_specs=VMEM_SPEC,
+        out_shape=out_shape,
+        in_specs=[pl.BlockSpec(memory_space=pltpu.MemorySpace.SMEM)] + [VMEM_SPEC] * 4,
+        out_specs=(VMEM_SPEC, VMEM_SPEC, VMEM_SPEC),
         compiler_params=pltpu.CompilerParams(vmem_limit_bytes=32 * 1024 * 1024),
-    )(u, reservoir, block_weight, entry_weight)
+    )(lists, u, reservoir, block_weight, entry_weight)
 
 
 def step_call(flags, acc, lon_a, lon_b, lat_a, lat_b, sel_n, sel_s, entry_weight, read_weight):
@@ -125,8 +137,6 @@
     read_weight = readout[0, 0]
     lists = intersection[0, 0]
     half = current.shape[1] // LONC
-    sel_n = selector(lists[0])
-    sel_s = selector(lists[1])
     lon_even = (lax.axis_index("lon") % 2 == 0).astype(jnp.int32)
     lat_even = (lax.axis_index("lat") % 2 == 0).astype(jnp.int32)
     flags = jnp.stack([lon_even, lat_even])
@@ -147,7 +157,7 @@
         lon_a = lax.ppermute(send_a, "lon", lon_pairs_a)
         lat_b = lax.ppermute(rounded, "lat", lat_pairs_b)
         lat_a = lax.ppermute(rounded, "lat", lat_pairs_a)
-        acc = couple_call(rounded, reservoir, block_weight, entry_weight)
+        acc, sel_n, sel_s = couple_call(lists, rounded, reservoir, block_weight, entry_weight)
         current, rounded, send_a, send_b, reservoir = step_call(
             flags, acc, lon_a, lon_b, lat_a, lat_b, sel_n, sel_s, entry_weight, read_weight)
         outputs.append(current)

time: 227 us -> 227 us (level)
  waiting for transfers between devices: 58 us -> 50 us
  Pallas kernels: 13.7 us -> 18.2 us
  starting transfers between devices: 144 us -> 148 us
    ppermute x8, waiting for transfers between devices: 58 us -> 49.9 us  [per_device(): lon_b = lax.ppermute(send_b, 'lon', lon_pairs_b)]
    pallas_call x8, Pallas kernels: 5.81 us -> 10.3 us  [couple_call(): pl.pallas_call(couple_kernel, out_shape=out_shape, in_specs=[pl.BlockSpec...]
    ppermute x8, starting transfers between devices: 74.2 us -> 78.2 us  [per_device(): lon_b = lax.ppermute(send_b, 'lon', lon_pairs_b)]
    unnamed x21 -> x25, local copies, waits for them, and re-layouts: 4.88 us -> 6.33 us
  transfers between devices with their start and end apart: 32 -> 32, of which waited for: 7 -> 7; matrix products, arithmetic and copies ran while one was open for 1% -> 0% of each run, Pallas kernels for 3% -> 5%
where the time goes in v6:
time: 227 us; the launch traced here: 226 us
  starting transfers between devices  148 us (65%)
  waiting for transfers between devices  50 us (22%)
  Pallas kernels  18.2 us (8%)
  local copies, waits for them, and re-layouts  8.1 us (4%)
    ppermute x8, starting transfers between devices, per_device(): lon_b = lax.ppermute(send_b, 'lon', lon_pairs_b)  78.2 us
    ppermute x8, waiting for transfers between devices, per_device(): lon_b = lax.ppermute(send_b, 'lon', lon_pairs_b)  49.9 us
    ppermute x8, starting transfers between devices, per_device(): lat_b = lax.ppermute(rounded, 'lat', lat_pairs_b)  31 us
    ppermute x8, starting transfers between devices, per_device(): lat_a = lax.ppermute(rounded, 'lat', lat_pairs_a)  22.2 us
    ppermute x8, starting transfers between devices, per_device(): lon_a = lax.ppermute(send_a, 'lon', lon_pairs_a)  17.1 us
    pallas_call x8, Pallas kernels, couple_call(): pl.pallas_call(couple_kernel, out_shape=out_shape, in_specs=[pl.BlockSpec...  10.3 us
    pallas_call x7, Pallas kernels, step_call(): pl.pallas_call(step_kernel, out_shape=out_shape, in_specs=[pl.BlockSpec(m...  7.93 us
    unnamed x25, local copies, waits for them, and re-layouts  6.33 us
  transfers between devices with their start and end apart: 32, of which 7 were waited for; matrix products, arithmetic and copies ran while one was open for 0% of the time, Pallas kernels for 5%

profile of v6, /device:TPU:1, one launch (start us, length us, event | category | flops | bytes accessed | tf_op | source)
XLA Modules:
  0.0 226.2 jit_solution(18366574309551630332)
XLA Ops:
  0.0 0.8 convert_bitcast_fusion.u_ref
  0.8 8.7 %collective-permute-start.2 = (bf16[64,256]{1,0:T(8,128)(2,1)S(1)}, bf16[64,256]{1,0:T(8,128)(2,1)S(1)}, u32[]{:S(2)}, u32[]{:S(2)}) collective-permute-start(bf16[64,256]{1,0:T(8,128)(2,1)S(1)} %convert_bitcast_fusion.u_ref), channel_id=1, source_target_pairs={{0,32},{32,0},{64,96},{96,64},{128,160},{160,128},{192,224},{224,1... | collective-permute-start | bytes 98312 | tf_op jit(solution)/shard_map/ppermute | solution.py:159
  9.6 1.9 collective-permute-start.3
  11.5 15.4 %collective-permute-start.1 = (bf16[64,128]{1,0:T(8,128)(2,1)S(1)}, bf16[64,128]{1,0:T(8,128)(2,1)S(1)}, u32[]{:S(2)}, u32[]{:S(2)}) collective-permute-start(bf16[64,128]{1,0:T(8,128)(2,1)S(1)} %get-tuple-element.139), channel_id=1, source_target_pairs={{0,31},{1,2},{2,1},{3,4},{4,3},{5,6},{6,5},{7,8},{8,7},{9,10},{10,... | collective-permute-start | bytes 49160 | tf_op jit(solution)/shard_map/ppermute | solution.py:156
  26.9 1.9 collective-permute-start
  28.9 0.1 pad_add_fusion.flag_ref
  28.9 1.6 copy-done
  30.5 1.0 copy-done.2
  31.6 0.9 copy-done.6
  32.5 0.7 copy-done.7
  33.2 1.3 shard_map.64
  34.6 1.2 copy-done.4
  35.8 1.1 shard_map.65
  36.9 3.4 %collective-permute-start.7 = (bf16[64,256]{1,0:T(8,128)(2,1)S(1)}, bf16[64,256]{1,0:T(8,128)(2,1)S(1)}, u32[]{:S(2)}, u32[]{:S(2)}) collective-permute-start(bf16[64,256]{1,0:T(8,128)(2,1)S(1)} %get-tuple-element.69.u_ref), channel_id=1, source_target_pairs={{32,64},{64,32},{96,128},{128,96},{160,192},{192,160},{224,256},{2... | collective-permute-start | bytes 98312 | tf_op jit(solution)/shard_map/ppermute | solution.py:158
  40.4 1.9 collective-permute-start.6
  42.3 3.6 %collective-permute-start.4 = (bf16[64,128]{1,0:T(8,128)(2,1)S(1)}, bf16[64,128]{1,0:T(8,128)(2,1)S(1)}, u32[]{:S(2)}, u32[]{:S(2)}) collective-permute-start(bf16[64,128]{1,0:T(8,128)(2,1)S(1)} %get-tuple-element.72), channel_id=1, source_target_pairs={{0,1},{1,0},{2,3},{3,2},{4,5},{5,4},{6,7},{7,6},{8,9},{9,8},{10,11... | collective-permute-start | bytes 49160 | tf_op jit(solution)/shard_map/ppermute | solution.py:157
  45.9 9.2 %collective-permute-start.5 = (bf16[64,128]{1,0:T(8,128)(2,1)S(1)}, bf16[64,128]{1,0:T(8,128)(2,1)S(1)}, u32[]{:S(2)}, u32[]{:S(2)}) collective-permute-start(bf16[64,128]{1,0:T(8,128)(2,1)S(1)} %get-tuple-element.73), channel_id=1, source_target_pairs={{0,31},{1,2},{2,1},{3,4},{4,3},{5,6},{6,5},{7,8},{8,7},{9,10},{10,... | collective-permute-start | bytes 49160 | tf_op jit(solution)/shard_map/ppermute | solution.py:156
  55.2 1.3 shard_map.66
  56.5 0.0 collective-permute-done.4.la_ref
  56.5 6.9 %collective-permute-done.5.lb_ref = bf16[64,128]{1,0:T(8,128)(2,1)S(1)} collective-permute-done((bf16[64,128]{1,0:T(8,128)(2,1)S(1)}, bf16[64,128]{1,0:T(8,128)(2,1)S(1)}, u32[]{:S(2)}, u32[]{:S(2)}) %collective-permute-start.5) | collective-permute-done | bytes 16416 | tf_op jit(solution)/shard_map/ppermute | solution.py:156
  63.4 1.1 shard_map.67
  64.5 4.5 %collective-permute-start.11 = (bf16[64,256]{1,0:T(8,128)(2,1)S(1)}, bf16[64,256]{1,0:T(8,128)(2,1)S(1)}, u32[]{:S(2)}, u32[]{:S(2)}) collective-permute-start(bf16[64,256]{1,0:T(8,128)(2,1)S(1)} %get-tuple-element.77.u_ref), channel_id=1, source_target_pairs={{32,64},{64,32},{96,128},{128,96},{160,192},{192,160},{224,256},{2... | collective-permute-start | bytes 98312 | tf_op jit(solution)/shard_map/ppermute | solution.py:158
  69.0 1.9 collective-permute-start.10
  70.9 1.9 collective-permute-start.8
  72.8 8.8 %collective-permute-start.9 = (bf16[64,128]{1,0:T(8,128)(2,1)S(1)}, bf16[64,128]{1,0:T(8,128)(2,1)S(1)}, u32[]{:S(2)}, u32[]{:S(2)}) collective-permute-start(bf16[64,128]{1,0:T(8,128)(2,1)S(1)} %get-tuple-element.81), channel_id=1, source_target_pairs={{0,31},{1,2},{2,1},{3,4},{4,3},{5,6},{6,5},{7,8},{8,7},{9,10},{10,... | collective-permute-start | bytes 49160 | tf_op jit(solution)/shard_map/ppermute | solution.py:156
  81.7 1.3 shard_map.68
  83.0 7.3 %collective-permute-done.9.lb_ref = bf16[64,128]{1,0:T(8,128)(2,1)S(1)} collective-permute-done((bf16[64,128]{1,0:T(8,128)(2,1)S(1)}, bf16[64,128]{1,0:T(8,128)(2,1)S(1)}, u32[]{:S(2)}, u32[]{:S(2)}) %collective-permute-start.9) | collective-permute-done | bytes 16416 | tf_op jit(solution)/shard_map/ppermute | solution.py:156
  90.3 1.1 shard_map.69
  91.4 4.2 %collective-permute-start.15 = (bf16[64,256]{1,0:T(8,128)(2,1)S(1)}, bf16[64,256]{1,0:T(8,128)(2,1)S(1)}, u32[]{:S(2)}, u32[]{:S(2)}) collective-permute-start(bf16[64,256]{1,0:T(8,128)(2,1)S(1)} %get-tuple-element.85.u_ref), channel_id=1, source_target_pairs={{32,64},{64,32},{96,128},{128,96},{160,192},{192,160},{224,256},{2... | collective-permute-start | bytes 98312 | tf_op jit(solution)/shard_map/ppermute | solution.py:158
  95.6 1.9 collective-permute-start.14
  97.5 1.9 collective-permute-start.12
  99.4 9.0 %collective-permute-start.13 = (bf16[64,128]{1,0:T(8,128)(2,1)S(1)}, bf16[64,128]{1,0:T(8,128)(2,1)S(1)}, u32[]{:S(2)}, u32[]{:S(2)}) collective-permute-start(bf16[64,128]{1,0:T(8,128)(2,1)S(1)} %get-tuple-element.89), channel_id=1, source_target_pairs={{0,31},{1,2},{2,1},{3,4},{4,3},{5,6},{6,5},{7,8},{8,7},{9,10},{10,... | collective-permute-start | bytes 49160 | tf_op jit(solution)/shard_map/ppermute | solution.py:156
  108.5 1.3 shard_map.70
  109.8 7.1 %collective-permute-done.13.lb_ref = bf16[64,128]{1,0:T(8,128)(2,1)S(1)} collective-permute-done((bf16[64,128]{1,0:T(8,128)(2,1)S(1)}, bf16[64,128]{1,0:T(8,128)(2,1)S(1)}, u32[]{:S(2)}, u32[]{:S(2)}) %collective-permute-start.13) | collective-permute-done | bytes 16416 | tf_op jit(solution)/shard_map/ppermute | solution.py:156
  116.9 1.1 shard_map.71
  118.0 5.4 %collective-permute-start.19 = (bf16[64,256]{1,0:T(8,128)(2,1)S(1)}, bf16[64,256]{1,0:T(8,128)(2,1)S(1)}, u32[]{:S(2)}, u32[]{:S(2)}) collective-permute-start(bf16[64,256]{1,0:T(8,128)(2,1)S(1)} %get-tuple-element.93.u_ref), channel_id=1, source_target_pairs={{32,64},{64,32},{96,128},{128,96},{160,192},{192,160},{224,256},{2... | collective-permute-start | bytes 98312 | tf_op jit(solution)/shard_map/ppermute | solution.py:158
  123.4 1.9 collective-permute-start.18
  125.3 1.9 collective-permute-start.16
  127.3 8.8 %collective-permute-start.17 = (bf16[64,128]{1,0:T(8,128)(2,1)S(1)}, bf16[64,128]{1,0:T(8,128)(2,1)S(1)}, u32[]{:S(2)}, u32[]{:S(2)}) collective-permute-start(bf16[64,128]{1,0:T(8,128)(2,1)S(1)} %get-tuple-element.97), channel_id=1, source_target_pairs={{0,31},{1,2},{2,1},{3,4},{4,3},{5,6},{6,5},{7,8},{8,7},{9,10},{10,... | collective-permute-start | bytes 49160 | tf_op jit(solution)/shard_map/ppermute | solution.py:156
  136.1 1.3 shard_map.72
  137.4 7.3 %collective-permute-done.17.lb_ref = bf16[64,128]{1,0:T(8,128)(2,1)S(1)} collective-permute-done((bf16[64,128]{1,0:T(8,128)(2,1)S(1)}, bf16[64,128]{1,0:T(8,128)(2,1)S(1)}, u32[]{:S(2)}, u32[]{:S(2)}) %collective-permute-start.17) | collective-permute-done | bytes 16416 | tf_op jit(solution)/shard_map/ppermute | solution.py:156
  144.7 1.1 shard_map.73
  145.8 3.5 %collective-permute-start.23 = (bf16[64,256]{1,0:T(8,128)(2,1)S(1)}, bf16[64,256]{1,0:T(8,128)(2,1)S(1)}, u32[]{:S(2)}, u32[]{:S(2)}) collective-permute-start(bf16[64,256]{1,0:T(8,128)(2,1)S(1)} %get-tuple-element.101.u_ref), channel_id=1, source_target_pairs={{32,64},{64,32},{96,128},{128,96},{160,192},{192,160},{224,256},{2... | collective-permute-start | bytes 98312 | tf_op jit(solution)/shard_map/ppermute | solution.py:158
  149.4 1.9 collective-permute-start.22
  151.3 1.9 collective-permute-start.20
  153.2 8.7 %collective-permute-start.21 = (bf16[64,128]{1,0:T(8,128)(2,1)S(1)}, bf16[64,128]{1,0:T(8,128)(2,1)S(1)}, u32[]{:S(2)}, u32[]{:S(2)}) collective-permute-start(bf16[64,128]{1,0:T(8,128)(2,1)S(1)} %get-tuple-element.105), channel_id=1, source_target_pairs={{0,31},{1,2},{2,1},{3,4},{4,3},{5,6},{6,5},{7,8},{8,7},{9,10},{10,... | collective-permute-start | bytes 49160 | tf_op jit(solution)/shard_map/ppermute | solution.py:156
  162.0 1.3 shard_map.74
  163.3 7.4 %collective-permute-done.21.lb_ref = bf16[64,128]{1,0:T(8,128)(2,1)S(1)} collective-permute-done((bf16[64,128]{1,0:T(8,128)(2,1)S(1)}, bf16[64,128]{1,0:T(8,128)(2,1)S(1)}, u32[]{:S(2)}, u32[]{:S(2)}) %collective-permute-start.21) | collective-permute-done | bytes 16416 | tf_op jit(solution)/shard_map/ppermute | solution.py:156
  170.7 1.1 shard_map.75
  171.8 4.3 %collective-permute-start.27 = (bf16[64,256]{1,0:T(8,128)(2,1)S(1)}, bf16[64,256]{1,0:T(8,128)(2,1)S(1)}, u32[]{:S(2)}, u32[]{:S(2)}) collective-permute-start(bf16[64,256]{1,0:T(8,128)(2,1)S(1)} %get-tuple-element.109.u_ref), channel_id=1, source_target_pairs={{32,64},{64,32},{96,128},{128,96},{160,192},{192,160},{224,256},{2... | collective-permute-start | bytes 98312 | tf_op jit(solution)/shard_map/ppermute | solution.py:158
  176.1 1.9 collective-permute-start.26
  178.1 1.9 collective-permute-start.24
  180.0 8.9 %collective-permute-start.25 = (bf16[64,128]{1,0:T(8,128)(2,1)S(1)}, bf16[64,128]{1,0:T(8,128)(2,1)S(1)}, u32[]{:S(2)}, u32[]{:S(2)}) collective-permute-start(bf16[64,128]{1,0:T(8,128)(2,1)S(1)} %get-tuple-element.113), channel_id=1, source_target_pairs={{0,31},{1,2},{2,1},{3,4},{4,3},{5,6},{6,5},{7,8},{8,7},{9,10},{10,... | collective-permute-start | bytes 49160 | tf_op jit(solution)/shard_map/ppermute | solution.py:156
  188.9 1.3 shard_map.76
  190.2 7.2 %collective-permute-done.25.lb_ref = bf16[64,128]{1,0:T(8,128)(2,1)S(1)} collective-permute-done((bf16[64,128]{1,0:T(8,128)(2,1)S(1)}, bf16[64,128]{1,0:T(8,128)(2,1)S(1)}, u32[]{:S(2)}, u32[]{:S(2)}) %collective-permute-start.25) | collective-permute-done | bytes 16416 | tf_op jit(solution)/shard_map/ppermute | solution.py:156
  197.4 1.1 shard_map.77
  198.6 3.8 %collective-permute-start.31 = (bf16[64,256]{1,0:T(8,128)(2,1)S(1)}, bf16[64,256]{1,0:T(8,128)(2,1)S(1)}, u32[]{:S(2)}, u32[]{:S(2)}) collective-permute-start(bf16[64,256]{1,0:T(8,128)(2,1)S(1)} %get-tuple-element.117.u_ref), channel_id=1, source_target_pairs={{32,64},{64,32},{96,128},{128,96},{160,192},{192,160},{224,256},{2... | collective-permute-start | bytes 98312 | tf_op jit(solution)/shard_map/ppermute | solution.py:158
  202.3 1.9 collective-permute-start.30
  204.3 1.9 collective-permute-start.28
  206.2 9.4 %collective-permute-start.29 = (bf16[64,128]{1,0:T(8,128)(2,1)S(1)}, bf16[64,128]{1,0:T(8,128)(2,1)S(1)}, u32[]{:S(2)}, u32[]{:S(2)}) collective-permute-start(bf16[64,128]{1,0:T(8,128)(2,1)S(1)} %get-tuple-element.121), channel_id=1, source_target_pairs={{0,31},{1,2},{2,1},{3,4},{4,3},{5,6},{6,5},{7,8},{8,7},{9,10},{10,... | collective-permute-start | bytes 49160 | tf_op jit(solution)/shard_map/ppermute | solution.py:156
  215.7 1.3 shard_map.78
  217.0 6.7 %collective-permute-done.29 = bf16[64,128]{1,0:T(8,128)(2,1)S(1)} collective-permute-done((bf16[64,128]{1,0:T(8,128)(2,1)S(1)}, bf16[64,128]{1,0:T(8,128)(2,1)S(1)}, u32[]{:S(2)}, u32[]{:S(2)}) %collective-permute-start.29) | collective-permute-done | bytes 16416 | tf_op jit(solution)/shard_map/ppermute | solution.py:156
  223.6 1.8 shard_map.79
  225.4 0.8 copy-done.8
  (44 shorter events, 0.2 us)
Async XLA Ops:
  0.8 33.7 %collective-permute-start.2 = (bf16[64,256]{1,0:T(8,128)(2,1)S(1)}, bf16[64,256]{1,0:T(8,128)(2,1)S(1)}, u32[]{:S(2)}, u32[]{:S(2)}) collective-permute-start(bf16[64,256]{1,0:T(8,128)(2,1)S(1)} %convert_bitcast_fusion.u_ref), channel_id=1, source_target_pairs={{0,32},{32,0},{64,96},{96,64},{128,160},{160,128},{192,224},{224,1... | collective-permute-start | bytes 98312 | tf_op jit(solution)/shard_map/ppermute | solution.py:159
  9.6 24.9 %collective-permute-start.3 = (bf16[64,256]{1,0:T(8,128)(2,1)S(1)}, bf16[64,256]{1,0:T(8,128)(2,1)S(1)}, u32[]{:S(2)}, u32[]{:S(2)}) collective-permute-start(bf16[64,256]{1,0:T(8,128)(2,1)S(1)} %convert_bitcast_fusion.u_ref), channel_id=1, source_target_pairs={{32,64},{64,32},{96,128},{128,96},{160,192},{192,160},{224,256},{2... | collective-permute-start | bytes 98312 | tf_op jit(solution)/shard_map/ppermute | solution.py:158
  11.5 23.0 %collective-permute-start.1 = (bf16[64,128]{1,0:T(8,128)(2,1)S(1)}, bf16[64,128]{1,0:T(8,128)(2,1)S(1)}, u32[]{:S(2)}, u32[]{:S(2)}) collective-permute-start(bf16[64,128]{1,0:T(8,128)(2,1)S(1)} %get-tuple-element.139), channel_id=1, source_target_pairs={{0,31},{1,2},{2,1},{3,4},{4,3},{5,6},{6,5},{7,8},{8,7},{9,10},{10,... | collective-permute-start | bytes 49160 | tf_op jit(solution)/shard_map/ppermute | solution.py:156
  26.9 7.6 %collective-permute-start = (bf16[64,128]{1,0:T(8,128)(2,1)S(1)}, bf16[64,128]{1,0:T(8,128)(2,1)S(1)}, u32[]{:S(2)}, u32[]{:S(2)}) collective-permute-start(bf16[64,128]{1,0:T(8,128)(2,1)S(1)} %get-tuple-element.140), channel_id=1, source_target_pairs={{0,1},{1,0},{2,3},{3,2},{4,5},{5,4},{6,7},{7,6},{8,9},{9,8},{10,11... | collective-permute-start | bytes 49160 | tf_op jit(solution)/shard_map/ppermute | solution.py:157
  28.9 1.6 copy-start
  30.5 1.0 copy-start.2
  31.6 0.9 copy-start.6
  32.5 0.7 copy-start.7
  33.2 1.3 copy-start.3
  33.2 22.0 %copy-start.1 = (bf16[1,1,16,4,128,128]{5,4,3,2,1,0:T(8,128)(2,1)S(1)}, bf16[1,1,16,4,128,128]{5,4,3,2,1,0:T(8,128)(2,1)}, u32[]{:S(2)}) copy-start(bf16[1,1,16,4,128,128]{5,4,3,2,1,0:T(8,128)(2,1)} %param.8) | copy-start | bytes 6291460
  34.5 1.2 copy-start.4
  36.9 26.5 %copy-start.5 = (bf16[1,1,2048,256]{3,2,1,0:T(8,128)(2,1)S(1)}, bf16[1,1,2048,256]{3,2,1,0:T(8,128)(2,1)}, u32[]{:S(2)}) copy-start(bf16[1,1,2048,256]{3,2,1,0:T(8,128)(2,1)} %param.10) | copy-start | bytes 3145732
  36.9 26.4 %collective-permute-start.7 = (bf16[64,256]{1,0:T(8,128)(2,1)S(1)}, bf16[64,256]{1,0:T(8,128)(2,1)S(1)}, u32[]{:S(2)}, u32[]{:S(2)}) collective-permute-start(bf16[64,256]{1,0:T(8,128)(2,1)S(1)} %get-tuple-element.69.u_ref), channel_id=1, source_target_pairs={{32,64},{64,32},{96,128},{128,96},{160,192},{192,160},{224,256},{2... | collective-permute-start | bytes 98312 | tf_op jit(solution)/shard_map/ppermute | solution.py:158
  40.4 23.0 %collective-permute-start.6 = (bf16[64,256]{1,0:T(8,128)(2,1)S(1)}, bf16[64,256]{1,0:T(8,128)(2,1)S(1)}, u32[]{:S(2)}, u32[]{:S(2)}) collective-permute-start(bf16[64,256]{1,0:T(8,128)(2,1)S(1)} %get-tuple-element.69.u_ref), channel_id=1, source_target_pairs={{0,32},{32,0},{64,96},{96,64},{128,160},{160,128},{192,224},{224,1... | collective-permute-start | bytes 98312 | tf_op jit(solution)/shard_map/ppermute | solution.py:159
  42.3 14.2 %collective-permute-start.4 = (bf16[64,128]{1,0:T(8,128)(2,1)S(1)}, bf16[64,128]{1,0:T(8,128)(2,1)S(1)}, u32[]{:S(2)}, u32[]{:S(2)}) collective-permute-start(bf16[64,128]{1,0:T(8,128)(2,1)S(1)} %get-tuple-element.72), channel_id=1, source_target_pairs={{0,1},{1,0},{2,3},{3,2},{4,5},{5,4},{6,7},{7,6},{8,9},{9,8},{10,11... | collective-permute-start | bytes 49160 | tf_op jit(solution)/shard_map/ppermute | solution.py:157
  45.9 17.4 %collective-permute-start.5 = (bf16[64,128]{1,0:T(8,128)(2,1)S(1)}, bf16[64,128]{1,0:T(8,128)(2,1)S(1)}, u32[]{:S(2)}, u32[]{:S(2)}) collective-permute-start(bf16[64,128]{1,0:T(8,128)(2,1)S(1)} %get-tuple-element.73), channel_id=1, source_target_pairs={{0,31},{1,2},{2,1},{3,4},{4,3},{5,6},{6,5},{7,8},{8,7},{9,10},{10,... | collective-permute-start | bytes 49160 | tf_op jit(solution)/shard_map/ppermute | solution.py:156
  64.5 25.7 %collective-permute-start.11 = (bf16[64,256]{1,0:T(8,128)(2,1)S(1)}, bf16[64,256]{1,0:T(8,128)(2,1)S(1)}, u32[]{:S(2)}, u32[]{:S(2)}) collective-permute-start(bf16[64,256]{1,0:T(8,128)(2,1)S(1)} %get-tuple-element.77.u_ref), channel_id=1, source_target_pairs={{32,64},{64,32},{96,128},{128,96},{160,192},{192,160},{224,256},{2... | collective-permute-start | bytes 98312 | tf_op jit(solution)/shard_map/ppermute | solution.py:158
  69.0 21.3 %collective-permute-start.10 = (bf16[64,256]{1,0:T(8,128)(2,1)S(1)}, bf16[64,256]{1,0:T(8,128)(2,1)S(1)}, u32[]{:S(2)}, u32[]{:S(2)}) collective-permute-start(bf16[64,256]{1,0:T(8,128)(2,1)S(1)} %get-tuple-element.77.u_ref), channel_id=1, source_target_pairs={{0,32},{32,0},{64,96},{96,64},{128,160},{160,128},{192,224},{224,1... | collective-permute-start | bytes 98312 | tf_op jit(solution)/shard_map/ppermute | solution.py:159
  70.9 12.0 %collective-permute-start.8 = (bf16[64,128]{1,0:T(8,128)(2,1)S(1)}, bf16[64,128]{1,0:T(8,128)(2,1)S(1)}, u32[]{:S(2)}, u32[]{:S(2)}) collective-permute-start(bf16[64,128]{1,0:T(8,128)(2,1)S(1)} %get-tuple-element.80), channel_id=1, source_target_pairs={{0,1},{1,0},{2,3},{3,2},{4,5},{5,4},{6,7},{7,6},{8,9},{9,8},{10,11... | collective-permute-start | bytes 49160 | tf_op jit(solution)/shard_map/ppermute | solution.py:157
  72.8 17.4 %collective-permute-start.9 = (bf16[64,128]{1,0:T(8,128)(2,1)S(1)}, bf16[64,128]{1,0:T(8,128)(2,1)S(1)}, u32[]{:S(2)}, u32[]{:S(2)}) collective-permute-start(bf16[64,128]{1,0:T(8,128)(2,1)S(1)} %get-tuple-element.81), channel_id=1, source_target_pairs={{0,31},{1,2},{2,1},{3,4},{4,3},{5,6},{6,5},{7,8},{8,7},{9,10},{10,... | collective-permute-start | bytes 49160 | tf_op jit(solution)/shard_map/ppermute | solution.py:156
  91.4 25.5 %collective-permute-start.15 = (bf16[64,256]{1,0:T(8,128)(2,1)S(1)}, bf16[64,256]{1,0:T(8,128)(2,1)S(1)}, u32[]{:S(2)}, u32[]{:S(2)}) collective-permute-start(bf16[64,256]{1,0:T(8,128)(2,1)S(1)} %get-tuple-element.85.u_ref), channel_id=1, source_target_pairs={{32,64},{64,32},{96,128},{128,96},{160,192},{192,160},{224,256},{2... | collective-permute-start | bytes 98312 | tf_op jit(solution)/shard_map/ppermute | solution.py:158
  95.6 21.3 %collective-permute-start.14 = (bf16[64,256]{1,0:T(8,128)(2,1)S(1)}, bf16[64,256]{1,0:T(8,128)(2,1)S(1)}, u32[]{:S(2)}, u32[]{:S(2)}) collective-permute-start(bf16[64,256]{1,0:T(8,128)(2,1)S(1)} %get-tuple-element.85.u_ref), channel_id=1, source_target_pairs={{0,32},{32,0},{64,96},{96,64},{128,160},{160,128},{192,224},{224,1... | collective-permute-start | bytes 98312 | tf_op jit(solution)/shard_map/ppermute | solution.py:159
  97.5 12.2 %collective-permute-start.12 = (bf16[64,128]{1,0:T(8,128)(2,1)S(1)}, bf16[64,128]{1,0:T(8,128)(2,1)S(1)}, u32[]{:S(2)}, u32[]{:S(2)}) collective-permute-start(bf16[64,128]{1,0:T(8,128)(2,1)S(1)} %get-tuple-element.88), channel_id=1, source_target_pairs={{0,1},{1,0},{2,3},{3,2},{4,5},{5,4},{6,7},{7,6},{8,9},{9,8},{10,11... | collective-permute-start | bytes 49160 | tf_op jit(solution)/shard_map/ppermute | solution.py:157
  99.4 17.4 %collective-permute-start.13 = (bf16[64,128]{1,0:T(8,128)(2,1)S(1)}, bf16[64,128]{1,0:T(8,128)(2,1)S(1)}, u32[]{:S(2)}, u32[]{:S(2)}) collective-permute-start(bf16[64,128]{1,0:T(8,128)(2,1)S(1)} %get-tuple-element.89), channel_id=1, source_target_pairs={{0,31},{1,2},{2,1},{3,4},{4,3},{5,6},{6,5},{7,8},{8,7},{9,10},{10,... | collective-permute-start | bytes 49160 | tf_op jit(solution)/shard_map/ppermute | solution.py:156
  118.0 26.7 %collective-permute-start.19 = (bf16[64,256]{1,0:T(8,128)(2,1)S(1)}, bf16[64,256]{1,0:T(8,128)(2,1)S(1)}, u32[]{:S(2)}, u32[]{:S(2)}) collective-permute-start(bf16[64,256]{1,0:T(8,128)(2,1)S(1)} %get-tuple-element.93.u_ref), channel_id=1, source_target_pairs={{32,64},{64,32},{96,128},{128,96},{160,192},{192,160},{224,256},{2... | collective-permute-start | bytes 98312 | tf_op jit(solution)/shard_map/ppermute | solution.py:158
  123.4 21.3 %collective-permute-start.18 = (bf16[64,256]{1,0:T(8,128)(2,1)S(1)}, bf16[64,256]{1,0:T(8,128)(2,1)S(1)}, u32[]{:S(2)}, u32[]{:S(2)}) collective-permute-start(bf16[64,256]{1,0:T(8,128)(2,1)S(1)} %get-tuple-element.93.u_ref), channel_id=1, source_target_pairs={{0,32},{32,0},{64,96},{96,64},{128,160},{160,128},{192,224},{224,1... | collective-permute-start | bytes 98312 | tf_op jit(solution)/shard_map/ppermute | solution.py:159
  125.3 12.0 %collective-permute-start.16 = (bf16[64,128]{1,0:T(8,128)(2,1)S(1)}, bf16[64,128]{1,0:T(8,128)(2,1)S(1)}, u32[]{:S(2)}, u32[]{:S(2)}) collective-permute-start(bf16[64,128]{1,0:T(8,128)(2,1)S(1)} %get-tuple-element.96), channel_id=1, source_target_pairs={{0,1},{1,0},{2,3},{3,2},{4,5},{5,4},{6,7},{7,6},{8,9},{9,8},{10,11... | collective-permute-start | bytes 49160 | tf_op jit(solution)/shard_map/ppermute | solution.py:157
  127.3 17.4 %collective-permute-start.17 = (bf16[64,128]{1,0:T(8,128)(2,1)S(1)}, bf16[64,128]{1,0:T(8,128)(2,1)S(1)}, u32[]{:S(2)}, u32[]{:S(2)}) collective-permute-start(bf16[64,128]{1,0:T(8,128)(2,1)S(1)} %get-tuple-element.97), channel_id=1, source_target_pairs={{0,31},{1,2},{2,1},{3,4},{4,3},{5,6},{6,5},{7,8},{8,7},{9,10},{10,... | collective-permute-start | bytes 49160 | tf_op jit(solution)/shard_map/ppermute | solution.py:156
  145.8 24.8 %collective-permute-start.23 = (bf16[64,256]{1,0:T(8,128)(2,1)S(1)}, bf16[64,256]{1,0:T(8,128)(2,1)S(1)}, u32[]{:S(2)}, u32[]{:S(2)}) collective-permute-start(bf16[64,256]{1,0:T(8,128)(2,1)S(1)} %get-tuple-element.101.u_ref), channel_id=1, source_target_pairs={{32,64},{64,32},{96,128},{128,96},{160,192},{192,160},{224,256},{2... | collective-permute-start | bytes 98312 | tf_op jit(solution)/shard_map/ppermute | solution.py:158
  149.4 21.3 %collective-permute-start.22 = (bf16[64,256]{1,0:T(8,128)(2,1)S(1)}, bf16[64,256]{1,0:T(8,128)(2,1)S(1)}, u32[]{:S(2)}, u32[]{:S(2)}) collective-permute-start(bf16[64,256]{1,0:T(8,128)(2,1)S(1)} %get-tuple-element.101.u_ref), channel_id=1, source_target_pairs={{0,32},{32,0},{64,96},{96,64},{128,160},{160,128},{192,224},{224,1... | collective-permute-start | bytes 98312 | tf_op jit(solution)/shard_map/ppermute | solution.py:159
  151.3 11.9 %collective-permute-start.20 = (bf16[64,128]{1,0:T(8,128)(2,1)S(1)}, bf16[64,128]{1,0:T(8,128)(2,1)S(1)}, u32[]{:S(2)}, u32[]{:S(2)}) collective-permute-start(bf16[64,128]{1,0:T(8,128)(2,1)S(1)} %get-tuple-element.104), channel_id=1, source_target_pairs={{0,1},{1,0},{2,3},{3,2},{4,5},{5,4},{6,7},{7,6},{8,9},{9,8},{10,11... | collective-permute-start | bytes 49160 | tf_op jit(solution)/shard_map/ppermute | solution.py:157
  153.2 17.4 %collective-permute-start.21 = (bf16[64,128]{1,0:T(8,128)(2,1)S(1)}, bf16[64,128]{1,0:T(8,128)(2,1)S(1)}, u32[]{:S(2)}, u32[]{:S(2)}) collective-permute-start(bf16[64,128]{1,0:T(8,128)(2,1)S(1)} %get-tuple-element.105), channel_id=1, source_target_pairs={{0,31},{1,2},{2,1},{3,4},{4,3},{5,6},{6,5},{7,8},{8,7},{9,10},{10,... | collective-permute-start | bytes 49160 | tf_op jit(solution)/shard_map/ppermute | solution.py:156
  171.8 25.6 %collective-permute-start.27 = (bf16[64,256]{1,0:T(8,128)(2,1)S(1)}, bf16[64,256]{1,0:T(8,128)(2,1)S(1)}, u32[]{:S(2)}, u32[]{:S(2)}) collective-permute-start(bf16[64,256]{1,0:T(8,128)(2,1)S(1)} %get-tuple-element.109.u_ref), channel_id=1, source_target_pairs={{32,64},{64,32},{96,128},{128,96},{160,192},{192,160},{224,256},{2... | collective-permute-start | bytes 98312 | tf_op jit(solution)/shard_map/ppermute | solution.py:158
  176.1 21.3 %collective-permute-start.26 = (bf16[64,256]{1,0:T(8,128)(2,1)S(1)}, bf16[64,256]{1,0:T(8,128)(2,1)S(1)}, u32[]{:S(2)}, u32[]{:S(2)}) collective-permute-start(bf16[64,256]{1,0:T(8,128)(2,1)S(1)} %get-tuple-element.109.u_ref), channel_id=1, source_target_pairs={{0,32},{32,0},{64,96},{96,64},{128,160},{160,128},{192,224},{224,1... | collective-permute-start | bytes 98312 | tf_op jit(solution)/shard_map/ppermute | solution.py:159
  178.1 12.1 %collective-permute-start.24 = (bf16[64,128]{1,0:T(8,128)(2,1)S(1)}, bf16[64,128]{1,0:T(8,128)(2,1)S(1)}, u32[]{:S(2)}, u32[]{:S(2)}) collective-permute-start(bf16[64,128]{1,0:T(8,128)(2,1)S(1)} %get-tuple-element.112), channel_id=1, source_target_pairs={{0,1},{1,0},{2,3},{3,2},{4,5},{5,4},{6,7},{7,6},{8,9},{9,8},{10,11... | collective-permute-start | bytes 49160 | tf_op jit(solution)/shard_map/ppermute | solution.py:157
  180.0 17.4 %collective-permute-start.25 = (bf16[64,128]{1,0:T(8,128)(2,1)S(1)}, bf16[64,128]{1,0:T(8,128)(2,1)S(1)}, u32[]{:S(2)}, u32[]{:S(2)}) collective-permute-start(bf16[64,128]{1,0:T(8,128)(2,1)S(1)} %get-tuple-element.113), channel_id=1, source_target_pairs={{0,31},{1,2},{2,1},{3,4},{4,3},{5,6},{6,5},{7,8},{8,7},{9,10},{10,... | collective-permute-start | bytes 49160 | tf_op jit(solution)/shard_map/ppermute | solution.py:156
  198.6 25.1 %collective-permute-start.31 = (bf16[64,256]{1,0:T(8,128)(2,1)S(1)}, bf16[64,256]{1,0:T(8,128)(2,1)S(1)}, u32[]{:S(2)}, u32[]{:S(2)}) collective-permute-start(bf16[64,256]{1,0:T(8,128)(2,1)S(1)} %get-tuple-element.117.u_ref), channel_id=1, source_target_pairs={{32,64},{64,32},{96,128},{128,96},{160,192},{192,160},{224,256},{2... | collective-permute-start | bytes 98312 | tf_op jit(solution)/shard_map/ppermute | solution.py:158
  202.3 21.3 %collective-permute-start.30 = (bf16[64,256]{1,0:T(8,128)(2,1)S(1)}, bf16[64,256]{1,0:T(8,128)(2,1)S(1)}, u32[]{:S(2)}, u32[]{:S(2)}) collective-permute-start(bf16[64,256]{1,0:T(8,128)(2,1)S(1)} %get-tuple-element.117.u_ref), channel_id=1, source_target_pairs={{0,32},{32,0},{64,96},{96,64},{128,160},{160,128},{192,224},{224,1... | collective-permute-start | bytes 98312 | tf_op jit(solution)/shard_map/ppermute | solution.py:159
  204.3 12.7 %collective-permute-start.28 = (bf16[64,128]{1,0:T(8,128)(2,1)S(1)}, bf16[64,128]{1,0:T(8,128)(2,1)S(1)}, u32[]{:S(2)}, u32[]{:S(2)}) collective-permute-start(bf16[64,128]{1,0:T(8,128)(2,1)S(1)} %get-tuple-element.120), channel_id=1, source_target_pairs={{0,1},{1,0},{2,3},{3,2},{4,5},{5,4},{6,7},{7,6},{8,9},{9,8},{10,11... | collective-permute-start | bytes 49160 | tf_op jit(solution)/shard_map/ppermute | solution.py:157
  206.2 17.4 %collective-permute-start.29 = (bf16[64,128]{1,0:T(8,128)(2,1)S(1)}, bf16[64,128]{1,0:T(8,128)(2,1)S(1)}, u32[]{:S(2)}, u32[]{:S(2)}) collective-permute-start(bf16[64,128]{1,0:T(8,128)(2,1)S(1)} %get-tuple-element.121), channel_id=1, source_target_pairs={{0,31},{1,2},{2,1},{3,4},{4,3},{5,6},{6,5},{7,8},{8,7},{9,10},{10,... | collective-permute-start | bytes 49160 | tf_op jit(solution)/shard_map/ppermute | solution.py:156
  225.4 0.8 copy-start.8
